TPU v7x, 32 devices: a whole 2x2x4 slice. The times are simulated.
32 devices in a mesh: wide: 16 (over z, y, x), narrow: 2 (over core).
Axes of the slice: x: 2, y: 2, z: 4, core: 2. Of those that a mesh axis runs over, the one named last changes fastest.
Arguments:
- sample_t: float32 [512, 65536], P(('wide', 'narrow')), may hold values from -300 to 300
Outputs:
- basis: float32 [65536, 512], P(('wide', 'narrow'))
- factor_out: float32 [512, 512], replicated
All inputs are finite; a program needn't handle non-finite values.
Results may differ from a plain program's by a relative error of at most 0.000084.
Values sent between devices are 32-bit elements; how exact they have to be, the bound alone decides.
No kernel may reach another device: no remote copies, remote signals or barrier semaphores. Data moves between devices by JAX's collectives and lax.ppermute only.
A program may use at most 64 MiB of HBM per device.

v0:
```python
import math

import jax
import jax.numpy as jnp
from jax import lax
from jax.sharding import PartitionSpec as P

AXES = ("wide", "narrow")


def factor_pair(matrix):
    lower = lax.linalg.cholesky(matrix)
    identity = jnp.eye(matrix.shape[0], dtype=matrix.dtype)
    solved = lax.linalg.triangular_solve(lower, identity, left_side=True, lower=True)
    return (lower, solved)


def _pair(count, bit):
    return [(i, i ^ bit) for i in range(count)]


def sum_by_halving(local, count):
    steps = count.bit_length() - 1
    assert 1 << steps == count and local.shape[0] % count == 0
    idx = lax.axis_index(AXES)
    buf = local
    for k in range(steps):
        half = buf.shape[0] // 2
        b = (idx >> k) & 1
        keep = lax.dynamic_slice_in_dim(buf, b * half, half, 0)
        send = lax.dynamic_slice_in_dim(buf, (1 - b) * half, half, 0)
        buf = keep + lax.ppermute(send, AXES, _pair(count, 1 << k))
    for k in reversed(range(steps)):
        b = (idx >> k) & 1
        recv = lax.ppermute(buf, AXES, _pair(count, 1 << k))
        lo = jnp.where(b == 0, buf, recv)
        hi = jnp.where(b == 0, recv, buf)
        buf = jnp.concatenate([lo, hi], 0)
    return buf


def per_device(sample_t):
    wide_count = lax.axis_size("wide")
    narrow_count = lax.axis_size("narrow")
    count = wide_count * narrow_count
    rows_t = lax.all_to_all(sample_t, AXES, split_axis=1, concat_axis=0, tiled=True)
    gram_local = jnp.dot(
        rows_t, rows_t.T, precision=lax.Precision.HIGHEST, preferred_element_type=jnp.float32
    )
    gram_total = sum_by_halving(gram_local, count)
    lower, lower_inv = factor_pair(gram_total)
    upper_factor = lower.T
    inverse = lower_inv.T
    total_rows = rows_t.shape[1] * count
    scale_root = math.sqrt(total_rows)
    product = lax.dot_general(
        rows_t,
        inverse,
        (((0,), (0,)), ((), ())),
        precision=lax.Precision.HIGHEST,
        preferred_element_type=jnp.float32,
    )
    return (product * scale_root, upper_factor / scale_root)


def solution(mesh):
    in_specs = (P(AXES, None),)
    out_specs = (P(AXES, None), P())
    return jax.shard_map(
        per_device, mesh=mesh, in_specs=in_specs, out_specs=out_specs, check_vma=False
    )
```

profile of v0, /device:TPU:0, one launch (start us, length us, event | category | flops | bytes accessed | tf_op | source)
XLA Modules:
  0.0 332.4 jit_solution(7485908230748255586)
XLA Ops:
  0.6 4.7 %copy.28 = f32[2,32,8,2048]{3,2,0,1:T(8,128)} copy(f32[2,32,8,2048]{3,2,1,0:T(8,128)} %bitcast.63) | data formatting | bytes 8388608 | tf_op jit(solution)/shard_map/all_to_all | solution.py:46
  5.3 7.4 %all-to-all-start = ((f32[16,32,2048]{2,0,1:T(8,128)}), f32[16,32,2048]{2,0,1:T(8,128)}, u32[]{:S(2)}, u32[]{:S(2)}) async-start(f32[16,32,2048]{2,0,1:T(8,128)} %bitcast.62), calls=%async_computation | async-start | bytes 8388608 | tf_op jit(solution)/shard_map/all_to_all | solution.py:46
  12.8 93.9 %all-to-all-done = f32[16,32,2048]{2,0,1:T(8,128)} async-done(((f32[16,32,2048]{2,0,1:T(8,128)}), f32[16,32,2048]{2,0,1:T(8,128)}, u32[]{:S(2)}, u32[]{:S(2)}) %all-to-all-start) | async-done | bytes 4194336 | tf_op jit(solution)/shard_map/all_to_all | solution.py:46
  106.6 9.5 %fusion.41 = f32[512,512]{1,0:T(8,128)S(1)} fusion(f32[512,2048]{1,0:T(8,128)} %bitcast.1), kind=kOutput, calls=%fused_computation.105 | convolution fusion | flops 6442450944 | bytes 5242880 | tf_op jit(solution)/shard_map/dot_general | solution.py:47
  119.6 7.1 %collective-permute-done.1 = f32[128,512]{1,0:T(8,128)S(1)} collective-permute-done((f32[128,512]{1,0:T(8,128)S(1)}, f32[128,512]{1,0:T(8,128)S(1)}, u32[]{:S(2)}, u32[]{:S(2)}) %collective-permute-start.1) | collective-permute-done | bytes 262176 | tf_op jit(solution)/shard_map/ppermute | solution.py:32
  128.0 3.7 %collective-permute-done.2 = f32[64,512]{1,0:T(8,128)S(1)} collective-permute-done((f32[64,512]{1,0:T(8,128)S(1)}, f32[64,512]{1,0:T(8,128)S(1)}, u32[]{:S(2)}, u32[]{:S(2)}) %collective-permute-start.2) | collective-permute-done | bytes 131104 | tf_op jit(solution)/shard_map/ppermute | solution.py:32
  131.9 4.2 %collective-permute-done.3 = f32[32,512]{1,0:T(8,128)S(1)} collective-permute-done((f32[32,512]{1,0:T(8,128)S(1)}, f32[32,512]{1,0:T(8,128)S(1)}, u32[]{:S(2)}, u32[]{:S(2)}) %collective-permute-start.3) | collective-permute-done | bytes 65568 | tf_op jit(solution)/shard_map/ppermute | solution.py:32
  136.9 4.7 %collective-permute-done.4 = f32[16,512]{1,0:T(8,128)S(1)} collective-permute-done((f32[16,512]{1,0:T(8,128)S(1)}, f32[16,512]{1,0:T(8,128)S(1)}, u32[]{:S(2)}, u32[]{:S(2)}) %collective-permute-start.4) | collective-permute-done | bytes 32800 | tf_op jit(solution)/shard_map/ppermute | solution.py:32
  142.1 4.4 %collective-permute-done.5 = f32[16,512]{1,0:T(8,128)S(1)} collective-permute-done((f32[16,512]{1,0:T(8,128)S(1)}, f32[16,512]{1,0:T(8,128)S(1)}, u32[]{:S(2)}, u32[]{:S(2)}) %collective-permute-start.5) | collective-permute-done | bytes 32800 | tf_op jit(solution)/shard_map/ppermute | solution.py:35
  146.8 6.3 %collective-permute-done.6 = f32[32,512]{0,1:T(8,128)S(1)} collective-permute-done((f32[32,512]{0,1:T(8,128)S(1)}, f32[32,512]{0,1:T(8,128)S(1)}, u32[]{:S(2)}, u32[]{:S(2)}) %collective-permute-start.6) | collective-permute-done | bytes 65568 | tf_op jit(solution)/shard_map/ppermute | solution.py:35
  154.6 5.1 %collective-permute-done.7 = f32[64,512]{0,1:T(8,128)S(1)} collective-permute-done((f32[64,512]{0,1:T(8,128)S(1)}, f32[64,512]{0,1:T(8,128)S(1)}, u32[]{:S(2)}, u32[]{:S(2)}) %collective-permute-start.7) | collective-permute-done | bytes 131104 | tf_op jit(solution)/shard_map/ppermute | solution.py:35
  161.3 5.1 %collective-permute-done.8 = f32[128,512]{0,1:T(8,128)S(1)} collective-permute-done((f32[128,512]{0,1:T(8,128)S(1)}, f32[128,512]{0,1:T(8,128)S(1)}, u32[]{:S(2)}, u32[]{:S(2)}) %collective-permute-start.8) | collective-permute-done | bytes 262176 | tf_op jit(solution)/shard_map/ppermute | solution.py:35
  169.4 11.7 %cholesky.104 = f32[128,128]{1,0:T(8,128)S(1)} custom-call(f32[128,128]{1,0:T(8,128)S(1)} %cholesky.266), custom_call_target="Cholesky" | custom-call | tf_op jit(solution)/shard_map/cholesky | solution.py:12
  181.1 9.8 %custom-call.23 = f32[1,128,128]{1,2,0:T(8,128)S(1)} custom-call(f32[1,128,128]{2,1,0:T(8,128)S(1)} %get-tuple-element.47), custom_call_target="InvertDiagBlocksLowerTriangular" | custom-call | tf_op jit(solution)/shard_map/cholesky | solution.py:12
  191.7 11.9 %cholesky.217 = f32[128,128]{1,0:T(8,128)S(1)} custom-call(f32[128,128]{1,0:T(8,128)S(1)} %cholesky.270), custom_call_target="Cholesky" | custom-call | tf_op jit(solution)/shard_map/cholesky | solution.py:12
  203.7 9.8 %custom-call.24 = f32[1,128,128]{1,2,0:T(8,128)S(1)} custom-call(f32[1,128,128]{2,1,0:T(8,128)S(1)} %get-tuple-element.44), custom_call_target="InvertDiagBlocksLowerTriangular" | custom-call | tf_op jit(solution)/shard_map/cholesky | solution.py:12
  214.2 11.7 %cholesky.238 = f32[128,128]{1,0:T(8,128)S(1)} custom-call(f32[128,128]{1,0:T(8,128)S(1)} %cholesky.275), custom_call_target="Cholesky" | custom-call | tf_op jit(solution)/shard_map/cholesky | solution.py:12
  226.6 9.8 %custom-call.25 = f32[1,128,128]{1,2,0:T(8,128)S(1)} custom-call(f32[1,128,128]{2,1,0:T(8,128)S(1)} %get-tuple-element.41), custom_call_target="InvertDiagBlocksLowerTriangular" | custom-call | tf_op jit(solution)/shard_map/cholesky | solution.py:12
  237.0 12.0 %cholesky.255 = f32[128,128]{1,0:T(8,128)S(1)} custom-call(f32[128,128]{1,0:T(8,128)S(1)} %convolution_subtract_fusion.5), custom_call_target="Cholesky" | custom-call | tf_op jit(solution)/shard_map/cholesky | solution.py:12
  255.5 14.4 %while.1 = (s32[]{:T(128)}, f32[512,512]{1,0:T(8,128)}, s32[4,2]{0,1:T(2,128)S(1)}, f32[4,128,128]{2,1,0:T(8,128)}, s32[]{:T(128)}) while((s32[]{:T(128)}, f32[512,512]{1,0:T(8,128)}, s32[4,2]{0,1:T(2,128)S(1)}, f32[4,128,128]{2,1,0:T(8,128)}, s32[]{:T(128)}) %tuple.41), condition=%wide.while_cond, body=%wide.while_body.sunk | while | flops 2 | bytes 132205 | solution.py:14
  263.4 2.9 bitcast_dynamic-update-slice_fusion.2
  269.9 40.1 %custom-call.26 = f32[4,128,128]{1,2,0:T(8,128)S(1)} custom-call(f32[4,128,128]{2,1,0:T(8,128)} %get-tuple-element.9), custom_call_target="InvertDiagBlocksLowerTriangular" | custom-call | tf_op jit(solution)/shard_map/triangular_solve | solution.py:14
  316.5 10.1 %multiply_bitcast_fusion = f32[2048,512]{0,1:T(8,128)} fusion(f32[512,2048]{1,0:T(8,128)} %bitcast.1, f32[128,512]{1,0:T(8,128)S(1)} %fusion.28, f32[128,512]{1,0:T(8,128)S(1)} %fusion.29, f32[128,512]{1,0:T(8,128)S(1)} %fusion.31, f32[128,512]{1,0:T(8,128)S(1)} %fusion.19), kind=kOutput, calls=%fused_computation.3 | convolution fusion | flops 6444285952 | bytes 9437184 | tf_op jit(solution)/shard_map/dot_general | solution.py:56
  326.6 5.3 %copy.24 = f32[2048,512]{1,0:T(8,128)} copy(f32[2048,512]{0,1:T(8,128)} %multiply_bitcast_fusion) | data formatting | bytes 8388608
  (79 shorter events, 36.9 us)
Async XLA Ops:
  5.3 101.3 %all-to-all-start = ((f32[16,32,2048]{2,0,1:T(8,128)}), f32[16,32,2048]{2,0,1:T(8,128)}, u32[]{:S(2)}, u32[]{:S(2)}) async-start(f32[16,32,2048]{2,0,1:T(8,128)} %bitcast.62), calls=%async_computation | async-start | bytes 8388608 | tf_op jit(solution)/shard_map/all_to_all | solution.py:46
  116.2 2.0 collective-permute-start
  118.3 8.4 %collective-permute-start.1 = (f32[128,512]{1,0:T(8,128)S(1)}, f32[128,512]{1,0:T(8,128)S(1)}, u32[]{:S(2)}, u32[]{:S(2)}) collective-permute-start(f32[128,512]{1,0:T(8,128)S(1)} %constant_dynamic-slice_fusion.4), channel_id=1, source_target_pairs={{0,2},{1,3},{2,0},{3,1},{4,6},{5,7},{6,4},{7,5},{8,10},{9,11},{10,... | collective-permute-start | bytes 786440 | tf_op jit(solution)/shard_map/ppermute | solution.py:32
  126.7 5.0 %collective-permute-start.2 = (f32[64,512]{1,0:T(8,128)S(1)}, f32[64,512]{1,0:T(8,128)S(1)}, u32[]{:S(2)}, u32[]{:S(2)}) collective-permute-start(f32[64,512]{1,0:T(8,128)S(1)} %constant_dynamic-slice_fusion.3), channel_id=1, source_target_pairs={{0,4},{1,5},{2,6},{3,7},{4,0},{5,1},{6,2},{7,3},{8,12},{9,13},{10,... | collective-permute-start | bytes 393224 | tf_op jit(solution)/shard_map/ppermute | solution.py:32
  131.8 4.3 %collective-permute-start.3 = (f32[32,512]{1,0:T(8,128)S(1)}, f32[32,512]{1,0:T(8,128)S(1)}, u32[]{:S(2)}, u32[]{:S(2)}) collective-permute-start(f32[32,512]{1,0:T(8,128)S(1)} %constant_dynamic-slice_fusion.2), channel_id=1, source_target_pairs={{0,8},{1,9},{2,10},{3,11},{4,12},{5,13},{6,14},{7,15},{8,0},{9,1},... | collective-permute-start | bytes 196616 | tf_op jit(solution)/shard_map/ppermute | solution.py:32
  136.2 5.4 %collective-permute-start.4 = (f32[16,512]{1,0:T(8,128)S(1)}, f32[16,512]{1,0:T(8,128)S(1)}, u32[]{:S(2)}, u32[]{:S(2)}) collective-permute-start(f32[16,512]{1,0:T(8,128)S(1)} %constant_dynamic-slice_fusion.1), channel_id=1, source_target_pairs={{0,16},{1,17},{2,18},{3,19},{4,20},{5,21},{6,22},{7,23},{8,24},{9,... | collective-permute-start | bytes 98312 | tf_op jit(solution)/shard_map/ppermute | solution.py:32
  141.6 4.9 %collective-permute-start.5 = (f32[16,512]{1,0:T(8,128)S(1)}, f32[16,512]{1,0:T(8,128)S(1)}, u32[]{:S(2)}, u32[]{:S(2)}) collective-permute-start(f32[16,512]{1,0:T(8,128)S(1)} %dynamic-slice_add_fusion.4), channel_id=1, source_target_pairs={{0,16},{1,17},{2,18},{3,19},{4,20},{5,21},{6,22},{7,23},{8,24},{9,... | collective-permute-start | bytes 98312 | tf_op jit(solution)/shard_map/ppermute | solution.py:35
  146.6 6.4 %collective-permute-start.6 = (f32[32,512]{0,1:T(8,128)S(1)}, f32[32,512]{0,1:T(8,128)S(1)}, u32[]{:S(2)}, u32[]{:S(2)}) collective-permute-start(f32[32,512]{0,1:T(8,128)S(1)} %copy.21), channel_id=1, source_target_pairs={{0,8},{1,9},{2,10},{3,11},{4,12},{5,13},{6,14},{7,15},{8,0},{9,1},... | collective-permute-start | bytes 196616 | tf_op jit(solution)/shard_map/ppermute | solution.py:35
  153.3 6.4 %collective-permute-start.7 = (f32[64,512]{0,1:T(8,128)S(1)}, f32[64,512]{0,1:T(8,128)S(1)}, u32[]{:S(2)}, u32[]{:S(2)}) collective-permute-start(f32[64,512]{0,1:T(8,128)S(1)} %pad_maximum_fusion.2), channel_id=1, source_target_pairs={{0,4},{1,5},{2,6},{3,7},{4,0},{5,1},{6,2},{7,3},{8,12},{9,13},{10,... | collective-permute-start | bytes 393224 | tf_op jit(solution)/shard_map/ppermute | solution.py:35
  160.0 6.4 %collective-permute-start.8 = (f32[128,512]{0,1:T(8,128)S(1)}, f32[128,512]{0,1:T(8,128)S(1)}, u32[]{:S(2)}, u32[]{:S(2)}) collective-permute-start(f32[128,512]{0,1:T(8,128)S(1)} %pad_maximum_fusion.3), channel_id=1, source_target_pairs={{0,2},{1,3},{2,0},{3,1},{4,6},{5,7},{6,4},{7,5},{8,10},{9,11},{10,... | collective-permute-start | bytes 786440 | tf_op jit(solution)/shard_map/ppermute | solution.py:35
  166.6 2.0 collective-permute-start.9
  213.5 97.6 %copy-start = (f32[512,512]{1,0:T(8,128)S(1)}, f32[512,512]{1,0:T(8,128)}, u32[]{:S(2)}) copy-start(f32[512,512]{1,0:T(8,128)} %fusion.17) | copy-start | bytes 3145732
where the time goes:
time: 337 us; the launch traced here: 332 us
  waiting for transfers between devices  136 us (40%)
  other arithmetic  123 us (36%)
  matrix products  27.9 us (8%)
  local copies, waits for them, and re-layouts  26.4 us (8%)
  starting transfers between devices  14.2 us (4%)
  between operations  4.11 us (1%)
    all_to_all x1, waiting for transfers between devices, per_device(): lax.all_to_all(sample_t, AXES, split_axis=1, concat_axis=0, tiled=True)  93.9 us
    another operation x14, other arithmetic, factor_pair(): lower = lax.linalg.cholesky(matrix)  78.9 us
    another operation x2, other arithmetic, factor_pair(): lax.linalg.triangular_solve(lower, identity, left_side=True, lower=True)  40.1 us
    ppermute x5, waiting for transfers between devices, sum_by_halving(): buf = keep + lax.ppermute(send, AXES, _pair(count, 1 << k))  21.6 us
    ppermute x5, waiting for transfers between devices, sum_by_halving(): recv = lax.ppermute(buf, AXES, _pair(count, 1 << k))  21 us
    another operation x12, local copies, waits for them, and re-layouts  14.4 us
    dot_general x1, matrix products, per_device(): lax.dot_general(rows_t, inverse, (((0,), (0,)), ((), ())), precision=lax....  10.1 us
    dot_general x1, matrix products, per_device(): jnp.dot(rows_t, rows_t.T, precision=lax.Precision.HIGHEST, preferred_elem...  9.48 us
  transfers between devices with their start and end apart: 11, of which 10 were waited for; matrix products, arithmetic and copies ran while one was open for 1% of the time, Pallas kernels for 0%

commit v1 on v0

--- a/solution.py
+++ b/solution.py
@@ -8,11 +8,46 @@
 AXES = ("wide", "narrow")
 
 
-def factor_pair(matrix):
-    lower = lax.linalg.cholesky(matrix)
-    identity = jnp.eye(matrix.shape[0], dtype=matrix.dtype)
+def _mm(a, b):
+    return jnp.dot(a, b, precision=lax.Precision.HIGHEST, preferred_element_type=jnp.float32)
+
+
+def _diag_pair(block):
+    lower = lax.linalg.cholesky(block)
+    identity = jnp.eye(block.shape[0], dtype=block.dtype)
     solved = lax.linalg.triangular_solve(lower, identity, left_side=True, lower=True)
-    return (lower, solved)
+    return lower, solved
+
+
+def factor_pair(matrix, b=128):
+    n = matrix.shape[0]
+    nb = n // b
+    trail = matrix
+    l_blk = {}
+    d_inv = []
+    for k in range(nb):
+        l_kk, i_kk = _diag_pair(trail[:b, :b])
+        d_inv.append(i_kk)
+        l_blk[k, k] = l_kk
+        if k < nb - 1:
+            panel = _mm(trail[b:, :b], i_kk.T)
+            for i in range(k + 1, nb):
+                l_blk[i, k] = panel[(i - k - 1) * b:(i - k) * b]
+            trail = trail[b:, b:] - _mm(panel, panel.T)
+    inv = {}
+    for j in range(nb):
+        inv[j, j] = d_inv[j]
+        for i in range(j + 1, nb):
+            acc = _mm(l_blk[i, j], inv[j, j])
+            for m in range(j + 1, i):
+                acc = acc + _mm(l_blk[i, m], inv[m, j])
+            inv[i, j] = -_mm(d_inv[i], acc)
+    zero = jnp.zeros((b, b), matrix.dtype)
+    lower = jnp.concatenate(
+        [jnp.concatenate([l_blk.get((i, j), zero) for j in range(nb)], 1) for i in range(nb)], 0)
+    lower_inv = jnp.concatenate(
+        [jnp.concatenate([inv.get((i, j), zero) for j in range(nb)], 1) for i in range(nb)], 0)
+    return (lower, lower_inv)
 
 
 def _pair(count, bit):

time: 337 us -> 292 us (0.87)
  other arithmetic: 123 us -> 92.6 us
  local copies, waits for them, and re-layouts: 26.4 us -> 13.1 us
    another operation x16 -> x20, other arithmetic: 119 us -> 91.6 us  [the longest x12 49.8 us: _diag_pair(): lower = lax.linalg.cholesky(block)]
    another operation x17 -> x5, local copies, waits for them, and re-layouts: 14.5 us -> 0.28 us  [the longest x3 0.26 us: _diag_pair(): lax.linalg.triangular_solve(lower, identity, left_side=True, lower=True)]
    another operation x13 -> x4, matrix products: 8.32 us -> 1.08 us  [_diag_pair(): lax.linalg.triangular_solve(lower, identity, left_side=True, lower=True)]
    dot_general x0 -> x22, matrix products: none -> 7.13 us  [_mm(): jnp.dot(a, b, precision=lax.Precision.HIGHEST, preferred_element_type=jnp...]
    unnamed x4 -> x9, local copies, waits for them, and re-layouts: 6.65 us -> 7.13 us
  transfers between devices with their start and end apart: 11 -> 11, of which waited for: 10 -> 11; matrix products, arithmetic and copies ran while one was open for 1% -> 0% of each run, Pallas kernels for 0% -> 0%
where the time goes in v1:
time: 292 us; the launch traced here: 288 us
  waiting for transfers between devices  138 us (47%)
  other arithmetic  92.6 us (32%)
  matrix products  27.7 us (9%)
  starting transfers between devices  14.2 us (5%)
  local copies, waits for them, and re-layouts  13.1 us (4%)
    all_to_all x1, waiting for transfers between devices, per_device(): lax.all_to_all(sample_t, AXES, split_axis=1, concat_axis=0, tiled=True)  93.9 us
    another operation x12, other arithmetic, _diag_pair(): lower = lax.linalg.cholesky(block)  49.8 us
    another operation x8, other arithmetic, _diag_pair(): lax.linalg.triangular_solve(lower, identity, left_side=True, lower=True)  41.9 us
    ppermute x5, waiting for transfers between devices, sum_by_halving(): recv = lax.ppermute(buf, AXES, _pair(count, 1 << k))  22.8 us
    ppermute x5, waiting for transfers between devices, sum_by_halving(): buf = keep + lax.ppermute(send, AXES, _pair(count, 1 << k))  21.6 us
    dot_general x1, matrix products, per_device(): lax.dot_general(rows_t, inverse, (((0,), (0,)), ((), ())), precision=lax....  10 us
    dot_general x1, matrix products, per_device(): jnp.dot(rows_t, rows_t.T, precision=lax.Precision.HIGHEST, preferred_elem...  9.48 us
    all_to_all x1, starting transfers between devices, per_device(): lax.all_to_all(sample_t, AXES, split_axis=1, concat_axis=0, tiled=True)  7.43 us
  transfers between devices with their start and end apart: 11, of which 11 were waited for; matrix products, arithmetic and copies ran while one was open for 0% of the time, Pallas kernels for 0%

profile of v1, /device:TPU:0, one launch (start us, length us, event | category | flops | bytes accessed | tf_op | source)
XLA Modules:
  0.0 287.7 jit_solution(4122485212012799821)
XLA Ops:
  0.6 4.7 %copy.140 = f32[2,32,8,2048]{3,2,0,1:T(8,128)} copy(f32[2,32,8,2048]{3,2,1,0:T(8,128)} %bitcast.83) | data formatting | bytes 8388608 | tf_op jit(solution)/shard_map/all_to_all | solution.py:81
  5.3 7.4 %all-to-all-start = ((f32[16,32,2048]{2,0,1:T(8,128)}), f32[16,32,2048]{2,0,1:T(8,128)}, u32[]{:S(2)}, u32[]{:S(2)}) async-start(f32[16,32,2048]{2,0,1:T(8,128)} %bitcast.82), calls=%async_computation | async-start | bytes 8388608 | tf_op jit(solution)/shard_map/all_to_all | solution.py:81
  12.8 93.9 %all-to-all-done = f32[16,32,2048]{2,0,1:T(8,128)} async-done(((f32[16,32,2048]{2,0,1:T(8,128)}), f32[16,32,2048]{2,0,1:T(8,128)}, u32[]{:S(2)}, u32[]{:S(2)}) %all-to-all-start) | async-done | bytes 4194336 | tf_op jit(solution)/shard_map/all_to_all | solution.py:81
  106.6 9.5 %fusion.71 = f32[512,512]{1,0:T(8,128)S(1)} fusion(f32[512,2048]{1,0:T(8,128)} %bitcast.1), kind=kOutput, calls=%fused_computation.137 | convolution fusion | flops 6442450944 | bytes 5242880 | tf_op jit(solution)/shard_map/dot_general | solution.py:82
  116.3 1.9 collective-permute-done
  119.6 7.1 %collective-permute-done.1 = f32[128,512]{1,0:T(8,128)S(1)} collective-permute-done((f32[128,512]{1,0:T(8,128)S(1)}, f32[128,512]{1,0:T(8,128)S(1)}, u32[]{:S(2)}, u32[]{:S(2)}) %collective-permute-start.1) | collective-permute-done | bytes 262176 | tf_op jit(solution)/shard_map/ppermute | solution.py:67
  128.0 3.7 %collective-permute-done.2 = f32[64,512]{1,0:T(8,128)S(1)} collective-permute-done((f32[64,512]{1,0:T(8,128)S(1)}, f32[64,512]{1,0:T(8,128)S(1)}, u32[]{:S(2)}, u32[]{:S(2)}) %collective-permute-start.2) | collective-permute-done | bytes 131104 | tf_op jit(solution)/shard_map/ppermute | solution.py:67
  131.9 4.2 %collective-permute-done.3 = f32[32,512]{1,0:T(8,128)S(1)} collective-permute-done((f32[32,512]{1,0:T(8,128)S(1)}, f32[32,512]{1,0:T(8,128)S(1)}, u32[]{:S(2)}, u32[]{:S(2)}) %collective-permute-start.3) | collective-permute-done | bytes 65568 | tf_op jit(solution)/shard_map/ppermute | solution.py:67
  136.9 4.7 %collective-permute-done.4 = f32[16,512]{1,0:T(8,128)S(1)} collective-permute-done((f32[16,512]{1,0:T(8,128)S(1)}, f32[16,512]{1,0:T(8,128)S(1)}, u32[]{:S(2)}, u32[]{:S(2)}) %collective-permute-start.4) | collective-permute-done | bytes 32800 | tf_op jit(solution)/shard_map/ppermute | solution.py:67
  142.1 4.4 %collective-permute-done.5 = f32[16,512]{1,0:T(8,128)S(1)} collective-permute-done((f32[16,512]{1,0:T(8,128)S(1)}, f32[16,512]{1,0:T(8,128)S(1)}, u32[]{:S(2)}, u32[]{:S(2)}) %collective-permute-start.5) | collective-permute-done | bytes 32800 | tf_op jit(solution)/shard_map/ppermute | solution.py:70
  146.8 6.3 %collective-permute-done.6 = f32[32,512]{0,1:T(8,128)S(1)} collective-permute-done((f32[32,512]{0,1:T(8,128)S(1)}, f32[32,512]{0,1:T(8,128)S(1)}, u32[]{:S(2)}, u32[]{:S(2)}) %collective-permute-start.6) | collective-permute-done | bytes 65568 | tf_op jit(solution)/shard_map/ppermute | solution.py:70
  154.6 5.1 %collective-permute-done.7 = f32[64,512]{0,1:T(8,128)S(1)} collective-permute-done((f32[64,512]{0,1:T(8,128)S(1)}, f32[64,512]{0,1:T(8,128)S(1)}, u32[]{:S(2)}, u32[]{:S(2)}) %collective-permute-start.7) | collective-permute-done | bytes 131104 | tf_op jit(solution)/shard_map/ppermute | solution.py:70
  161.3 5.1 %collective-permute-done.8 = f32[128,512]{0,1:T(8,128)S(1)} collective-permute-done((f32[128,512]{0,1:T(8,128)S(1)}, f32[128,512]{0,1:T(8,128)S(1)}, u32[]{:S(2)}, u32[]{:S(2)}) %collective-permute-start.8) | collective-permute-done | bytes 262176 | tf_op jit(solution)/shard_map/ppermute | solution.py:70
  166.7 1.9 collective-permute-done.9
  168.9 11.7 %custom-call.12 = f32[128,128]{1,0:T(8,128)S(1)} custom-call(f32[128,128]{1,0:T(8,128)S(1)} %copy.97), custom_call_target="Cholesky" | custom-call | tf_op jit(solution)/shard_map/cholesky/custom-call.1 | solution.py:16
  182.0 9.8 %custom-call.13 = f32[1,128,128]{1,2,0:T(8,128)S(1)} custom-call(f32[1,128,128]{2,1,0:T(8,128)S(1)} %get-tuple-element.18), custom_call_target="InvertDiagBlocksLowerTriangular" | custom-call | tf_op jit(solution)/shard_map/triangular_solve/custom-call.0 | solution.py:18
  194.2 11.9 %custom-call.14 = f32[128,128]{1,0:T(8,128)S(1)} custom-call(f32[128,128]{1,0:T(8,128)S(1)} %copy.101), custom_call_target="Cholesky" | custom-call | tf_op jit(solution)/shard_map/cholesky/custom-call.1 | solution.py:16
  207.5 9.8 %custom-call.15 = f32[1,128,128]{1,2,0:T(8,128)S(1)} custom-call(f32[1,128,128]{2,1,0:T(8,128)S(1)} %get-tuple-element.16), custom_call_target="InvertDiagBlocksLowerTriangular" | custom-call | tf_op jit(solution)/shard_map/triangular_solve/custom-call.0 | solution.py:18
  218.5 11.7 %custom-call.16 = f32[128,128]{1,0:T(8,128)S(1)} custom-call(f32[128,128]{1,0:T(8,128)S(1)} %fusion.46), custom_call_target="Cholesky" | custom-call | tf_op jit(solution)/shard_map/cholesky/custom-call.1 | solution.py:16
  231.6 9.8 %custom-call.17 = f32[1,128,128]{1,2,0:T(8,128)S(1)} custom-call(f32[1,128,128]{2,1,0:T(8,128)S(1)} %get-tuple-element.14), custom_call_target="InvertDiagBlocksLowerTriangular" | custom-call | tf_op jit(solution)/shard_map/triangular_solve/custom-call.0 | solution.py:18
  245.3 11.7 %custom-call.18 = f32[128,128]{1,0:T(8,128)S(1)} custom-call(f32[128,128]{1,0:T(8,128)S(1)} %broadcast_multiply_fusion), custom_call_target="Cholesky" | custom-call | tf_op jit(solution)/shard_map/cholesky/custom-call.1 | solution.py:16
  258.3 9.8 %custom-call.19 = f32[1,128,128]{1,2,0:T(8,128)S(1)} custom-call(f32[1,128,128]{2,1,0:T(8,128)S(1)} %get-tuple-element.12), custom_call_target="InvertDiagBlocksLowerTriangular" | custom-call | tf_op jit(solution)/shard_map/triangular_solve/custom-call.0 | solution.py:18
  270.3 10.0 %multiply_bitcast_fusion = f32[2048,512]{0,1:T(8,128)} fusion(f32[512,2048]{1,0:T(8,128)} %bitcast.1, f32[128,256]{1,0:T(8,128)S(1)} %broadcast.51, f32[128,128]{1,0:T(8,128)S(1)} %broadcast.64, f32[128,128]{1,0:T(8,128)S(1)} %fusion.38, f32[128,128]{1,0:T(8,128)S(1)} %copy.120, f32[128,128]{1,0:T(8,128)S(1)} %convolution_negate_fusion, ...), kind=kOutput, calls=%fused_computation.1 | convolution fusion | flops 6446907392 | bytes 9240576 | tf_op jit(solution)/shard_map/dot_general | solution.py:91
  280.4 5.3 %copy.122 = f32[2048,512]{1,0:T(8,128)} copy(f32[2048,512]{0,1:T(8,128)} %multiply_bitcast_fusion) | data formatting | bytes 8388608
  (98 shorter events, 24.4 us)
Async XLA Ops:
  5.3 101.3 %all-to-all-start = ((f32[16,32,2048]{2,0,1:T(8,128)}), f32[16,32,2048]{2,0,1:T(8,128)}, u32[]{:S(2)}, u32[]{:S(2)}) async-start(f32[16,32,2048]{2,0,1:T(8,128)} %bitcast.82), calls=%async_computation | async-start | bytes 8388608 | tf_op jit(solution)/shard_map/all_to_all | solution.py:81
  116.2 2.0 collective-permute-start
  118.3 8.4 %collective-permute-start.1 = (f32[128,512]{1,0:T(8,128)S(1)}, f32[128,512]{1,0:T(8,128)S(1)}, u32[]{:S(2)}, u32[]{:S(2)}) collective-permute-start(f32[128,512]{1,0:T(8,128)S(1)} %constant_dynamic-slice_fusion.3), channel_id=1, source_target_pairs={{0,2},{1,3},{2,0},{3,1},{4,6},{5,7},{6,4},{7,5},{8,10},{9,11},{10,... | collective-permute-start | bytes 786440 | tf_op jit(solution)/shard_map/ppermute | solution.py:67
  126.7 5.0 %collective-permute-start.2 = (f32[64,512]{1,0:T(8,128)S(1)}, f32[64,512]{1,0:T(8,128)S(1)}, u32[]{:S(2)}, u32[]{:S(2)}) collective-permute-start(f32[64,512]{1,0:T(8,128)S(1)} %constant_dynamic-slice_fusion.2), channel_id=1, source_target_pairs={{0,4},{1,5},{2,6},{3,7},{4,0},{5,1},{6,2},{7,3},{8,12},{9,13},{10,... | collective-permute-start | bytes 393224 | tf_op jit(solution)/shard_map/ppermute | solution.py:67
  131.8 4.3 %collective-permute-start.3 = (f32[32,512]{1,0:T(8,128)S(1)}, f32[32,512]{1,0:T(8,128)S(1)}, u32[]{:S(2)}, u32[]{:S(2)}) collective-permute-start(f32[32,512]{1,0:T(8,128)S(1)} %constant_dynamic-slice_fusion.1), channel_id=1, source_target_pairs={{0,8},{1,9},{2,10},{3,11},{4,12},{5,13},{6,14},{7,15},{8,0},{9,1},... | collective-permute-start | bytes 196616 | tf_op jit(solution)/shard_map/ppermute | solution.py:67
  136.2 5.4 %collective-permute-start.4 = (f32[16,512]{1,0:T(8,128)S(1)}, f32[16,512]{1,0:T(8,128)S(1)}, u32[]{:S(2)}, u32[]{:S(2)}) collective-permute-start(f32[16,512]{1,0:T(8,128)S(1)} %constant_dynamic-slice_fusion), channel_id=1, source_target_pairs={{0,16},{1,17},{2,18},{3,19},{4,20},{5,21},{6,22},{7,23},{8,24},{9,... | collective-permute-start | bytes 98312 | tf_op jit(solution)/shard_map/ppermute | solution.py:67
  141.6 4.9 %collective-permute-start.5 = (f32[16,512]{1,0:T(8,128)S(1)}, f32[16,512]{1,0:T(8,128)S(1)}, u32[]{:S(2)}, u32[]{:S(2)}) collective-permute-start(f32[16,512]{1,0:T(8,128)S(1)} %dynamic-slice_add_fusion.4), channel_id=1, source_target_pairs={{0,16},{1,17},{2,18},{3,19},{4,20},{5,21},{6,22},{7,23},{8,24},{9,... | collective-permute-start | bytes 98312 | tf_op jit(solution)/shard_map/ppermute | solution.py:70
  146.6 6.4 %collective-permute-start.6 = (f32[32,512]{0,1:T(8,128)S(1)}, f32[32,512]{0,1:T(8,128)S(1)}, u32[]{:S(2)}, u32[]{:S(2)}) collective-permute-start(f32[32,512]{0,1:T(8,128)S(1)} %copy.93), channel_id=1, source_target_pairs={{0,8},{1,9},{2,10},{3,11},{4,12},{5,13},{6,14},{7,15},{8,0},{9,1},... | collective-permute-start | bytes 196616 | tf_op jit(solution)/shard_map/ppermute | solution.py:70
  153.3 6.4 %collective-permute-start.7 = (f32[64,512]{0,1:T(8,128)S(1)}, f32[64,512]{0,1:T(8,128)S(1)}, u32[]{:S(2)}, u32[]{:S(2)}) collective-permute-start(f32[64,512]{0,1:T(8,128)S(1)} %pad_maximum_fusion.6), channel_id=1, source_target_pairs={{0,4},{1,5},{2,6},{3,7},{4,0},{5,1},{6,2},{7,3},{8,12},{9,13},{10,... | collective-permute-start | bytes 393224 | tf_op jit(solution)/shard_map/ppermute | solution.py:70
  160.0 6.4 %collective-permute-start.8 = (f32[128,512]{0,1:T(8,128)S(1)}, f32[128,512]{0,1:T(8,128)S(1)}, u32[]{:S(2)}, u32[]{:S(2)}) collective-permute-start(f32[128,512]{0,1:T(8,128)S(1)} %pad_maximum_fusion.7), channel_id=1, source_target_pairs={{0,2},{1,3},{2,0},{3,1},{4,6},{5,7},{6,4},{7,5},{8,10},{9,11},{10,... | collective-permute-start | bytes 786440 | tf_op jit(solution)/shard_map/ppermute | solution.py:70
  166.6 2.0 collective-permute-start.9

commit v2 on v1

--- a/solution.py
+++ b/solution.py
@@ -3,6 +3,8 @@
 import jax
 import jax.numpy as jnp
 from jax import lax
+from jax.experimental import pallas as pl
+from jax.experimental.pallas import tpu as pltpu
 from jax.sharding import PartitionSpec as P
 
 AXES = ("wide", "narrow")
@@ -12,11 +14,40 @@
     return jnp.dot(a, b, precision=lax.Precision.HIGHEST, preferred_element_type=jnp.float32)
 
 
+def _diag_kernel(a_ref, r_ref, w_ref, s_ref):
+    b = a_ref.shape[0]
+    s_ref[...] = a_ref[...]
+    rows = lax.broadcasted_iota(jnp.int32, (b, 1), 0)
+    lanes = lax.broadcasted_iota(jnp.int32, (1, b), 1)
+    w_ref[...] = (lax.broadcasted_iota(jnp.int32, (b, b), 0)
+                  == lax.broadcasted_iota(jnp.int32, (b, b), 1)).astype(jnp.float32)
+    for j in range(b):
+        lo = (j // 8) * 8
+        a = s_ref[lo:, :]
+        d = a[j - lo:j - lo + 1, j:j + 1]
+        s = 1.0 / jnp.sqrt(d)
+        row = jnp.where(lanes >= j, a[j - lo:j - lo + 1, :] * s, 0.0)
+        col = jnp.where(rows[lo:] >= j, a[:, j:j + 1] * s, 0.0)
+        r_ref[j:j + 1, :] = row
+        s_ref[lo:, :] = a - col * row
+        wrow = w_ref[j:j + 1, :] * s
+        w_ref[j:j + 1, :] = wrow
+        below = jnp.where(rows[lo:] > j, col, 0.0)
+        w_ref[lo:, :] = w_ref[lo:, :] - below * wrow
+
+
 def _diag_pair(block):
-    lower = lax.linalg.cholesky(block)
-    identity = jnp.eye(block.shape[0], dtype=block.dtype)
-    solved = lax.linalg.triangular_solve(lower, identity, left_side=True, lower=True)
-    return lower, solved
+    b = block.shape[0]
+    sym = (block + block.T) * 0.5
+    r, w = pl.pallas_call(
+        _diag_kernel,
+        out_shape=(jax.ShapeDtypeStruct((b, b), jnp.float32),
+                   jax.ShapeDtypeStruct((b, b), jnp.float32)),
+        scratch_shapes=[pltpu.VMEM((b, b), jnp.float32)],
+        cost_estimate=pl.CostEstimate(flops=4 * b * b * b, transcendentals=b,
+                                      bytes_accessed=12 * b * b),
+    )(sym)
+    return r.T, w
 
 
 def factor_pair(matrix, b=128):

time: 292 us -> 274 us (0.938)
  other arithmetic: 92.6 us -> 2.26 us
  Pallas kernels: 0 us -> 57.1 us
  matrix products: 27.7 us -> 38.8 us
  local copies, waits for them, and re-layouts: 13.1 us -> 17 us
    another operation x20 -> x0, other arithmetic: 91.6 us -> none  [the longest x12 49.8 us: _diag_pair(): lower = lax.linalg.cholesky(block)]
    pallas_call x0 -> x4, Pallas kernels: none -> 57.1 us  [_diag_pair(): pl.pallas_call(_diag_kernel, out_shape=(jax.ShapeDtypeStruct((b, b), jnp....]
    dot_general x22, matrix products: 7.13 us -> 19 us  [_mm(): jnp.dot(a, b, precision=lax.Precision.HIGHEST, preferred_element_type=jnp...]
    unnamed x9 -> x17, local copies, waits for them, and re-layouts: 7.13 us -> 7.15 us
where the time goes in v2:
time: 274 us; the launch traced here: 269 us
  waiting for transfers between devices  138 us (50%)
  Pallas kernels  57.1 us (21%)
  matrix products  38.8 us (14%)
  local copies, waits for them, and re-layouts  17 us (6%)
  starting transfers between devices  14.2 us (5%)
    all_to_all x1, waiting for transfers between devices, per_device(): lax.all_to_all(sample_t, AXES, split_axis=1, concat_axis=0, tiled=True)  93.9 us
    pallas_call x4, Pallas kernels, _diag_pair(): pl.pallas_call(_diag_kernel, out_shape=(jax.ShapeDtypeStruct((b, b), jnp....  57.1 us
    ppermute x5, waiting for transfers between devices, sum_by_halving(): recv = lax.ppermute(buf, AXES, _pair(count, 1 << k))  22.8 us
    ppermute x5, waiting for transfers between devices, sum_by_halving(): buf = keep + lax.ppermute(send, AXES, _pair(count, 1 << k))  21.7 us
    dot_general x22, matrix products, _mm(): jnp.dot(a, b, precision=lax.Precision.HIGHEST, preferred_element_type=jnp...  19 us
    dot_general x1, matrix products, per_device(): lax.dot_general(rows_t, inverse, (((0,), (0,)), ((), ())), precision=lax....  10.2 us
    dot_general x1, matrix products, per_device(): jnp.dot(rows_t, rows_t.T, precision=lax.Precision.HIGHEST, preferred_elem...  9.59 us
    all_to_all x1, starting transfers between devices, per_device(): lax.all_to_all(sample_t, AXES, split_axis=1, concat_axis=0, tiled=True)  7.43 us
  transfers between devices with their start and end apart: 11, of which 11 were waited for; matrix products, arithmetic and copies ran while one was open for 0% of the time, Pallas kernels for 0%

profile of v2, /device:TPU:0, one launch (start us, length us, event | category | flops | bytes accessed | tf_op | source)
XLA Modules:
  0.0 269.4 jit_solution(10256534505400046472)
XLA Ops:
  0.6 4.7 %copy.144 = f32[2,32,8,2048]{3,2,0,1:T(8,128)} copy(f32[2,32,8,2048]{3,2,1,0:T(8,128)} %bitcast.67) | data formatting | bytes 8388608 | tf_op jit(solution)/shard_map/all_to_all | solution.py:112
  5.3 7.4 %all-to-all-start = ((f32[16,32,2048]{2,0,1:T(8,128)}), f32[16,32,2048]{2,0,1:T(8,128)}, u32[]{:S(2)}, u32[]{:S(2)}) async-start(f32[16,32,2048]{2,0,1:T(8,128)} %bitcast.66), calls=%async_computation | async-start | bytes 8388608 | tf_op jit(solution)/shard_map/all_to_all | solution.py:112
  12.8 93.9 %all-to-all-done = f32[16,32,2048]{2,0,1:T(8,128)} async-done(((f32[16,32,2048]{2,0,1:T(8,128)}), f32[16,32,2048]{2,0,1:T(8,128)}, u32[]{:S(2)}, u32[]{:S(2)}) %all-to-all-start) | async-done | bytes 4194336 | tf_op jit(solution)/shard_map/all_to_all | solution.py:112
  106.6 9.6 %fusion.57 = f32[512,512]{1,0:T(8,128)S(1)} fusion(f32[512,2048]{1,0:T(8,128)} %bitcast.1), kind=kOutput, calls=%fused_computation.107 | convolution fusion | flops 6442450944 | bytes 5242880 | tf_op jit(solution)/shard_map/dot_general | solution.py:113
  116.4 1.9 collective-permute-done
  118.4 1.3 collective-permute-start.1
  119.7 7.1 %collective-permute-done.1 = f32[128,512]{1,0:T(8,128)S(1)} collective-permute-done((f32[128,512]{1,0:T(8,128)S(1)}, f32[128,512]{1,0:T(8,128)S(1)}, u32[]{:S(2)}, u32[]{:S(2)}) %collective-permute-start.1) | collective-permute-done | bytes 262176 | tf_op jit(solution)/shard_map/ppermute | solution.py:98
  128.2 3.7 %collective-permute-done.2 = f32[64,512]{1,0:T(8,128)S(1)} collective-permute-done((f32[64,512]{1,0:T(8,128)S(1)}, f32[64,512]{1,0:T(8,128)S(1)}, u32[]{:S(2)}, u32[]{:S(2)}) %collective-permute-start.2) | collective-permute-done | bytes 131104 | tf_op jit(solution)/shard_map/ppermute | solution.py:98
  132.0 4.2 %collective-permute-done.3 = f32[32,512]{1,0:T(8,128)S(1)} collective-permute-done((f32[32,512]{1,0:T(8,128)S(1)}, f32[32,512]{1,0:T(8,128)S(1)}, u32[]{:S(2)}, u32[]{:S(2)}) %collective-permute-start.3) | collective-permute-done | bytes 65568 | tf_op jit(solution)/shard_map/ppermute | solution.py:98
  137.0 4.7 %collective-permute-done.4 = f32[16,512]{1,0:T(8,128)S(1)} collective-permute-done((f32[16,512]{1,0:T(8,128)S(1)}, f32[16,512]{1,0:T(8,128)S(1)}, u32[]{:S(2)}, u32[]{:S(2)}) %collective-permute-start.4) | collective-permute-done | bytes 32800 | tf_op jit(solution)/shard_map/ppermute | solution.py:98
  142.2 4.4 %collective-permute-done.5 = f32[16,512]{1,0:T(8,128)S(1)} collective-permute-done((f32[16,512]{1,0:T(8,128)S(1)}, f32[16,512]{1,0:T(8,128)S(1)}, u32[]{:S(2)}, u32[]{:S(2)}) %collective-permute-start.5) | collective-permute-done | bytes 32800 | tf_op jit(solution)/shard_map/ppermute | solution.py:101
  146.9 6.3 %collective-permute-done.6 = f32[32,512]{0,1:T(8,128)S(1)} collective-permute-done((f32[32,512]{0,1:T(8,128)S(1)}, f32[32,512]{0,1:T(8,128)S(1)}, u32[]{:S(2)}, u32[]{:S(2)}) %collective-permute-start.6) | collective-permute-done | bytes 65568 | tf_op jit(solution)/shard_map/ppermute | solution.py:101
  153.4 1.3 collective-permute-start.7
  154.7 5.1 %collective-permute-done.7 = f32[64,512]{0,1:T(8,128)S(1)} collective-permute-done((f32[64,512]{0,1:T(8,128)S(1)}, f32[64,512]{0,1:T(8,128)S(1)}, u32[]{:S(2)}, u32[]{:S(2)}) %collective-permute-start.7) | collective-permute-done | bytes 131104 | tf_op jit(solution)/shard_map/ppermute | solution.py:101
  160.1 1.4 collective-permute-start.8
  161.4 5.1 %collective-permute-done.8 = f32[128,512]{0,1:T(8,128)S(1)} collective-permute-done((f32[128,512]{0,1:T(8,128)S(1)}, f32[128,512]{0,1:T(8,128)S(1)}, u32[]{:S(2)}, u32[]{:S(2)}) %collective-permute-start.8) | collective-permute-done | bytes 262176 | tf_op jit(solution)/shard_map/ppermute | solution.py:101
  166.8 1.9 collective-permute-done.9
  169.6 14.2 %shard_map.30 = (f32[128,128]{1,0:T(8,128)}, f32[128,128]{1,0:T(8,128)}) custom-call(f32[128,128]{1,0:T(8,128)} %copy.100.a_ref), custom_call_target="tpu_custom_call" | custom-call | flops 8388608 | bytes 196608 | tf_op jit(solution)/shard_map/pallas_call | solution.py:42
  190.0 14.4 %shard_map.31 = (f32[128,128]{1,0:T(8,128)}, f32[128,128]{1,0:T(8,128)}) custom-call(f32[128,128]{1,0:T(8,128)} %copy.104.a_ref), custom_call_target="tpu_custom_call" | custom-call | flops 8388608 | bytes 196608 | tf_op jit(solution)/shard_map/pallas_call | solution.py:42
  209.0 14.2 %shard_map.32 = (f32[128,128]{1,0:T(8,128)}, f32[128,128]{1,0:T(8,128)}) custom-call(f32[128,128]{1,0:T(8,128)} %fusion.36.a_ref), custom_call_target="tpu_custom_call" | custom-call | flops 8388608 | bytes 196608 | tf_op jit(solution)/shard_map/pallas_call | solution.py:42
  232.9 14.4 %shard_map.33 = (f32[128,128]{1,0:T(8,128)}, f32[128,128]{1,0:T(8,128)}) custom-call(f32[128,128]{1,0:T(8,128)} %broadcast_multiply_fusion.a_ref), custom_call_target="tpu_custom_call" | custom-call | flops 8388608 | bytes 196608 | tf_op jit(solution)/shard_map/pallas_call | solution.py:42
  252.0 10.2 %multiply_bitcast_fusion = f32[2048,512]{0,1:T(8,128)} fusion(f32[512,2048]{1,0:T(8,128)} %bitcast.1, f32[128,256]{1,0:T(8,128)S(1)} %broadcast.17, f32[128,128]{1,0:T(8,128)S(1)} %broadcast_in_dim.3, f32[128,128]{1,0:T(8,128)S(1)} %copy-done, f32[128,128]{1,0:T(8,128)} %get-tuple-element.13, f32[128,128]{1,0:T(8,128)S(1)} %convolution_negate_fusion, ...), kind=kOutput, calls=%fused_computation.1 | convolution fusion | flops 6446907392 | bytes 9240576 | tf_op jit(solution)/shard_map/dot_general | solution.py:122
  262.2 5.3 %copy.126 = f32[2048,512]{1,0:T(8,128)} copy(f32[2048,512]{0,1:T(8,128)} %multiply_bitcast_fusion) | data formatting | bytes 8388608
  267.6 1.3 copy.127
  (87 shorter events, 29.7 us)
Async XLA Ops:
  5.3 101.3 %all-to-all-start = ((f32[16,32,2048]{2,0,1:T(8,128)}), f32[16,32,2048]{2,0,1:T(8,128)}, u32[]{:S(2)}, u32[]{:S(2)}) async-start(f32[16,32,2048]{2,0,1:T(8,128)} %bitcast.66), calls=%async_computation | async-start | bytes 8388608 | tf_op jit(solution)/shard_map/all_to_all | solution.py:112
  116.3 2.0 collective-permute-start
  118.4 8.4 %collective-permute-start.1 = (f32[128,512]{1,0:T(8,128)S(1)}, f32[128,512]{1,0:T(8,128)S(1)}, u32[]{:S(2)}, u32[]{:S(2)}) collective-permute-start(f32[128,512]{1,0:T(8,128)S(1)} %constant_dynamic-slice_fusion.3), channel_id=1, source_target_pairs={{0,2},{1,3},{2,0},{3,1},{4,6},{5,7},{6,4},{7,5},{8,10},{9,11},{10,... | collective-permute-start | bytes 786440 | tf_op jit(solution)/shard_map/ppermute | solution.py:98
  126.9 5.0 %collective-permute-start.2 = (f32[64,512]{1,0:T(8,128)S(1)}, f32[64,512]{1,0:T(8,128)S(1)}, u32[]{:S(2)}, u32[]{:S(2)}) collective-permute-start(f32[64,512]{1,0:T(8,128)S(1)} %constant_dynamic-slice_fusion.2), channel_id=1, source_target_pairs={{0,4},{1,5},{2,6},{3,7},{4,0},{5,1},{6,2},{7,3},{8,12},{9,13},{10,... | collective-permute-start | bytes 393224 | tf_op jit(solution)/shard_map/ppermute | solution.py:98
  131.9 4.3 %collective-permute-start.3 = (f32[32,512]{1,0:T(8,128)S(1)}, f32[32,512]{1,0:T(8,128)S(1)}, u32[]{:S(2)}, u32[]{:S(2)}) collective-permute-start(f32[32,512]{1,0:T(8,128)S(1)} %constant_dynamic-slice_fusion.1), channel_id=1, source_target_pairs={{0,8},{1,9},{2,10},{3,11},{4,12},{5,13},{6,14},{7,15},{8,0},{9,1},... | collective-permute-start | bytes 196616 | tf_op jit(solution)/shard_map/ppermute | solution.py:98
  136.3 5.4 %collective-permute-start.4 = (f32[16,512]{1,0:T(8,128)S(1)}, f32[16,512]{1,0:T(8,128)S(1)}, u32[]{:S(2)}, u32[]{:S(2)}) collective-permute-start(f32[16,512]{1,0:T(8,128)S(1)} %constant_dynamic-slice_fusion), channel_id=1, source_target_pairs={{0,16},{1,17},{2,18},{3,19},{4,20},{5,21},{6,22},{7,23},{8,24},{9,... | collective-permute-start | bytes 98312 | tf_op jit(solution)/shard_map/ppermute | solution.py:98
  141.7 4.9 %collective-permute-start.5 = (f32[16,512]{1,0:T(8,128)S(1)}, f32[16,512]{1,0:T(8,128)S(1)}, u32[]{:S(2)}, u32[]{:S(2)}) collective-permute-start(f32[16,512]{1,0:T(8,128)S(1)} %dynamic-slice_add_fusion.4), channel_id=1, source_target_pairs={{0,16},{1,17},{2,18},{3,19},{4,20},{5,21},{6,22},{7,23},{8,24},{9,... | collective-permute-start | bytes 98312 | tf_op jit(solution)/shard_map/ppermute | solution.py:101
  146.8 6.4 %collective-permute-start.6 = (f32[32,512]{0,1:T(8,128)S(1)}, f32[32,512]{0,1:T(8,128)S(1)}, u32[]{:S(2)}, u32[]{:S(2)}) collective-permute-start(f32[32,512]{0,1:T(8,128)S(1)} %copy.96), channel_id=1, source_target_pairs={{0,8},{1,9},{2,10},{3,11},{4,12},{5,13},{6,14},{7,15},{8,0},{9,1},... | collective-permute-start | bytes 196616 | tf_op jit(solution)/shard_map/ppermute | solution.py:101
  153.4 6.4 %collective-permute-start.7 = (f32[64,512]{0,1:T(8,128)S(1)}, f32[64,512]{0,1:T(8,128)S(1)}, u32[]{:S(2)}, u32[]{:S(2)}) collective-permute-start(f32[64,512]{0,1:T(8,128)S(1)} %pad_maximum_fusion.6), channel_id=1, source_target_pairs={{0,4},{1,5},{2,6},{3,7},{4,0},{5,1},{6,2},{7,3},{8,12},{9,13},{10,... | collective-permute-start | bytes 393224 | tf_op jit(solution)/shard_map/ppermute | solution.py:101
  160.1 6.4 %collective-permute-start.8 = (f32[128,512]{0,1:T(8,128)S(1)}, f32[128,512]{0,1:T(8,128)S(1)}, u32[]{:S(2)}, u32[]{:S(2)}) collective-permute-start(f32[128,512]{0,1:T(8,128)S(1)} %pad_maximum_fusion.7), channel_id=1, source_target_pairs={{0,2},{1,3},{2,0},{3,1},{4,6},{5,7},{6,4},{7,5},{8,10},{9,11},{10,... | collective-permute-start | bytes 786440 | tf_op jit(solution)/shard_map/ppermute | solution.py:101
  166.7 2.0 collective-permute-start.9
  183.8 42.0 %copy-start.3 = (f32[128,128]{1,0:T(8,128)S(1)}, f32[128,128]{1,0:T(8,128)}, u32[]{:S(2)}) copy-start(f32[128,128]{1,0:T(8,128)} %get-tuple-element.14) | copy-start | bytes 196612
  189.1 62.9 %copy-start = (f32[128,128]{1,0:T(8,128)S(1)}, f32[128,128]{1,0:T(8,128)}, u32[]{:S(2)}) copy-start(f32[128,128]{1,0:T(8,128)} %get-tuple-element.10) | copy-start | bytes 196612
  204.3 47.7 %copy-start.1 = (f32[128,128]{1,0:T(8,128)S(1)}, f32[128,128]{1,0:T(8,128)}, u32[]{:S(2)}) copy-start(f32[128,128]{1,0:T(8,128)} %get-tuple-element.11) | copy-start | bytes 196612
  223.2 28.9 %copy-start.2 = (f32[128,128]{1,0:T(8,128)S(1)}, f32[128,128]{1,0:T(8,128)}, u32[]{:S(2)}) copy-start(f32[128,128]{1,0:T(8,128)} %get-tuple-element.12) | copy-start | bytes 196612

commit v3 on v2

--- a/solution.py
+++ b/solution.py
@@ -4,7 +4,6 @@
 import jax.numpy as jnp
 from jax import lax
 from jax.experimental import pallas as pl
-from jax.experimental.pallas import tpu as pltpu
 from jax.sharding import PartitionSpec as P
 
 AXES = ("wide", "narrow")
@@ -14,26 +13,23 @@
     return jnp.dot(a, b, precision=lax.Precision.HIGHEST, preferred_element_type=jnp.float32)
 
 
-def _diag_kernel(a_ref, r_ref, w_ref, s_ref):
+def _diag_kernel(a_ref, r_ref, w_ref):
     b = a_ref.shape[0]
-    s_ref[...] = a_ref[...]
     rows = lax.broadcasted_iota(jnp.int32, (b, 1), 0)
     lanes = lax.broadcasted_iota(jnp.int32, (1, b), 1)
-    w_ref[...] = (lax.broadcasted_iota(jnp.int32, (b, b), 0)
-                  == lax.broadcasted_iota(jnp.int32, (b, b), 1)).astype(jnp.float32)
+    a = a_ref[...]
+    w = (lax.broadcasted_iota(jnp.int32, (b, b), 0)
+         == lax.broadcasted_iota(jnp.int32, (b, b), 1)).astype(jnp.float32)
     for j in range(b):
-        lo = (j // 8) * 8
-        a = s_ref[lo:, :]
-        d = a[j - lo:j - lo + 1, j:j + 1]
-        s = 1.0 / jnp.sqrt(d)
-        row = jnp.where(lanes >= j, a[j - lo:j - lo + 1, :] * s, 0.0)
-        col = jnp.where(rows[lo:] >= j, a[:, j:j + 1] * s, 0.0)
+        s = lax.rsqrt(a[j:j + 1, j:j + 1])
+        row = jnp.where(lanes >= j, a[j:j + 1, :] * s, 0.0)
+        col = jnp.where(rows >= j, a[:, j:j + 1] * s, 0.0)
         r_ref[j:j + 1, :] = row
-        s_ref[lo:, :] = a - col * row
-        wrow = w_ref[j:j + 1, :] * s
-        w_ref[j:j + 1, :] = wrow
-        below = jnp.where(rows[lo:] > j, col, 0.0)
-        w_ref[lo:, :] = w_ref[lo:, :] - below * wrow
+        a = a - col * row
+        wrow = w[j:j + 1, :] * s
+        below = jnp.where(rows > j, col, 0.0)
+        w = w * jnp.where(rows == j, s, 1.0) - below * wrow
+    w_ref[...] = w
 
 
 def _diag_pair(block):
@@ -43,7 +39,6 @@
         _diag_kernel,
         out_shape=(jax.ShapeDtypeStruct((b, b), jnp.float32),
                    jax.ShapeDtypeStruct((b, b), jnp.float32)),
-        scratch_shapes=[pltpu.VMEM((b, b), jnp.float32)],
         cost_estimate=pl.CostEstimate(flops=4 * b * b * b, transcendentals=b,
                                       bytes_accessed=12 * b * b),
     )(sym)

time: 274 us -> 260 us (0.949); the launches traced: 269 us -> 258 us
  Pallas kernels: 57.1 us -> 46.4 us
    pallas_call x4, Pallas kernels: 57.1 us -> 46.4 us  [_diag_pair(): pl.pallas_call(_diag_kernel, out_shape=(jax.ShapeDtypeStruct((b, b), jnp....]
where the time goes in v3:
time: 260 us; the launch traced here: 258 us
  waiting for transfers between devices  138 us (53%)
  Pallas kernels  46.4 us (18%)
  matrix products  38.8 us (15%)
  local copies, waits for them, and re-layouts  17 us (7%)
  starting transfers between devices  14.2 us (5%)
    all_to_all x1, waiting for transfers between devices, per_device(): lax.all_to_all(sample_t, AXES, split_axis=1, concat_axis=0, tiled=True)  93.9 us
    pallas_call x4, Pallas kernels, _diag_pair(): pl.pallas_call(_diag_kernel, out_shape=(jax.ShapeDtypeStruct((b, b), jnp....  46.4 us
    ppermute x5, waiting for transfers between devices, sum_by_halving(): recv = lax.ppermute(buf, AXES, _pair(count, 1 << k))  22.8 us
    ppermute x5, waiting for transfers between devices, sum_by_halving(): buf = keep + lax.ppermute(send, AXES, _pair(count, 1 << k))  21.6 us
    dot_general x22, matrix products, _mm(): jnp.dot(a, b, precision=lax.Precision.HIGHEST, preferred_element_type=jnp...  19 us
    dot_general x1, matrix products, per_device(): lax.dot_general(rows_t, inverse, (((0,), (0,)), ((), ())), precision=lax....  10.2 us
    dot_general x1, matrix products, per_device(): jnp.dot(rows_t, rows_t.T, precision=lax.Precision.HIGHEST, preferred_elem...  9.59 us
    all_to_all x1, starting transfers between devices, per_device(): lax.all_to_all(sample_t, AXES, split_axis=1, concat_axis=0, tiled=True)  7.43 us
  transfers between devices with their start and end apart: 11, of which 11 were waited for; matrix products, arithmetic and copies ran while one was open for 0% of the time, Pallas kernels for 0%

profile of v3, /device:TPU:0, one launch (start us, length us, event | category | flops | bytes accessed | tf_op | source)
XLA Modules:
  0.0 258.2 jit_solution(4244730422111956266)
XLA Ops:
  0.6 4.7 %copy.144 = f32[2,32,8,2048]{3,2,0,1:T(8,128)} copy(f32[2,32,8,2048]{3,2,1,0:T(8,128)} %bitcast.67) | data formatting | bytes 8388608 | tf_op jit(solution)/shard_map/all_to_all | solution.py:107
  5.3 7.4 %all-to-all-start = ((f32[16,32,2048]{2,0,1:T(8,128)}), f32[16,32,2048]{2,0,1:T(8,128)}, u32[]{:S(2)}, u32[]{:S(2)}) async-start(f32[16,32,2048]{2,0,1:T(8,128)} %bitcast.66), calls=%async_computation | async-start | bytes 8388608 | tf_op jit(solution)/shard_map/all_to_all | solution.py:107
  12.8 93.9 %all-to-all-done = f32[16,32,2048]{2,0,1:T(8,128)} async-done(((f32[16,32,2048]{2,0,1:T(8,128)}), f32[16,32,2048]{2,0,1:T(8,128)}, u32[]{:S(2)}, u32[]{:S(2)}) %all-to-all-start) | async-done | bytes 4194336 | tf_op jit(solution)/shard_map/all_to_all | solution.py:107
  106.6 9.6 %fusion.57 = f32[512,512]{1,0:T(8,128)S(1)} fusion(f32[512,2048]{1,0:T(8,128)} %bitcast.1), kind=kOutput, calls=%fused_computation.107 | convolution fusion | flops 6442450944 | bytes 5242880 | tf_op jit(solution)/shard_map/dot_general | solution.py:108
  116.4 1.9 collective-permute-done
  118.4 1.3 collective-permute-start.1
  119.7 7.1 %collective-permute-done.1 = f32[128,512]{1,0:T(8,128)S(1)} collective-permute-done((f32[128,512]{1,0:T(8,128)S(1)}, f32[128,512]{1,0:T(8,128)S(1)}, u32[]{:S(2)}, u32[]{:S(2)}) %collective-permute-start.1) | collective-permute-done | bytes 262176 | tf_op jit(solution)/shard_map/ppermute | solution.py:93
  128.2 3.7 %collective-permute-done.2 = f32[64,512]{1,0:T(8,128)S(1)} collective-permute-done((f32[64,512]{1,0:T(8,128)S(1)}, f32[64,512]{1,0:T(8,128)S(1)}, u32[]{:S(2)}, u32[]{:S(2)}) %collective-permute-start.2) | collective-permute-done | bytes 131104 | tf_op jit(solution)/shard_map/ppermute | solution.py:93
  132.0 4.2 %collective-permute-done.3 = f32[32,512]{1,0:T(8,128)S(1)} collective-permute-done((f32[32,512]{1,0:T(8,128)S(1)}, f32[32,512]{1,0:T(8,128)S(1)}, u32[]{:S(2)}, u32[]{:S(2)}) %collective-permute-start.3) | collective-permute-done | bytes 65568 | tf_op jit(solution)/shard_map/ppermute | solution.py:93
  137.0 4.7 %collective-permute-done.4 = f32[16,512]{1,0:T(8,128)S(1)} collective-permute-done((f32[16,512]{1,0:T(8,128)S(1)}, f32[16,512]{1,0:T(8,128)S(1)}, u32[]{:S(2)}, u32[]{:S(2)}) %collective-permute-start.4) | collective-permute-done | bytes 32800 | tf_op jit(solution)/shard_map/ppermute | solution.py:93
  142.2 4.4 %collective-permute-done.5 = f32[16,512]{1,0:T(8,128)S(1)} collective-permute-done((f32[16,512]{1,0:T(8,128)S(1)}, f32[16,512]{1,0:T(8,128)S(1)}, u32[]{:S(2)}, u32[]{:S(2)}) %collective-permute-start.5) | collective-permute-done | bytes 32800 | tf_op jit(solution)/shard_map/ppermute | solution.py:96
  146.9 6.3 %collective-permute-done.6 = f32[32,512]{0,1:T(8,128)S(1)} collective-permute-done((f32[32,512]{0,1:T(8,128)S(1)}, f32[32,512]{0,1:T(8,128)S(1)}, u32[]{:S(2)}, u32[]{:S(2)}) %collective-permute-start.6) | collective-permute-done | bytes 65568 | tf_op jit(solution)/shard_map/ppermute | solution.py:96
  153.4 1.3 collective-permute-start.7
  154.7 5.1 %collective-permute-done.7 = f32[64,512]{0,1:T(8,128)S(1)} collective-permute-done((f32[64,512]{0,1:T(8,128)S(1)}, f32[64,512]{0,1:T(8,128)S(1)}, u32[]{:S(2)}, u32[]{:S(2)}) %collective-permute-start.7) | collective-permute-done | bytes 131104 | tf_op jit(solution)/shard_map/ppermute | solution.py:96
  160.1 1.4 collective-permute-start.8
  161.5 5.1 %collective-permute-done.8 = f32[128,512]{0,1:T(8,128)S(1)} collective-permute-done((f32[128,512]{0,1:T(8,128)S(1)}, f32[128,512]{0,1:T(8,128)S(1)}, u32[]{:S(2)}, u32[]{:S(2)}) %collective-permute-start.8) | collective-permute-done | bytes 262176 | tf_op jit(solution)/shard_map/ppermute | solution.py:96
  166.8 1.9 collective-permute-done.9
  169.6 11.5 %shard_map.30 = (f32[128,128]{1,0:T(8,128)}, f32[128,128]{1,0:T(8,128)}) custom-call(f32[128,128]{1,0:T(8,128)} %copy.100.a_ref), custom_call_target="tpu_custom_call" | custom-call | flops 8388608 | bytes 196608 | tf_op jit(solution)/shard_map/pallas_call | solution.py:38
  187.3 11.7 %shard_map.31 = (f32[128,128]{1,0:T(8,128)}, f32[128,128]{1,0:T(8,128)}) custom-call(f32[128,128]{1,0:T(8,128)} %copy.104.a_ref), custom_call_target="tpu_custom_call" | custom-call | flops 8388608 | bytes 196608 | tf_op jit(solution)/shard_map/pallas_call | solution.py:38
  203.6 11.5 %shard_map.32 = (f32[128,128]{1,0:T(8,128)}, f32[128,128]{1,0:T(8,128)}) custom-call(f32[128,128]{1,0:T(8,128)} %fusion.36.a_ref), custom_call_target="tpu_custom_call" | custom-call | flops 8388608 | bytes 196608 | tf_op jit(solution)/shard_map/pallas_call | solution.py:38
  224.9 11.7 %shard_map.33 = (f32[128,128]{1,0:T(8,128)}, f32[128,128]{1,0:T(8,128)}) custom-call(f32[128,128]{1,0:T(8,128)} %broadcast_multiply_fusion.a_ref), custom_call_target="tpu_custom_call" | custom-call | flops 8388608 | bytes 196608 | tf_op jit(solution)/shard_map/pallas_call | solution.py:38
  241.3 10.2 %multiply_bitcast_fusion = f32[2048,512]{0,1:T(8,128)} fusion(f32[512,2048]{1,0:T(8,128)} %bitcast.1, f32[128,256]{1,0:T(8,128)S(1)} %broadcast.17, f32[128,128]{1,0:T(8,128)S(1)} %broadcast_in_dim.3, f32[128,128]{1,0:T(8,128)S(1)} %copy-done, f32[128,128]{1,0:T(8,128)} %get-tuple-element.13, f32[128,128]{1,0:T(8,128)S(1)} %convolution_negate_fusion, ...), kind=kOutput, calls=%fused_computation.1 | convolution fusion | flops 6446907392 | bytes 9240576 | tf_op jit(solution)/shard_map/dot_general | solution.py:117
  251.5 5.3 %copy.126 = f32[2048,512]{1,0:T(8,128)} copy(f32[2048,512]{0,1:T(8,128)} %multiply_bitcast_fusion) | data formatting | bytes 8388608
  256.9 1.3 copy.127
  (87 shorter events, 29.7 us)
Async XLA Ops:
  5.3 101.3 %all-to-all-start = ((f32[16,32,2048]{2,0,1:T(8,128)}), f32[16,32,2048]{2,0,1:T(8,128)}, u32[]{:S(2)}, u32[]{:S(2)}) async-start(f32[16,32,2048]{2,0,1:T(8,128)} %bitcast.66), calls=%async_computation | async-start | bytes 8388608 | tf_op jit(solution)/shard_map/all_to_all | solution.py:107
  116.3 2.0 collective-permute-start
  118.4 8.4 %collective-permute-start.1 = (f32[128,512]{1,0:T(8,128)S(1)}, f32[128,512]{1,0:T(8,128)S(1)}, u32[]{:S(2)}, u32[]{:S(2)}) collective-permute-start(f32[128,512]{1,0:T(8,128)S(1)} %constant_dynamic-slice_fusion.3), channel_id=1, source_target_pairs={{0,2},{1,3},{2,0},{3,1},{4,6},{5,7},{6,4},{7,5},{8,10},{9,11},{10,... | collective-permute-start | bytes 786440 | tf_op jit(solution)/shard_map/ppermute | solution.py:93
  126.9 5.0 %collective-permute-start.2 = (f32[64,512]{1,0:T(8,128)S(1)}, f32[64,512]{1,0:T(8,128)S(1)}, u32[]{:S(2)}, u32[]{:S(2)}) collective-permute-start(f32[64,512]{1,0:T(8,128)S(1)} %constant_dynamic-slice_fusion.2), channel_id=1, source_target_pairs={{0,4},{1,5},{2,6},{3,7},{4,0},{5,1},{6,2},{7,3},{8,12},{9,13},{10,... | collective-permute-start | bytes 393224 | tf_op jit(solution)/shard_map/ppermute | solution.py:93
  131.9 4.3 %collective-permute-start.3 = (f32[32,512]{1,0:T(8,128)S(1)}, f32[32,512]{1,0:T(8,128)S(1)}, u32[]{:S(2)}, u32[]{:S(2)}) collective-permute-start(f32[32,512]{1,0:T(8,128)S(1)} %constant_dynamic-slice_fusion.1), channel_id=1, source_target_pairs={{0,8},{1,9},{2,10},{3,11},{4,12},{5,13},{6,14},{7,15},{8,0},{9,1},... | collective-permute-start | bytes 196616 | tf_op jit(solution)/shard_map/ppermute | solution.py:93
  136.3 5.4 %collective-permute-start.4 = (f32[16,512]{1,0:T(8,128)S(1)}, f32[16,512]{1,0:T(8,128)S(1)}, u32[]{:S(2)}, u32[]{:S(2)}) collective-permute-start(f32[16,512]{1,0:T(8,128)S(1)} %constant_dynamic-slice_fusion), channel_id=1, source_target_pairs={{0,16},{1,17},{2,18},{3,19},{4,20},{5,21},{6,22},{7,23},{8,24},{9,... | collective-permute-start | bytes 98312 | tf_op jit(solution)/shard_map/ppermute | solution.py:93
  141.7 4.9 %collective-permute-start.5 = (f32[16,512]{1,0:T(8,128)S(1)}, f32[16,512]{1,0:T(8,128)S(1)}, u32[]{:S(2)}, u32[]{:S(2)}) collective-permute-start(f32[16,512]{1,0:T(8,128)S(1)} %dynamic-slice_add_fusion.4), channel_id=1, source_target_pairs={{0,16},{1,17},{2,18},{3,19},{4,20},{5,21},{6,22},{7,23},{8,24},{9,... | collective-permute-start | bytes 98312 | tf_op jit(solution)/shard_map/ppermute | solution.py:96
  146.8 6.4 %collective-permute-start.6 = (f32[32,512]{0,1:T(8,128)S(1)}, f32[32,512]{0,1:T(8,128)S(1)}, u32[]{:S(2)}, u32[]{:S(2)}) collective-permute-start(f32[32,512]{0,1:T(8,128)S(1)} %copy.96), channel_id=1, source_target_pairs={{0,8},{1,9},{2,10},{3,11},{4,12},{5,13},{6,14},{7,15},{8,0},{9,1},... | collective-permute-start | bytes 196616 | tf_op jit(solution)/shard_map/ppermute | solution.py:96
  153.4 6.4 %collective-permute-start.7 = (f32[64,512]{0,1:T(8,128)S(1)}, f32[64,512]{0,1:T(8,128)S(1)}, u32[]{:S(2)}, u32[]{:S(2)}) collective-permute-start(f32[64,512]{0,1:T(8,128)S(1)} %pad_maximum_fusion.6), channel_id=1, source_target_pairs={{0,4},{1,5},{2,6},{3,7},{4,0},{5,1},{6,2},{7,3},{8,12},{9,13},{10,... | collective-permute-start | bytes 393224 | tf_op jit(solution)/shard_map/ppermute | solution.py:96
  160.1 6.4 %collective-permute-start.8 = (f32[128,512]{0,1:T(8,128)S(1)}, f32[128,512]{0,1:T(8,128)S(1)}, u32[]{:S(2)}, u32[]{:S(2)}) collective-permute-start(f32[128,512]{0,1:T(8,128)S(1)} %pad_maximum_fusion.7), channel_id=1, source_target_pairs={{0,2},{1,3},{2,0},{3,1},{4,6},{5,7},{6,4},{7,5},{8,10},{9,11},{10,... | collective-permute-start | bytes 786440 | tf_op jit(solution)/shard_map/ppermute | solution.py:96
  166.7 2.0 collective-permute-start.9
  181.1 36.6 %copy-start.3 = (f32[128,128]{1,0:T(8,128)S(1)}, f32[128,128]{1,0:T(8,128)}, u32[]{:S(2)}) copy-start(f32[128,128]{1,0:T(8,128)} %get-tuple-element.14) | copy-start | bytes 196612
  186.4 54.8 %copy-start = (f32[128,128]{1,0:T(8,128)S(1)}, f32[128,128]{1,0:T(8,128)}, u32[]{:S(2)}) copy-start(f32[128,128]{1,0:T(8,128)} %get-tuple-element.10) | copy-start | bytes 196612
  199.0 42.3 %copy-start.1 = (f32[128,128]{1,0:T(8,128)S(1)}, f32[128,128]{1,0:T(8,128)}, u32[]{:S(2)}) copy-start(f32[128,128]{1,0:T(8,128)} %get-tuple-element.11) | copy-start | bytes 196612
  215.1 26.2 %copy-start.2 = (f32[128,128]{1,0:T(8,128)S(1)}, f32[128,128]{1,0:T(8,128)}, u32[]{:S(2)}) copy-start(f32[128,128]{1,0:T(8,128)} %get-tuple-element.12) | copy-start | bytes 196612

commit v4 on v0

--- a/solution.py
+++ b/solution.py
@@ -1,18 +1,77 @@
+import functools
 import math
 
 import jax
 import jax.numpy as jnp
 from jax import lax
+from jax.experimental import pallas as pl
+from jax.experimental.pallas import tpu as pltpu
 from jax.sharding import PartitionSpec as P
 
 AXES = ("wide", "narrow")
 
 
-def factor_pair(matrix):
-    lower = lax.linalg.cholesky(matrix)
-    identity = jnp.eye(matrix.shape[0], dtype=matrix.dtype)
-    solved = lax.linalg.triangular_solve(lower, identity, left_side=True, lower=True)
-    return (lower, solved)
+HI = lax.Precision.HIGHEST
+NT = (((1,), (1,)), ((), ()))
+
+
+def _nt(a, b):
+    return lax.dot_general(a, b, NT, precision=HI, preferred_element_type=jnp.float32)
+
+
+def _nn(a, b):
+    return jnp.dot(a, b, precision=HI, preferred_element_type=jnp.float32)
+
+
+def _chain(a, r_ref):
+    b = a.shape[0]
+    rows = lax.broadcasted_iota(jnp.int32, (b, 1), 0)
+    lanes = lax.broadcasted_iota(jnp.int32, (1, b), 1)
+    w = (lax.broadcasted_iota(jnp.int32, (b, b), 0)
+         == lax.broadcasted_iota(jnp.int32, (b, b), 1)).astype(jnp.float32)
+    for j in range(b):
+        s = lax.rsqrt(a[j:j + 1, j:j + 1])
+        row = jnp.where(lanes >= j, a[j:j + 1, :] * s, 0.0)
+        col = jnp.where(rows >= j, a[:, j:j + 1] * s, 0.0)
+        r_ref[j:j + 1, :] = row
+        a = a - col * row
+        wrow = w[j:j + 1, :] * s
+        below = jnp.where(rows > j, col, 0.0)
+        w = w * jnp.where(rows == j, s, 1.0) - below * wrow
+    return w
+
+
+def _factor_kernel(g_ref, l_ref, w_ref, t_ref, r_ref, *, b):
+    n = g_ref.shape[0]
+    nb = n // b
+    t_ref[...] = g_ref[...]
+    l_ref[...] = jnp.zeros_like(l_ref)
+    w_ref[...] = jnp.zeros_like(w_ref)
+    for k in range(nb):
+        lo, hi = k * b, (k + 1) * b
+        blk = t_ref[lo:hi, lo:hi]
+        w_kk = _chain((blk + blk.T) * 0.5, r_ref)
+        l_ref[lo:hi, lo:hi] = r_ref[...].T
+        w_ref[lo:hi, lo:hi] = w_kk
+        if k > 0:
+            acc = _nn(l_ref[lo:hi, :lo], w_ref[:lo, :lo])
+            w_ref[lo:hi, :lo] = -_nn(w_kk, acc)
+        if k < nb - 1:
+            panel = _nt(t_ref[hi:, lo:hi], w_kk)
+            l_ref[hi:, lo:hi] = panel
+            t_ref[hi:, hi:] = t_ref[hi:, hi:] - _nt(panel, panel)
+
+
+def factor_pair(matrix, b=128):
+    n = matrix.shape[0]
+    return pl.pallas_call(
+        functools.partial(_factor_kernel, b=b),
+        out_shape=(jax.ShapeDtypeStruct((n, n), jnp.float32),
+                   jax.ShapeDtypeStruct((n, n), jnp.float32)),
+        scratch_shapes=[pltpu.VMEM((n, n), jnp.float32), pltpu.VMEM((b, b), jnp.float32)],
+        cost_estimate=pl.CostEstimate(flops=2 * n * n * n, transcendentals=n,
+                                      bytes_accessed=12 * n * n),
+    )(matrix)
 
 
 def _pair(count, bit):

time: 337 us -> 229 us (0.68); the launches traced: 332 us -> 229 us
  other arithmetic: 123 us -> 1.55 us
  Pallas kernels: 0 us -> 45.9 us
  local copies, waits for them, and re-layouts: 26.4 us -> 11.6 us
  matrix products: 27.9 us -> 20.1 us
    another operation x16 -> x0, other arithmetic: 119 us -> none  [the longest x14 78.9 us: factor_pair(): lower = lax.linalg.cholesky(matrix)]
    pallas_call x0 -> x1, Pallas kernels: none -> 45.9 us  [factor_pair(): pl.pallas_call(functools.partial(_factor_kernel, b=b), out_shape=(jax.Sha...]
    another operation x17 -> x0, local copies, waits for them, and re-layouts: 14.5 us -> none
    another operation x13 -> x0, matrix products: 8.32 us -> none  [the longest x7 6.44 us: factor_pair(): lax.linalg.triangular_solve(lower, identity, left_side=True, lower=True)]
  transfers between devices with their start and end apart: 11 -> 11, of which waited for: 10 -> 11; matrix products, arithmetic and copies ran while one was open for 1% -> 0% of each run, Pallas kernels for 0% -> 0%
where the time goes in v4:
time: 229 us
  waiting for transfers between devices  135 us (59%)
  Pallas kernels  45.9 us (20%)
  matrix products  20.1 us (9%)
  starting transfers between devices  14.1 us (6%)
  local copies, waits for them, and re-layouts  11.6 us (5%)
    all_to_all x1, waiting for transfers between devices, per_device(): lax.all_to_all(sample_t, AXES, split_axis=1, concat_axis=0, tiled=True)  93.9 us
    pallas_call x1, Pallas kernels, factor_pair(): pl.pallas_call(functools.partial(_factor_kernel, b=b), out_shape=(jax.Sha...  45.9 us
    ppermute x5, waiting for transfers between devices, sum_by_halving(): buf = keep + lax.ppermute(send, AXES, _pair(count, 1 << k))  21.6 us
    ppermute x5, waiting for transfers between devices, sum_by_halving(): recv = lax.ppermute(buf, AXES, _pair(count, 1 << k))  19.3 us
    dot_general x1, matrix products, per_device(): lax.dot_general(rows_t, inverse, (((0,), (0,)), ((), ())), precision=lax....  10.5 us
    dot_general x1, matrix products, per_device(): jnp.dot(rows_t, rows_t.T, precision=lax.Precision.HIGHEST, preferred_elem...  9.59 us
    all_to_all x1, starting transfers between devices, per_device(): lax.all_to_all(sample_t, AXES, split_axis=1, concat_axis=0, tiled=True)  7.43 us
    unnamed x4, local copies, waits for them, and re-layouts  6.74 us
  transfers between devices with their start and end apart: 11, of which 11 were waited for; matrix products, arithmetic and copies ran while one was open for 0% of the time, Pallas kernels for 0%

profile of v4, /device:TPU:0, one launch (start us, length us, event | category | flops | bytes accessed | tf_op | source)
XLA Modules:
  0.0 228.8 jit_solution(4642610339433943387)
XLA Ops:
  0.6 4.7 %copy.15 = f32[2,32,8,2048]{3,2,0,1:T(8,128)} copy(f32[2,32,8,2048]{3,2,1,0:T(8,128)} %bitcast.16) | data formatting | bytes 8388608 | tf_op jit(solution)/shard_map/all_to_all | solution.py:105
  5.3 7.4 %all-to-all-start = ((f32[16,32,2048]{2,0,1:T(8,128)}), f32[16,32,2048]{2,0,1:T(8,128)}, u32[]{:S(2)}, u32[]{:S(2)}) async-start(f32[16,32,2048]{2,0,1:T(8,128)} %bitcast.15), calls=%async_computation | async-start | bytes 8388608 | tf_op jit(solution)/shard_map/all_to_all | solution.py:105
  12.8 93.9 %all-to-all-done = f32[16,32,2048]{2,0,1:T(8,128)} async-done(((f32[16,32,2048]{2,0,1:T(8,128)}), f32[16,32,2048]{2,0,1:T(8,128)}, u32[]{:S(2)}, u32[]{:S(2)}) %all-to-all-start) | async-done | bytes 4194336 | tf_op jit(solution)/shard_map/all_to_all | solution.py:105
  106.6 9.6 %fusion = f32[512,512]{1,0:T(8,128)S(1)} fusion(f32[512,2048]{1,0:T(8,128)} %bitcast.1), kind=kOutput, calls=%fused_computation.28 | convolution fusion | flops 6442450944 | bytes 5242880 | tf_op jit(solution)/shard_map/dot_general | solution.py:106
  116.4 1.9 collective-permute-done
  118.4 1.3 collective-permute-start.1
  119.7 7.1 %collective-permute-done.1 = f32[128,512]{1,0:T(8,128)S(1)} collective-permute-done((f32[128,512]{1,0:T(8,128)S(1)}, f32[128,512]{1,0:T(8,128)S(1)}, u32[]{:S(2)}, u32[]{:S(2)}) %collective-permute-start.1) | collective-permute-done | bytes 262176 | tf_op jit(solution)/shard_map/ppermute | solution.py:91
  126.9 1.3 collective-permute-start.2
  128.2 3.7 %collective-permute-done.2 = f32[64,512]{1,0:T(8,128)S(1)} collective-permute-done((f32[64,512]{1,0:T(8,128)S(1)}, f32[64,512]{1,0:T(8,128)S(1)}, u32[]{:S(2)}, u32[]{:S(2)}) %collective-permute-start.2) | collective-permute-done | bytes 131104 | tf_op jit(solution)/shard_map/ppermute | solution.py:91
  132.0 4.2 %collective-permute-done.3 = f32[32,512]{1,0:T(8,128)S(1)} collective-permute-done((f32[32,512]{1,0:T(8,128)S(1)}, f32[32,512]{1,0:T(8,128)S(1)}, u32[]{:S(2)}, u32[]{:S(2)}) %collective-permute-start.3) | collective-permute-done | bytes 65568 | tf_op jit(solution)/shard_map/ppermute | solution.py:91
  136.3 0.7 collective-permute-start.4
  137.0 4.7 %collective-permute-done.4 = f32[16,512]{1,0:T(8,128)S(1)} collective-permute-done((f32[16,512]{1,0:T(8,128)S(1)}, f32[16,512]{1,0:T(8,128)S(1)}, u32[]{:S(2)}, u32[]{:S(2)}) %collective-permute-start.4) | collective-permute-done | bytes 32800 | tf_op jit(solution)/shard_map/ppermute | solution.py:91
  142.2 4.3 %collective-permute-done.5 = f32[16,512]{1,0:T(8,128)S(1)} collective-permute-done((f32[16,512]{1,0:T(8,128)S(1)}, f32[16,512]{1,0:T(8,128)S(1)}, u32[]{:S(2)}, u32[]{:S(2)}) %collective-permute-start.5) | collective-permute-done | bytes 32800 | tf_op jit(solution)/shard_map/ppermute | solution.py:94
  146.6 4.2 %collective-permute-done.6 = f32[32,512]{1,0:T(8,128)S(1)} collective-permute-done((f32[32,512]{1,0:T(8,128)S(1)}, f32[32,512]{1,0:T(8,128)S(1)}, u32[]{:S(2)}, u32[]{:S(2)}) %collective-permute-start.6) | collective-permute-done | bytes 65568 | tf_op jit(solution)/shard_map/ppermute | solution.py:94
  150.9 1.3 collective-permute-start.7
  152.2 3.7 %collective-permute-done.7 = f32[64,512]{1,0:T(8,128)S(1)} collective-permute-done((f32[64,512]{1,0:T(8,128)S(1)}, f32[64,512]{1,0:T(8,128)S(1)}, u32[]{:S(2)}, u32[]{:S(2)}) %collective-permute-start.7) | collective-permute-done | bytes 131104 | tf_op jit(solution)/shard_map/ppermute | solution.py:94
  156.0 1.3 collective-permute-start.8
  157.3 5.1 %collective-permute-done.8 = f32[128,512]{1,0:T(8,128)S(1)} collective-permute-done((f32[128,512]{1,0:T(8,128)S(1)}, f32[128,512]{1,0:T(8,128)S(1)}, u32[]{:S(2)}, u32[]{:S(2)}) %collective-permute-start.8) | collective-permute-done | bytes 262176 | tf_op jit(solution)/shard_map/ppermute | solution.py:94
  162.6 1.9 collective-permute-done.9
  164.6 1.0 pad_maximum_fusion.g_ref
  165.6 45.9 %shard_map.30 = (f32[512,512]{1,0:T(8,128)}, f32[512,512]{1,0:T(8,128)}) custom-call(f32[512,512]{1,0:T(8,128)} %pad_maximum_fusion.g_ref), custom_call_target="tpu_custom_call" | custom-call | flops 268435456 | bytes 3145728 | tf_op jit(solution)/shard_map/pallas_call | solution.py:67
  211.5 10.5 %multiply_bitcast_fusion = f32[2048,512]{0,1:T(8,128)} fusion(f32[512,512]{1,0:T(8,128)} %get-tuple-element.4, f32[512,2048]{1,0:T(8,128)} %bitcast.1), kind=kOutput, calls=%fused_computation.1 | convolution fusion | flops 6443499520 | bytes 9437184 | tf_op jit(solution)/shard_map/dot_general | solution.py:115
  222.0 5.4 %copy.11 = f32[2048,512]{1,0:T(8,128)} copy(f32[2048,512]{0,1:T(8,128)} %multiply_bitcast_fusion) | data formatting | bytes 8388608
  227.5 1.3 copy.12
  (27 shorter events, 1.4 us)
Async XLA Ops:
  5.3 101.3 %all-to-all-start = ((f32[16,32,2048]{2,0,1:T(8,128)}), f32[16,32,2048]{2,0,1:T(8,128)}, u32[]{:S(2)}, u32[]{:S(2)}) async-start(f32[16,32,2048]{2,0,1:T(8,128)} %bitcast.15), calls=%async_computation | async-start | bytes 8388608 | tf_op jit(solution)/shard_map/all_to_all | solution.py:105
  116.3 2.0 collective-permute-start
  118.4 8.4 %collective-permute-start.1 = (f32[128,512]{1,0:T(8,128)S(1)}, f32[128,512]{1,0:T(8,128)S(1)}, u32[]{:S(2)}, u32[]{:S(2)}) collective-permute-start(f32[128,512]{1,0:T(8,128)S(1)} %constant_dynamic-slice_fusion.3), channel_id=1, source_target_pairs={{0,2},{1,3},{2,0},{3,1},{4,6},{5,7},{6,4},{7,5},{8,10},{9,11},{10,... | collective-permute-start | bytes 786440 | tf_op jit(solution)/shard_map/ppermute | solution.py:91
  126.9 5.0 %collective-permute-start.2 = (f32[64,512]{1,0:T(8,128)S(1)}, f32[64,512]{1,0:T(8,128)S(1)}, u32[]{:S(2)}, u32[]{:S(2)}) collective-permute-start(f32[64,512]{1,0:T(8,128)S(1)} %constant_dynamic-slice_fusion.2), channel_id=1, source_target_pairs={{0,4},{1,5},{2,6},{3,7},{4,0},{5,1},{6,2},{7,3},{8,12},{9,13},{10,... | collective-permute-start | bytes 393224 | tf_op jit(solution)/shard_map/ppermute | solution.py:91
  131.9 4.3 %collective-permute-start.3 = (f32[32,512]{1,0:T(8,128)S(1)}, f32[32,512]{1,0:T(8,128)S(1)}, u32[]{:S(2)}, u32[]{:S(2)}) collective-permute-start(f32[32,512]{1,0:T(8,128)S(1)} %constant_dynamic-slice_fusion.1), channel_id=1, source_target_pairs={{0,8},{1,9},{2,10},{3,11},{4,12},{5,13},{6,14},{7,15},{8,0},{9,1},... | collective-permute-start | bytes 196616 | tf_op jit(solution)/shard_map/ppermute | solution.py:91
  136.3 5.4 %collective-permute-start.4 = (f32[16,512]{1,0:T(8,128)S(1)}, f32[16,512]{1,0:T(8,128)S(1)}, u32[]{:S(2)}, u32[]{:S(2)}) collective-permute-start(f32[16,512]{1,0:T(8,128)S(1)} %constant_dynamic-slice_fusion), channel_id=1, source_target_pairs={{0,16},{1,17},{2,18},{3,19},{4,20},{5,21},{6,22},{7,23},{8,24},{9,... | collective-permute-start | bytes 98312 | tf_op jit(solution)/shard_map/ppermute | solution.py:91
  141.7 4.8 %collective-permute-start.5 = (f32[16,512]{1,0:T(8,128)S(1)}, f32[16,512]{1,0:T(8,128)S(1)}, u32[]{:S(2)}, u32[]{:S(2)}) collective-permute-start(f32[16,512]{1,0:T(8,128)S(1)} %dynamic-slice_add_fusion.4), channel_id=1, source_target_pairs={{0,16},{1,17},{2,18},{3,19},{4,20},{5,21},{6,22},{7,23},{8,24},{9,... | collective-permute-start | bytes 98312 | tf_op jit(solution)/shard_map/ppermute | solution.py:94
  146.5 4.3 %collective-permute-start.6 = (f32[32,512]{1,0:T(8,128)S(1)}, f32[32,512]{1,0:T(8,128)S(1)}, u32[]{:S(2)}, u32[]{:S(2)}) collective-permute-start(f32[32,512]{1,0:T(8,128)S(1)} %pad_maximum_fusion.4), channel_id=1, source_target_pairs={{0,8},{1,9},{2,10},{3,11},{4,12},{5,13},{6,14},{7,15},{8,0},{9,1},... | collective-permute-start | bytes 196616 | tf_op jit(solution)/shard_map/ppermute | solution.py:94
  150.9 5.0 %collective-permute-start.7 = (f32[64,512]{1,0:T(8,128)S(1)}, f32[64,512]{1,0:T(8,128)S(1)}, u32[]{:S(2)}, u32[]{:S(2)}) collective-permute-start(f32[64,512]{1,0:T(8,128)S(1)} %pad_maximum_fusion.3), channel_id=1, source_target_pairs={{0,4},{1,5},{2,6},{3,7},{4,0},{5,1},{6,2},{7,3},{8,12},{9,13},{10,... | collective-permute-start | bytes 393224 | tf_op jit(solution)/shard_map/ppermute | solution.py:94
  156.0 6.4 %collective-permute-start.8 = (f32[128,512]{1,0:T(8,128)S(1)}, f32[128,512]{1,0:T(8,128)S(1)}, u32[]{:S(2)}, u32[]{:S(2)}) collective-permute-start(f32[128,512]{1,0:T(8,128)S(1)} %pad_maximum_fusion.2), channel_id=1, source_target_pairs={{0,2},{1,3},{2,0},{3,1},{4,6},{5,7},{6,4},{7,5},{8,10},{9,11},{10,... | collective-permute-start | bytes 786440 | tf_op jit(solution)/shard_map/ppermute | solution.py:94
  162.5 2.0 collective-permute-start.9
  222.0 5.4 %copy-start = (f32[512,512]{1,0:T(8,128)S(1)}, f32[512,512]{1,0:T(8,128)}, u32[]{:S(2)}) copy-start(f32[512,512]{1,0:T(8,128)} %get-tuple-element.5) | copy-start | bytes 3145732

commit v5 on v4

--- a/solution.py
+++ b/solution.py
@@ -74,6 +74,25 @@
     )(matrix)
 
 
+def _basis_kernel(rt_ref, w_ref, o_ref, *, scale):
+    y = _nn(w_ref[...], rt_ref[...])
+    o_ref[...] = y.T * scale
+
+
+def basis_rows(rows_t, lower_inv, scale, blk=256):
+    k, m = rows_t.shape
+    return pl.pallas_call(
+        functools.partial(_basis_kernel, scale=scale),
+        grid=(m // blk,),
+        in_specs=[pl.BlockSpec((k, blk), lambda i: (0, i)),
+                  pl.BlockSpec((k, k), lambda i: (0, 0))],
+        out_specs=pl.BlockSpec((blk, k), lambda i: (i, 0)),
+        out_shape=jax.ShapeDtypeStruct((m, k), jnp.float32),
+        cost_estimate=pl.CostEstimate(flops=2 * m * k * k, transcendentals=0,
+                                      bytes_accessed=4 * (2 * m * k + k * k)),
+    )(rows_t, lower_inv)
+
+
 def _pair(count, bit):
     return [(i, i ^ bit) for i in range(count)]
 
@@ -109,17 +128,10 @@
     gram_total = sum_by_halving(gram_local, count)
     lower, lower_inv = factor_pair(gram_total)
     upper_factor = lower.T
-    inverse = lower_inv.T
     total_rows = rows_t.shape[1] * count
     scale_root = math.sqrt(total_rows)
-    product = lax.dot_general(
-        rows_t,
-        inverse,
-        (((0,), (0,)), ((), ())),
-        precision=lax.Precision.HIGHEST,
-        preferred_element_type=jnp.float32,
-    )
-    return (product * scale_root, upper_factor / scale_root)
+    product = basis_rows(rows_t, lower_inv, scale_root)
+    return (product, upper_factor / scale_root)
 
 
 def solution(mesh):

time: 229 us -> 225 us (0.983)
  Pallas kernels: 45.9 us -> 57.7 us
  matrix products: 20.1 us -> 9.59 us
  local copies, waits for them, and re-layouts: 11.6 us -> 6.12 us
    pallas_call x0 -> x1, Pallas kernels: none -> 11.8 us  [basis_rows(): pl.pallas_call(functools.partial(_basis_kernel, scale=scale), grid=(m //...]
    dot_general x1 -> x0, matrix products: 10.5 us -> none  [per_device(): lax.dot_general(rows_t, inverse, (((0,), (0,)), ((), ())), precision=lax....]
    unnamed x4 -> x3, local copies, waits for them, and re-layouts: 6.74 us -> 1.31 us
where the time goes in v5:
time: 225 us
  waiting for transfers between devices  135 us (60%)
  Pallas kernels  57.7 us (26%)
  starting transfers between devices  14.1 us (6%)
  matrix products  9.59 us (4%)
  local copies, waits for them, and re-layouts  6.12 us (3%)
    all_to_all x1, waiting for transfers between devices, per_device(): lax.all_to_all(sample_t, AXES, split_axis=1, concat_axis=0, tiled=True)  93.9 us
    pallas_call x1, Pallas kernels, factor_pair(): pl.pallas_call(functools.partial(_factor_kernel, b=b), out_shape=(jax.Sha...  45.9 us
    ppermute x5, waiting for transfers between devices, sum_by_halving(): buf = keep + lax.ppermute(send, AXES, _pair(count, 1 << k))  21.6 us
    ppermute x5, waiting for transfers between devices, sum_by_halving(): recv = lax.ppermute(buf, AXES, _pair(count, 1 << k))  19.3 us
    pallas_call x1, Pallas kernels, basis_rows(): pl.pallas_call(functools.partial(_basis_kernel, scale=scale), grid=(m //...  11.8 us
    dot_general x1, matrix products, per_device(): jnp.dot(rows_t, rows_t.T, precision=lax.Precision.HIGHEST, preferred_elem...  9.59 us
    all_to_all x1, starting transfers between devices, per_device(): lax.all_to_all(sample_t, AXES, split_axis=1, concat_axis=0, tiled=True)  7.43 us
    all_to_all x1, local copies, waits for them, and re-layouts, per_device(): lax.all_to_all(sample_t, AXES, split_axis=1, concat_axis=0, tiled=True)  4.7 us
  transfers between devices with their start and end apart: 11, of which 11 were waited for; matrix products, arithmetic and copies ran while one was open for 0% of the time, Pallas kernels for 0%

profile of v5, /device:TPU:0, one launch (start us, length us, event | category | flops | bytes accessed | tf_op | source)
XLA Modules:
  0.0 224.8 jit_solution(2706466512250424989)
XLA Ops:
  0.6 4.7 %copy.7 = f32[2,32,8,2048]{3,2,0,1:T(8,128)} copy(f32[2,32,8,2048]{3,2,1,0:T(8,128)} %bitcast.12) | data formatting | bytes 8388608 | tf_op jit(solution)/shard_map/all_to_all | solution.py:124
  5.3 7.4 %all-to-all-start = ((f32[16,32,2048]{2,0,1:T(8,128)}), f32[16,32,2048]{2,0,1:T(8,128)}, u32[]{:S(2)}, u32[]{:S(2)}) async-start(f32[16,32,2048]{2,0,1:T(8,128)} %bitcast.11), calls=%async_computation | async-start | bytes 8388608 | tf_op jit(solution)/shard_map/all_to_all | solution.py:124
  12.8 93.9 %all-to-all-done = f32[16,32,2048]{2,0,1:T(8,128)} async-done(((f32[16,32,2048]{2,0,1:T(8,128)}), f32[16,32,2048]{2,0,1:T(8,128)}, u32[]{:S(2)}, u32[]{:S(2)}) %all-to-all-start) | async-done | bytes 4194336 | tf_op jit(solution)/shard_map/all_to_all | solution.py:124
  106.6 9.6 %fusion = f32[512,512]{1,0:T(8,128)S(1)} fusion(f32[512,2048]{1,0:T(8,128)} %bitcast.1.rt_ref), kind=kOutput, calls=%fused_computation.27 | convolution fusion | flops 6442450944 | bytes 5242880 | tf_op jit(solution)/shard_map/dot_general | solution.py:125
  116.4 1.9 collective-permute-done
  118.4 1.3 collective-permute-start.1
  119.7 7.1 %collective-permute-done.1 = f32[128,512]{1,0:T(8,128)S(1)} collective-permute-done((f32[128,512]{1,0:T(8,128)S(1)}, f32[128,512]{1,0:T(8,128)S(1)}, u32[]{:S(2)}, u32[]{:S(2)}) %collective-permute-start.1) | collective-permute-done | bytes 262176 | tf_op jit(solution)/shard_map/ppermute | solution.py:110
  126.9 1.3 collective-permute-start.2
  128.2 3.7 %collective-permute-done.2 = f32[64,512]{1,0:T(8,128)S(1)} collective-permute-done((f32[64,512]{1,0:T(8,128)S(1)}, f32[64,512]{1,0:T(8,128)S(1)}, u32[]{:S(2)}, u32[]{:S(2)}) %collective-permute-start.2) | collective-permute-done | bytes 131104 | tf_op jit(solution)/shard_map/ppermute | solution.py:110
  132.0 4.2 %collective-permute-done.3 = f32[32,512]{1,0:T(8,128)S(1)} collective-permute-done((f32[32,512]{1,0:T(8,128)S(1)}, f32[32,512]{1,0:T(8,128)S(1)}, u32[]{:S(2)}, u32[]{:S(2)}) %collective-permute-start.3) | collective-permute-done | bytes 65568 | tf_op jit(solution)/shard_map/ppermute | solution.py:110
  136.3 0.7 collective-permute-start.4
  137.0 4.7 %collective-permute-done.4 = f32[16,512]{1,0:T(8,128)S(1)} collective-permute-done((f32[16,512]{1,0:T(8,128)S(1)}, f32[16,512]{1,0:T(8,128)S(1)}, u32[]{:S(2)}, u32[]{:S(2)}) %collective-permute-start.4) | collective-permute-done | bytes 32800 | tf_op jit(solution)/shard_map/ppermute | solution.py:110
  141.7 0.5 collective-permute-start.5
  142.2 4.3 %collective-permute-done.5 = f32[16,512]{1,0:T(8,128)S(1)} collective-permute-done((f32[16,512]{1,0:T(8,128)S(1)}, f32[16,512]{1,0:T(8,128)S(1)}, u32[]{:S(2)}, u32[]{:S(2)}) %collective-permute-start.5) | collective-permute-done | bytes 32800 | tf_op jit(solution)/shard_map/ppermute | solution.py:113
  146.6 4.2 %collective-permute-done.6 = f32[32,512]{1,0:T(8,128)S(1)} collective-permute-done((f32[32,512]{1,0:T(8,128)S(1)}, f32[32,512]{1,0:T(8,128)S(1)}, u32[]{:S(2)}, u32[]{:S(2)}) %collective-permute-start.6) | collective-permute-done | bytes 65568 | tf_op jit(solution)/shard_map/ppermute | solution.py:113
  150.9 1.3 collective-permute-start.7
  152.2 3.7 %collective-permute-done.7 = f32[64,512]{1,0:T(8,128)S(1)} collective-permute-done((f32[64,512]{1,0:T(8,128)S(1)}, f32[64,512]{1,0:T(8,128)S(1)}, u32[]{:S(2)}, u32[]{:S(2)}) %collective-permute-start.7) | collective-permute-done | bytes 131104 | tf_op jit(solution)/shard_map/ppermute | solution.py:113
  156.0 1.3 collective-permute-start.8
  157.3 5.1 %collective-permute-done.8 = f32[128,512]{1,0:T(8,128)S(1)} collective-permute-done((f32[128,512]{1,0:T(8,128)S(1)}, f32[128,512]{1,0:T(8,128)S(1)}, u32[]{:S(2)}, u32[]{:S(2)}) %collective-permute-start.8) | collective-permute-done | bytes 262176 | tf_op jit(solution)/shard_map/ppermute | solution.py:113
  162.6 1.9 collective-permute-done.9
  164.6 1.0 pad_maximum_fusion.g_ref
  165.6 45.9 %shard_map.30 = (f32[512,512]{1,0:T(8,128)}, f32[512,512]{1,0:T(8,128)}) custom-call(f32[512,512]{1,0:T(8,128)} %pad_maximum_fusion.g_ref), custom_call_target="tpu_custom_call" | custom-call | flops 268435456 | bytes 3145728 | tf_op jit(solution)/shard_map/pallas_call | solution.py:67
  211.6 11.8 %shard_map.31 = f32[2048,512]{1,0:T(8,128)} custom-call(f32[512,2048]{1,0:T(8,128)} %bitcast.1.rt_ref, f32[512,512]{1,0:T(8,128)} %get-tuple-element.4.w_ref), custom_call_target="tpu_custom_call" | custom-call | flops 1073741824 | bytes 9437184 | tf_op jit(solution)/shard_map/pallas_call | solution.py:84
  223.5 1.3 copy.4
  (26 shorter events, 0.9 us)
Async XLA Ops:
  5.3 101.3 %all-to-all-start = ((f32[16,32,2048]{2,0,1:T(8,128)}), f32[16,32,2048]{2,0,1:T(8,128)}, u32[]{:S(2)}, u32[]{:S(2)}) async-start(f32[16,32,2048]{2,0,1:T(8,128)} %bitcast.11), calls=%async_computation | async-start | bytes 8388608 | tf_op jit(solution)/shard_map/all_to_all | solution.py:124
  116.3 2.0 collective-permute-start
  118.4 8.4 %collective-permute-start.1 = (f32[128,512]{1,0:T(8,128)S(1)}, f32[128,512]{1,0:T(8,128)S(1)}, u32[]{:S(2)}, u32[]{:S(2)}) collective-permute-start(f32[128,512]{1,0:T(8,128)S(1)} %constant_dynamic-slice_fusion.3), channel_id=1, source_target_pairs={{0,2},{1,3},{2,0},{3,1},{4,6},{5,7},{6,4},{7,5},{8,10},{9,11},{10,... | collective-permute-start | bytes 786440 | tf_op jit(solution)/shard_map/ppermute | solution.py:110
  126.9 5.0 %collective-permute-start.2 = (f32[64,512]{1,0:T(8,128)S(1)}, f32[64,512]{1,0:T(8,128)S(1)}, u32[]{:S(2)}, u32[]{:S(2)}) collective-permute-start(f32[64,512]{1,0:T(8,128)S(1)} %constant_dynamic-slice_fusion.2), channel_id=1, source_target_pairs={{0,4},{1,5},{2,6},{3,7},{4,0},{5,1},{6,2},{7,3},{8,12},{9,13},{10,... | collective-permute-start | bytes 393224 | tf_op jit(solution)/shard_map/ppermute | solution.py:110
  131.9 4.3 %collective-permute-start.3 = (f32[32,512]{1,0:T(8,128)S(1)}, f32[32,512]{1,0:T(8,128)S(1)}, u32[]{:S(2)}, u32[]{:S(2)}) collective-permute-start(f32[32,512]{1,0:T(8,128)S(1)} %constant_dynamic-slice_fusion.1), channel_id=1, source_target_pairs={{0,8},{1,9},{2,10},{3,11},{4,12},{5,13},{6,14},{7,15},{8,0},{9,1},... | collective-permute-start | bytes 196616 | tf_op jit(solution)/shard_map/ppermute | solution.py:110
  136.3 5.4 %collective-permute-start.4 = (f32[16,512]{1,0:T(8,128)S(1)}, f32[16,512]{1,0:T(8,128)S(1)}, u32[]{:S(2)}, u32[]{:S(2)}) collective-permute-start(f32[16,512]{1,0:T(8,128)S(1)} %constant_dynamic-slice_fusion), channel_id=1, source_target_pairs={{0,16},{1,17},{2,18},{3,19},{4,20},{5,21},{6,22},{7,23},{8,24},{9,... | collective-permute-start | bytes 98312 | tf_op jit(solution)/shard_map/ppermute | solution.py:110
  141.7 4.8 %collective-permute-start.5 = (f32[16,512]{1,0:T(8,128)S(1)}, f32[16,512]{1,0:T(8,128)S(1)}, u32[]{:S(2)}, u32[]{:S(2)}) collective-permute-start(f32[16,512]{1,0:T(8,128)S(1)} %dynamic-slice_add_fusion.4), channel_id=1, source_target_pairs={{0,16},{1,17},{2,18},{3,19},{4,20},{5,21},{6,22},{7,23},{8,24},{9,... | collective-permute-start | bytes 98312 | tf_op jit(solution)/shard_map/ppermute | solution.py:113
  146.5 4.3 %collective-permute-start.6 = (f32[32,512]{1,0:T(8,128)S(1)}, f32[32,512]{1,0:T(8,128)S(1)}, u32[]{:S(2)}, u32[]{:S(2)}) collective-permute-start(f32[32,512]{1,0:T(8,128)S(1)} %pad_maximum_fusion.4), channel_id=1, source_target_pairs={{0,8},{1,9},{2,10},{3,11},{4,12},{5,13},{6,14},{7,15},{8,0},{9,1},... | collective-permute-start | bytes 196616 | tf_op jit(solution)/shard_map/ppermute | solution.py:113
  150.9 5.0 %collective-permute-start.7 = (f32[64,512]{1,0:T(8,128)S(1)}, f32[64,512]{1,0:T(8,128)S(1)}, u32[]{:S(2)}, u32[]{:S(2)}) collective-permute-start(f32[64,512]{1,0:T(8,128)S(1)} %pad_maximum_fusion.3), channel_id=1, source_target_pairs={{0,4},{1,5},{2,6},{3,7},{4,0},{5,1},{6,2},{7,3},{8,12},{9,13},{10,... | collective-permute-start | bytes 393224 | tf_op jit(solution)/shard_map/ppermute | solution.py:113
  156.0 6.4 %collective-permute-start.8 = (f32[128,512]{1,0:T(8,128)S(1)}, f32[128,512]{1,0:T(8,128)S(1)}, u32[]{:S(2)}, u32[]{:S(2)}) collective-permute-start(f32[128,512]{1,0:T(8,128)S(1)} %pad_maximum_fusion.2), channel_id=1, source_target_pairs={{0,2},{1,3},{2,0},{3,1},{4,6},{5,7},{6,4},{7,5},{8,10},{9,11},{10,... | collective-permute-start | bytes 786440 | tf_op jit(solution)/shard_map/ppermute | solution.py:113
  162.5 2.0 collective-permute-start.9
  211.6 11.8 %copy-start = (f32[512,512]{1,0:T(8,128)S(1)}, f32[512,512]{1,0:T(8,128)}, u32[]{:S(2)}) copy-start(f32[512,512]{1,0:T(8,128)} %get-tuple-element.5) | copy-start | bytes 3145732

commit v6 on v5

--- a/solution.py
+++ b/solution.py
@@ -41,7 +41,7 @@
     return w
 
 
-def _factor_kernel(g_ref, l_ref, w_ref, t_ref, r_ref, *, b):
+def _factor_kernel(g_ref, l_ref, w_ref, u_ref, t_ref, r_ref, *, b, scale):
     n = g_ref.shape[0]
     nb = n // b
     t_ref[...] = g_ref[...]
@@ -60,13 +60,15 @@
             panel = _nt(t_ref[hi:, lo:hi], w_kk)
             l_ref[hi:, lo:hi] = panel
             t_ref[hi:, hi:] = t_ref[hi:, hi:] - _nt(panel, panel)
+    u_ref[...] = l_ref[...].T / scale
 
 
-def factor_pair(matrix, b=128):
+def factor_pair(matrix, scale, b=128):
     n = matrix.shape[0]
     return pl.pallas_call(
-        functools.partial(_factor_kernel, b=b),
+        functools.partial(_factor_kernel, b=b, scale=scale),
         out_shape=(jax.ShapeDtypeStruct((n, n), jnp.float32),
+                   jax.ShapeDtypeStruct((n, n), jnp.float32),
                    jax.ShapeDtypeStruct((n, n), jnp.float32)),
         scratch_shapes=[pltpu.VMEM((n, n), jnp.float32), pltpu.VMEM((b, b), jnp.float32)],
         cost_estimate=pl.CostEstimate(flops=2 * n * n * n, transcendentals=n,
@@ -79,7 +81,7 @@
     o_ref[...] = y.T * scale
 
 
-def basis_rows(rows_t, lower_inv, scale, blk=256):
+def basis_rows(rows_t, lower_inv, scale, blk=512):
     k, m = rows_t.shape
     return pl.pallas_call(
         functools.partial(_basis_kernel, scale=scale),
@@ -126,12 +128,11 @@
         rows_t, rows_t.T, precision=lax.Precision.HIGHEST, preferred_element_type=jnp.float32
     )
     gram_total = sum_by_halving(gram_local, count)
-    lower, lower_inv = factor_pair(gram_total)
-    upper_factor = lower.T
     total_rows = rows_t.shape[1] * count
     scale_root = math.sqrt(total_rows)
+    _, lower_inv, factor_out = factor_pair(gram_total, scale_root)
     product = basis_rows(rows_t, lower_inv, scale_root)
-    return (product, upper_factor / scale_root)
+    return (product, factor_out)
 
 
 def solution(mesh):

time: 225 us -> 223 us (level)
  no operation moved by 1% of the time
where the time goes in v6:
time: 223 us
  waiting for transfers between devices  135 us (61%)
  Pallas kernels  57 us (26%)
  starting transfers between devices  14.1 us (6%)
  matrix products  9.49 us (4%)
  local copies, waits for them, and re-layouts  4.81 us (2%)
    all_to_all x1, waiting for transfers between devices, per_device(): lax.all_to_all(sample_t, AXES, split_axis=1, concat_axis=0, tiled=True)  93.9 us
    pallas_call x1, Pallas kernels, factor_pair(): pl.pallas_call(functools.partial(_factor_kernel, b=b, scale=scale), out_s...  46.3 us
    ppermute x5, waiting for transfers between devices, sum_by_halving(): buf = keep + lax.ppermute(send, AXES, _pair(count, 1 << k))  21.7 us
    ppermute x5, waiting for transfers between devices, sum_by_halving(): recv = lax.ppermute(buf, AXES, _pair(count, 1 << k))  19.3 us
    pallas_call x1, Pallas kernels, basis_rows(): pl.pallas_call(functools.partial(_basis_kernel, scale=scale), grid=(m //...  10.7 us
    dot_general x1, matrix products, per_device(): jnp.dot(rows_t, rows_t.T, precision=lax.Precision.HIGHEST, preferred_elem...  9.49 us
    all_to_all x1, starting transfers between devices, per_device(): lax.all_to_all(sample_t, AXES, split_axis=1, concat_axis=0, tiled=True)  7.43 us
    all_to_all x1, local copies, waits for them, and re-layouts, per_device(): lax.all_to_all(sample_t, AXES, split_axis=1, concat_axis=0, tiled=True)  4.7 us
  transfers between devices with their start and end apart: 11, of which 11 were waited for; matrix products, arithmetic and copies ran while one was open for 0% of the time, Pallas kernels for 0%

profile of v6, /device:TPU:0, one launch (start us, length us, event | category | flops | bytes accessed | tf_op | source)
XLA Modules:
  0.0 222.5 jit_solution(16609367256389773328)
XLA Ops:
  0.6 4.7 %copy.6 = f32[2,32,8,2048]{3,2,0,1:T(8,128)} copy(f32[2,32,8,2048]{3,2,1,0:T(8,128)} %bitcast.10) | data formatting | bytes 8388608 | tf_op jit(solution)/shard_map/all_to_all | solution.py:126
  5.3 7.4 %all-to-all-start = ((f32[16,32,2048]{2,0,1:T(8,128)}), f32[16,32,2048]{2,0,1:T(8,128)}, u32[]{:S(2)}, u32[]{:S(2)}) async-start(f32[16,32,2048]{2,0,1:T(8,128)} %bitcast.9), calls=%async_computation | async-start | bytes 8388608 | tf_op jit(solution)/shard_map/all_to_all | solution.py:126
  12.8 93.9 %all-to-all-done = f32[16,32,2048]{2,0,1:T(8,128)} async-done(((f32[16,32,2048]{2,0,1:T(8,128)}), f32[16,32,2048]{2,0,1:T(8,128)}, u32[]{:S(2)}, u32[]{:S(2)}) %all-to-all-start) | async-done | bytes 4194336 | tf_op jit(solution)/shard_map/all_to_all | solution.py:126
  106.6 9.5 %fusion = f32[512,512]{1,0:T(8,128)S(1)} fusion(f32[512,2048]{1,0:T(8,128)} %bitcast.1.rt_ref), kind=kOutput, calls=%fused_computation.26 | convolution fusion | flops 6442450944 | bytes 5242880 | tf_op jit(solution)/shard_map/dot_general | solution.py:127
  116.3 1.9 collective-permute-done
  118.3 1.3 collective-permute-start.1
  119.6 7.1 %collective-permute-done.1 = f32[128,512]{1,0:T(8,128)S(1)} collective-permute-done((f32[128,512]{1,0:T(8,128)S(1)}, f32[128,512]{1,0:T(8,128)S(1)}, u32[]{:S(2)}, u32[]{:S(2)}) %collective-permute-start.1) | collective-permute-done | bytes 262176 | tf_op jit(solution)/shard_map/ppermute | solution.py:112
  126.8 1.3 collective-permute-start.2
  128.1 3.7 %collective-permute-done.2 = f32[64,512]{1,0:T(8,128)S(1)} collective-permute-done((f32[64,512]{1,0:T(8,128)S(1)}, f32[64,512]{1,0:T(8,128)S(1)}, u32[]{:S(2)}, u32[]{:S(2)}) %collective-permute-start.2) | collective-permute-done | bytes 131104 | tf_op jit(solution)/shard_map/ppermute | solution.py:112
  131.9 4.2 %collective-permute-done.3 = f32[32,512]{1,0:T(8,128)S(1)} collective-permute-done((f32[32,512]{1,0:T(8,128)S(1)}, f32[32,512]{1,0:T(8,128)S(1)}, u32[]{:S(2)}, u32[]{:S(2)}) %collective-permute-start.3) | collective-permute-done | bytes 65568 | tf_op jit(solution)/shard_map/ppermute | solution.py:112
  136.2 0.7 collective-permute-start.4
  136.9 4.7 %collective-permute-done.4 = f32[16,512]{1,0:T(8,128)S(1)} collective-permute-done((f32[16,512]{1,0:T(8,128)S(1)}, f32[16,512]{1,0:T(8,128)S(1)}, u32[]{:S(2)}, u32[]{:S(2)}) %collective-permute-start.4) | collective-permute-done | bytes 32800 | tf_op jit(solution)/shard_map/ppermute | solution.py:112
  141.6 0.5 collective-permute-start.5
  142.1 4.3 %collective-permute-done.5 = f32[16,512]{1,0:T(8,128)S(1)} collective-permute-done((f32[16,512]{1,0:T(8,128)S(1)}, f32[16,512]{1,0:T(8,128)S(1)}, u32[]{:S(2)}, u32[]{:S(2)}) %collective-permute-start.5) | collective-permute-done | bytes 32800 | tf_op jit(solution)/shard_map/ppermute | solution.py:115
  146.5 4.2 %collective-permute-done.6 = f32[32,512]{1,0:T(8,128)S(1)} collective-permute-done((f32[32,512]{1,0:T(8,128)S(1)}, f32[32,512]{1,0:T(8,128)S(1)}, u32[]{:S(2)}, u32[]{:S(2)}) %collective-permute-start.6) | collective-permute-done | bytes 65568 | tf_op jit(solution)/shard_map/ppermute | solution.py:115
  150.8 1.3 collective-permute-start.7
  152.1 3.7 %collective-permute-done.7 = f32[64,512]{1,0:T(8,128)S(1)} collective-permute-done((f32[64,512]{1,0:T(8,128)S(1)}, f32[64,512]{1,0:T(8,128)S(1)}, u32[]{:S(2)}, u32[]{:S(2)}) %collective-permute-start.7) | collective-permute-done | bytes 131104 | tf_op jit(solution)/shard_map/ppermute | solution.py:115
  155.9 1.3 collective-permute-start.8
  157.2 5.1 %collective-permute-done.8 = f32[128,512]{1,0:T(8,128)S(1)} collective-permute-done((f32[128,512]{1,0:T(8,128)S(1)}, f32[128,512]{1,0:T(8,128)S(1)}, u32[]{:S(2)}, u32[]{:S(2)}) %collective-permute-start.8) | collective-permute-done | bytes 262176 | tf_op jit(solution)/shard_map/ppermute | solution.py:115
  162.5 1.9 collective-permute-done.9
  164.4 0.1 broadcast_select_fusion.1
  164.5 1.0 pad_maximum_fusion.g_ref
  165.5 46.3 %shard_map.30 = (f32[512,512]{1,0:T(8,128)}, f32[512,512]{1,0:T(8,128)}, f32[512,512]{1,0:T(8,128)}) custom-call(f32[512,512]{1,0:T(8,128)} %pad_maximum_fusion.g_ref), custom_call_target="tpu_custom_call" | custom-call | flops 268435456 | bytes 3145728 | tf_op jit(solution)/shard_map/pallas_call | solution.py:68
  211.8 10.7 %shard_map.31 = f32[2048,512]{1,0:T(8,128)} custom-call(f32[512,2048]{1,0:T(8,128)} %bitcast.1.rt_ref, f32[512,512]{1,0:T(8,128)} %get-tuple-element.4.w_ref), custom_call_target="tpu_custom_call" | custom-call | flops 1073741824 | bytes 9437184 | tf_op jit(solution)/shard_map/pallas_call | solution.py:86
  (22 shorter events, 0.7 us)
Async XLA Ops:
  5.3 101.3 %all-to-all-start = ((f32[16,32,2048]{2,0,1:T(8,128)}), f32[16,32,2048]{2,0,1:T(8,128)}, u32[]{:S(2)}, u32[]{:S(2)}) async-start(f32[16,32,2048]{2,0,1:T(8,128)} %bitcast.9), calls=%async_computation | async-start | bytes 8388608 | tf_op jit(solution)/shard_map/all_to_all | solution.py:126
  116.2 2.0 collective-permute-start
  118.3 8.4 %collective-permute-start.1 = (f32[128,512]{1,0:T(8,128)S(1)}, f32[128,512]{1,0:T(8,128)S(1)}, u32[]{:S(2)}, u32[]{:S(2)}) collective-permute-start(f32[128,512]{1,0:T(8,128)S(1)} %constant_dynamic-slice_fusion.3), channel_id=1, source_target_pairs={{0,2},{1,3},{2,0},{3,1},{4,6},{5,7},{6,4},{7,5},{8,10},{9,11},{10,... | collective-permute-start | bytes 786440 | tf_op jit(solution)/shard_map/ppermute | solution.py:112
  126.8 5.0 %collective-permute-start.2 = (f32[64,512]{1,0:T(8,128)S(1)}, f32[64,512]{1,0:T(8,128)S(1)}, u32[]{:S(2)}, u32[]{:S(2)}) collective-permute-start(f32[64,512]{1,0:T(8,128)S(1)} %constant_dynamic-slice_fusion.2), channel_id=1, source_target_pairs={{0,4},{1,5},{2,6},{3,7},{4,0},{5,1},{6,2},{7,3},{8,12},{9,13},{10,... | collective-permute-start | bytes 393224 | tf_op jit(solution)/shard_map/ppermute | solution.py:112
  131.8 4.3 %collective-permute-start.3 = (f32[32,512]{1,0:T(8,128)S(1)}, f32[32,512]{1,0:T(8,128)S(1)}, u32[]{:S(2)}, u32[]{:S(2)}) collective-permute-start(f32[32,512]{1,0:T(8,128)S(1)} %constant_dynamic-slice_fusion.1), channel_id=1, source_target_pairs={{0,8},{1,9},{2,10},{3,11},{4,12},{5,13},{6,14},{7,15},{8,0},{9,1},... | collective-permute-start | bytes 196616 | tf_op jit(solution)/shard_map/ppermute | solution.py:112
  136.2 5.4 %collective-permute-start.4 = (f32[16,512]{1,0:T(8,128)S(1)}, f32[16,512]{1,0:T(8,128)S(1)}, u32[]{:S(2)}, u32[]{:S(2)}) collective-permute-start(f32[16,512]{1,0:T(8,128)S(1)} %constant_dynamic-slice_fusion), channel_id=1, source_target_pairs={{0,16},{1,17},{2,18},{3,19},{4,20},{5,21},{6,22},{7,23},{8,24},{9,... | collective-permute-start | bytes 98312 | tf_op jit(solution)/shard_map/ppermute | solution.py:112
  141.6 4.8 %collective-permute-start.5 = (f32[16,512]{1,0:T(8,128)S(1)}, f32[16,512]{1,0:T(8,128)S(1)}, u32[]{:S(2)}, u32[]{:S(2)}) collective-permute-start(f32[16,512]{1,0:T(8,128)S(1)} %dynamic-slice_add_fusion.4), channel_id=1, source_target_pairs={{0,16},{1,17},{2,18},{3,19},{4,20},{5,21},{6,22},{7,23},{8,24},{9,... | collective-permute-start | bytes 98312 | tf_op jit(solution)/shard_map/ppermute | solution.py:115
  146.4 4.3 %collective-permute-start.6 = (f32[32,512]{1,0:T(8,128)S(1)}, f32[32,512]{1,0:T(8,128)S(1)}, u32[]{:S(2)}, u32[]{:S(2)}) collective-permute-start(f32[32,512]{1,0:T(8,128)S(1)} %pad_maximum_fusion.4), channel_id=1, source_target_pairs={{0,8},{1,9},{2,10},{3,11},{4,12},{5,13},{6,14},{7,15},{8,0},{9,1},... | collective-permute-start | bytes 196616 | tf_op jit(solution)/shard_map/ppermute | solution.py:115
  150.8 5.0 %collective-permute-start.7 = (f32[64,512]{1,0:T(8,128)S(1)}, f32[64,512]{1,0:T(8,128)S(1)}, u32[]{:S(2)}, u32[]{:S(2)}) collective-permute-start(f32[64,512]{1,0:T(8,128)S(1)} %pad_maximum_fusion.3), channel_id=1, source_target_pairs={{0,4},{1,5},{2,6},{3,7},{4,0},{5,1},{6,2},{7,3},{8,12},{9,13},{10,... | collective-permute-start | bytes 393224 | tf_op jit(solution)/shard_map/ppermute | solution.py:115
  155.9 6.4 %collective-permute-start.8 = (f32[128,512]{1,0:T(8,128)S(1)}, f32[128,512]{1,0:T(8,128)S(1)}, u32[]{:S(2)}, u32[]{:S(2)}) collective-permute-start(f32[128,512]{1,0:T(8,128)S(1)} %pad_maximum_fusion.2), channel_id=1, source_target_pairs={{0,2},{1,3},{2,0},{3,1},{4,6},{5,7},{6,4},{7,5},{8,10},{9,11},{10,... | collective-permute-start | bytes 786440 | tf_op jit(solution)/shard_map/ppermute | solution.py:115
  162.4 2.0 collective-permute-start.9

commit v7 on v4

--- a/solution.py
+++ b/solution.py
@@ -41,7 +41,7 @@
     return w
 
 
-def _factor_kernel(g_ref, l_ref, w_ref, t_ref, r_ref, *, b):
+def _fused_kernel(g_ref, rt_ref, u_ref, o_ref, t_ref, r_ref, l_ref, w_ref, *, b, scale):
     n = g_ref.shape[0]
     nb = n // b
     t_ref[...] = g_ref[...]
@@ -60,18 +60,22 @@
             panel = _nt(t_ref[hi:, lo:hi], w_kk)
             l_ref[hi:, lo:hi] = panel
             t_ref[hi:, hi:] = t_ref[hi:, hi:] - _nt(panel, panel)
+        o_ref[:, lo:hi] = _nn(w_ref[lo:hi, :hi], rt_ref[:hi, :]).T * scale
+    u_ref[...] = l_ref[...].T / scale
 
 
-def factor_pair(matrix, b=128):
-    n = matrix.shape[0]
+def factor_and_basis(gram, rows_t, scale, b=128):
+    n = gram.shape[0]
+    m = rows_t.shape[1]
     return pl.pallas_call(
-        functools.partial(_factor_kernel, b=b),
+        functools.partial(_fused_kernel, b=b, scale=scale),
         out_shape=(jax.ShapeDtypeStruct((n, n), jnp.float32),
-                   jax.ShapeDtypeStruct((n, n), jnp.float32)),
-        scratch_shapes=[pltpu.VMEM((n, n), jnp.float32), pltpu.VMEM((b, b), jnp.float32)],
-        cost_estimate=pl.CostEstimate(flops=2 * n * n * n, transcendentals=n,
-                                      bytes_accessed=12 * n * n),
-    )(matrix)
+                   jax.ShapeDtypeStruct((m, n), jnp.float32)),
+        scratch_shapes=[pltpu.VMEM((n, n), jnp.float32), pltpu.VMEM((b, b), jnp.float32),
+                        pltpu.VMEM((n, n), jnp.float32), pltpu.VMEM((n, n), jnp.float32)],
+        cost_estimate=pl.CostEstimate(flops=2 * n * n * n + 2 * m * n * n, transcendentals=n,
+                                      bytes_accessed=4 * (3 * n * n + 2 * m * n)),
+    )(gram, rows_t)
 
 
 def _pair(count, bit):
@@ -107,19 +111,10 @@
         rows_t, rows_t.T, precision=lax.Precision.HIGHEST, preferred_element_type=jnp.float32
     )
     gram_total = sum_by_halving(gram_local, count)
-    lower, lower_inv = factor_pair(gram_total)
-    upper_factor = lower.T
-    inverse = lower_inv.T
     total_rows = rows_t.shape[1] * count
     scale_root = math.sqrt(total_rows)
-    product = lax.dot_general(
-        rows_t,
-        inverse,
-        (((0,), (0,)), ((), ())),
-        precision=lax.Precision.HIGHEST,
-        preferred_element_type=jnp.float32,
-    )
-    return (product * scale_root, upper_factor / scale_root)
+    factor_out, product = factor_and_basis(gram_total, rows_t, scale_root)
+    return (product, factor_out)
 
 
 def solution(mesh):

time: 229 us -> 218 us (0.952)
  matrix products: 20.1 us -> 9.49 us
  local copies, waits for them, and re-layouts: 11.6 us -> 4.81 us
  Pallas kernels: 45.9 us -> 52.3 us
    dot_general x1 -> x0, matrix products: 10.5 us -> none  [per_device(): lax.dot_general(rows_t, inverse, (((0,), (0,)), ((), ())), precision=lax....]
    unnamed x4 -> x0, local copies, waits for them, and re-layouts: 6.74 us -> none
    pallas_call x1, Pallas kernels: 45.9 us -> 52.3 us  [factor_and_basis(): pl.pallas_call(functools.partial(_fused_kernel, b=b, scale=scale), out_sh...]
where the time goes in v7:
time: 218 us
  waiting for transfers between devices  135 us (62%)
  Pallas kernels  52.3 us (24%)
  starting transfers between devices  14.1 us (6%)
  matrix products  9.49 us (4%)
  local copies, waits for them, and re-layouts  4.81 us (2%)
    all_to_all x1, waiting for transfers between devices, per_device(): lax.all_to_all(sample_t, AXES, split_axis=1, concat_axis=0, tiled=True)  93.9 us
    pallas_call x1, Pallas kernels, factor_and_basis(): pl.pallas_call(functools.partial(_fused_kernel, b=b, scale=scale), out_sh...  52.3 us
    ppermute x5, waiting for transfers between devices, sum_by_halving(): buf = keep + lax.ppermute(send, AXES, _pair(count, 1 << k))  21.7 us
    ppermute x5, waiting for transfers between devices, sum_by_halving(): recv = lax.ppermute(buf, AXES, _pair(count, 1 << k))  19.3 us
    dot_general x1, matrix products, per_device(): jnp.dot(rows_t, rows_t.T, precision=lax.Precision.HIGHEST, preferred_elem...  9.49 us
    all_to_all x1, starting transfers between devices, per_device(): lax.all_to_all(sample_t, AXES, split_axis=1, concat_axis=0, tiled=True)  7.43 us
    all_to_all x1, local copies, waits for them, and re-layouts, per_device(): lax.all_to_all(sample_t, AXES, split_axis=1, concat_axis=0, tiled=True)  4.7 us
  transfers between devices with their start and end apart: 11, of which 11 were waited for; matrix products, arithmetic and copies ran while one was open for 0% of the time, Pallas kernels for 0%

profile of v7, /device:TPU:0, one launch (start us, length us, event | category | flops | bytes accessed | tf_op | source)
XLA Modules:
  0.0 217.9 jit_solution(12058253802286233289)
XLA Ops:
  0.6 4.7 %copy.6 = f32[2,32,8,2048]{3,2,0,1:T(8,128)} copy(f32[2,32,8,2048]{3,2,1,0:T(8,128)} %bitcast.10) | data formatting | bytes 8388608 | tf_op jit(solution)/shard_map/all_to_all | solution.py:109
  5.3 7.4 %all-to-all-start = ((f32[16,32,2048]{2,0,1:T(8,128)}), f32[16,32,2048]{2,0,1:T(8,128)}, u32[]{:S(2)}, u32[]{:S(2)}) async-start(f32[16,32,2048]{2,0,1:T(8,128)} %bitcast.9), calls=%async_computation | async-start | bytes 8388608 | tf_op jit(solution)/shard_map/all_to_all | solution.py:109
  12.8 93.9 %all-to-all-done = f32[16,32,2048]{2,0,1:T(8,128)} async-done(((f32[16,32,2048]{2,0,1:T(8,128)}), f32[16,32,2048]{2,0,1:T(8,128)}, u32[]{:S(2)}, u32[]{:S(2)}) %all-to-all-start) | async-done | bytes 4194336 | tf_op jit(solution)/shard_map/all_to_all | solution.py:109
  106.6 9.5 %fusion = f32[512,512]{1,0:T(8,128)S(1)} fusion(f32[512,2048]{1,0:T(8,128)} %bitcast.1.rt_ref), kind=kOutput, calls=%fused_computation.26 | convolution fusion | flops 6442450944 | bytes 5242880 | tf_op jit(solution)/shard_map/dot_general | solution.py:110
  116.3 1.9 collective-permute-done
  118.2 0.1 dynamic-slice_add_fusion
  118.3 1.3 collective-permute-start.1
  119.6 7.1 %collective-permute-done.1 = f32[128,512]{1,0:T(8,128)S(1)} collective-permute-done((f32[128,512]{1,0:T(8,128)S(1)}, f32[128,512]{1,0:T(8,128)S(1)}, u32[]{:S(2)}, u32[]{:S(2)}) %collective-permute-start.1) | collective-permute-done | bytes 262176 | tf_op jit(solution)/shard_map/ppermute | solution.py:95
  126.8 1.3 collective-permute-start.2
  128.1 3.7 %collective-permute-done.2 = f32[64,512]{1,0:T(8,128)S(1)} collective-permute-done((f32[64,512]{1,0:T(8,128)S(1)}, f32[64,512]{1,0:T(8,128)S(1)}, u32[]{:S(2)}, u32[]{:S(2)}) %collective-permute-start.2) | collective-permute-done | bytes 131104 | tf_op jit(solution)/shard_map/ppermute | solution.py:95
  131.9 4.2 %collective-permute-done.3 = f32[32,512]{1,0:T(8,128)S(1)} collective-permute-done((f32[32,512]{1,0:T(8,128)S(1)}, f32[32,512]{1,0:T(8,128)S(1)}, u32[]{:S(2)}, u32[]{:S(2)}) %collective-permute-start.3) | collective-permute-done | bytes 65568 | tf_op jit(solution)/shard_map/ppermute | solution.py:95
  136.2 0.7 collective-permute-start.4
  136.9 4.7 %collective-permute-done.4 = f32[16,512]{1,0:T(8,128)S(1)} collective-permute-done((f32[16,512]{1,0:T(8,128)S(1)}, f32[16,512]{1,0:T(8,128)S(1)}, u32[]{:S(2)}, u32[]{:S(2)}) %collective-permute-start.4) | collective-permute-done | bytes 32800 | tf_op jit(solution)/shard_map/ppermute | solution.py:95
  141.6 0.5 collective-permute-start.5
  142.1 4.3 %collective-permute-done.5 = f32[16,512]{1,0:T(8,128)S(1)} collective-permute-done((f32[16,512]{1,0:T(8,128)S(1)}, f32[16,512]{1,0:T(8,128)S(1)}, u32[]{:S(2)}, u32[]{:S(2)}) %collective-permute-start.5) | collective-permute-done | bytes 32800 | tf_op jit(solution)/shard_map/ppermute | solution.py:98
  146.5 4.2 %collective-permute-done.6 = f32[32,512]{1,0:T(8,128)S(1)} collective-permute-done((f32[32,512]{1,0:T(8,128)S(1)}, f32[32,512]{1,0:T(8,128)S(1)}, u32[]{:S(2)}, u32[]{:S(2)}) %collective-permute-start.6) | collective-permute-done | bytes 65568 | tf_op jit(solution)/shard_map/ppermute | solution.py:98
  150.8 1.3 collective-permute-start.7
  152.1 3.7 %collective-permute-done.7 = f32[64,512]{1,0:T(8,128)S(1)} collective-permute-done((f32[64,512]{1,0:T(8,128)S(1)}, f32[64,512]{1,0:T(8,128)S(1)}, u32[]{:S(2)}, u32[]{:S(2)}) %collective-permute-start.7) | collective-permute-done | bytes 131104 | tf_op jit(solution)/shard_map/ppermute | solution.py:98
  155.9 1.3 collective-permute-start.8
  157.2 5.1 %collective-permute-done.8 = f32[128,512]{1,0:T(8,128)S(1)} collective-permute-done((f32[128,512]{1,0:T(8,128)S(1)}, f32[128,512]{1,0:T(8,128)S(1)}, u32[]{:S(2)}, u32[]{:S(2)}) %collective-permute-start.8) | collective-permute-done | bytes 262176 | tf_op jit(solution)/shard_map/ppermute | solution.py:98
  162.5 1.9 collective-permute-done.9
  164.4 0.1 broadcast_select_fusion.1
  164.5 1.1 pad_maximum_fusion.g_ref
  165.5 52.3 %shard_map.30 = (f32[512,512]{1,0:T(8,128)}, f32[2048,512]{1,0:T(8,128)}) custom-call(f32[512,512]{1,0:T(8,128)} %pad_maximum_fusion.g_ref, f32[512,2048]{1,0:T(8,128)} %bitcast.1.rt_ref), custom_call_target="tpu_custom_call" | custom-call | flops 1342177280 | bytes 11534336 | tf_op jit(solution)/shard_map/pallas_call | solution.py:70
  (21 shorter events, 0.6 us)
Async XLA Ops:
  5.3 101.3 %all-to-all-start = ((f32[16,32,2048]{2,0,1:T(8,128)}), f32[16,32,2048]{2,0,1:T(8,128)}, u32[]{:S(2)}, u32[]{:S(2)}) async-start(f32[16,32,2048]{2,0,1:T(8,128)} %bitcast.9), calls=%async_computation | async-start | bytes 8388608 | tf_op jit(solution)/shard_map/all_to_all | solution.py:109
  116.2 2.0 collective-permute-start
  118.3 8.4 %collective-permute-start.1 = (f32[128,512]{1,0:T(8,128)S(1)}, f32[128,512]{1,0:T(8,128)S(1)}, u32[]{:S(2)}, u32[]{:S(2)}) collective-permute-start(f32[128,512]{1,0:T(8,128)S(1)} %constant_dynamic-slice_fusion.3), channel_id=1, source_target_pairs={{0,2},{1,3},{2,0},{3,1},{4,6},{5,7},{6,4},{7,5},{8,10},{9,11},{10,... | collective-permute-start | bytes 786440 | tf_op jit(solution)/shard_map/ppermute | solution.py:95
  126.8 5.0 %collective-permute-start.2 = (f32[64,512]{1,0:T(8,128)S(1)}, f32[64,512]{1,0:T(8,128)S(1)}, u32[]{:S(2)}, u32[]{:S(2)}) collective-permute-start(f32[64,512]{1,0:T(8,128)S(1)} %constant_dynamic-slice_fusion.2), channel_id=1, source_target_pairs={{0,4},{1,5},{2,6},{3,7},{4,0},{5,1},{6,2},{7,3},{8,12},{9,13},{10,... | collective-permute-start | bytes 393224 | tf_op jit(solution)/shard_map/ppermute | solution.py:95
  131.8 4.3 %collective-permute-start.3 = (f32[32,512]{1,0:T(8,128)S(1)}, f32[32,512]{1,0:T(8,128)S(1)}, u32[]{:S(2)}, u32[]{:S(2)}) collective-permute-start(f32[32,512]{1,0:T(8,128)S(1)} %constant_dynamic-slice_fusion.1), channel_id=1, source_target_pairs={{0,8},{1,9},{2,10},{3,11},{4,12},{5,13},{6,14},{7,15},{8,0},{9,1},... | collective-permute-start | bytes 196616 | tf_op jit(solution)/shard_map/ppermute | solution.py:95
  136.2 5.4 %collective-permute-start.4 = (f32[16,512]{1,0:T(8,128)S(1)}, f32[16,512]{1,0:T(8,128)S(1)}, u32[]{:S(2)}, u32[]{:S(2)}) collective-permute-start(f32[16,512]{1,0:T(8,128)S(1)} %constant_dynamic-slice_fusion), channel_id=1, source_target_pairs={{0,16},{1,17},{2,18},{3,19},{4,20},{5,21},{6,22},{7,23},{8,24},{9,... | collective-permute-start | bytes 98312 | tf_op jit(solution)/shard_map/ppermute | solution.py:95
  141.6 4.8 %collective-permute-start.5 = (f32[16,512]{1,0:T(8,128)S(1)}, f32[16,512]{1,0:T(8,128)S(1)}, u32[]{:S(2)}, u32[]{:S(2)}) collective-permute-start(f32[16,512]{1,0:T(8,128)S(1)} %dynamic-slice_add_fusion.4), channel_id=1, source_target_pairs={{0,16},{1,17},{2,18},{3,19},{4,20},{5,21},{6,22},{7,23},{8,24},{9,... | collective-permute-start | bytes 98312 | tf_op jit(solution)/shard_map/ppermute | solution.py:98
  146.4 4.3 %collective-permute-start.6 = (f32[32,512]{1,0:T(8,128)S(1)}, f32[32,512]{1,0:T(8,128)S(1)}, u32[]{:S(2)}, u32[]{:S(2)}) collective-permute-start(f32[32,512]{1,0:T(8,128)S(1)} %pad_maximum_fusion.4), channel_id=1, source_target_pairs={{0,8},{1,9},{2,10},{3,11},{4,12},{5,13},{6,14},{7,15},{8,0},{9,1},... | collective-permute-start | bytes 196616 | tf_op jit(solution)/shard_map/ppermute | solution.py:98
  150.8 5.0 %collective-permute-start.7 = (f32[64,512]{1,0:T(8,128)S(1)}, f32[64,512]{1,0:T(8,128)S(1)}, u32[]{:S(2)}, u32[]{:S(2)}) collective-permute-start(f32[64,512]{1,0:T(8,128)S(1)} %pad_maximum_fusion.3), channel_id=1, source_target_pairs={{0,4},{1,5},{2,6},{3,7},{4,0},{5,1},{6,2},{7,3},{8,12},{9,13},{10,... | collective-permute-start | bytes 393224 | tf_op jit(solution)/shard_map/ppermute | solution.py:98
  155.9 6.4 %collective-permute-start.8 = (f32[128,512]{1,0:T(8,128)S(1)}, f32[128,512]{1,0:T(8,128)S(1)}, u32[]{:S(2)}, u32[]{:S(2)}) collective-permute-start(f32[128,512]{1,0:T(8,128)S(1)} %pad_maximum_fusion.2), channel_id=1, source_target_pairs={{0,2},{1,3},{2,0},{3,1},{4,6},{5,7},{6,4},{7,5},{8,10},{9,11},{10,... | collective-permute-start | bytes 786440 | tf_op jit(solution)/shard_map/ppermute | solution.py:98
  162.4 2.0 collective-permute-start.9

commit v8 on v7

--- a/solution.py
+++ b/solution.py
@@ -23,13 +23,16 @@
     return jnp.dot(a, b, precision=HI, preferred_element_type=jnp.float32)
 
 
-def _chain(a, r_ref):
+def _chain(a, r_ref, side=()):
     b = a.shape[0]
     rows = lax.broadcasted_iota(jnp.int32, (b, 1), 0)
     lanes = lax.broadcasted_iota(jnp.int32, (1, b), 1)
     w = (lax.broadcasted_iota(jnp.int32, (b, b), 0)
          == lax.broadcasted_iota(jnp.int32, (b, b), 1)).astype(jnp.float32)
+    every = b // max(len(side), 1)
     for j in range(b):
+        if side and j % every == 0 and j // every < len(side):
+            side[j // every]()
         s = lax.rsqrt(a[j:j + 1, j:j + 1])
         row = jnp.where(lanes >= j, a[j:j + 1, :] * s, 0.0)
         col = jnp.where(rows >= j, a[:, j:j + 1] * s, 0.0)
@@ -47,10 +50,20 @@
     t_ref[...] = g_ref[...]
     l_ref[...] = jnp.zeros_like(l_ref)
     w_ref[...] = jnp.zeros_like(w_ref)
+    m = rt_ref.shape[1]
+    piece = m // 8
+
+    def basis_piece(lo, hi, p):
+        def run():
+            cols = slice(p * piece, (p + 1) * piece)
+            o_ref[cols, lo:hi] = _nn(w_ref[lo:hi, :hi], rt_ref[:hi, cols]).T * scale
+        return run
+
+    side = ()
     for k in range(nb):
         lo, hi = k * b, (k + 1) * b
         blk = t_ref[lo:hi, lo:hi]
-        w_kk = _chain((blk + blk.T) * 0.5, r_ref)
+        w_kk = _chain((blk + blk.T) * 0.5, r_ref, side)
         l_ref[lo:hi, lo:hi] = r_ref[...].T
         w_ref[lo:hi, lo:hi] = w_kk
         if k > 0:
@@ -60,7 +73,9 @@
             panel = _nt(t_ref[hi:, lo:hi], w_kk)
             l_ref[hi:, lo:hi] = panel
             t_ref[hi:, hi:] = t_ref[hi:, hi:] - _nt(panel, panel)
-        o_ref[:, lo:hi] = _nn(w_ref[lo:hi, :hi], rt_ref[:hi, :]).T * scale
+        side = tuple(basis_piece(lo, hi, p) for p in range(8))
+    for run in side:
+        run()
     u_ref[...] = l_ref[...].T / scale
 
 

time: 218 us -> 217 us (level)
  no operation moved by 1% of the time
where the time goes in v8:
time: 217 us
  waiting for transfers between devices  135 us (62%)
  Pallas kernels  51.6 us (24%)
  starting transfers between devices  14.1 us (6%)
  matrix products  9.49 us (4%)
  local copies, waits for them, and re-layouts  4.81 us (2%)
    all_to_all x1, waiting for transfers between devices, per_device(): lax.all_to_all(sample_t, AXES, split_axis=1, concat_axis=0, tiled=True)  93.9 us
    pallas_call x1, Pallas kernels, factor_and_basis(): pl.pallas_call(functools.partial(_fused_kernel, b=b, scale=scale), out_sh...  51.6 us
    ppermute x5, waiting for transfers between devices, sum_by_halving(): buf = keep + lax.ppermute(send, AXES, _pair(count, 1 << k))  21.7 us
    ppermute x5, waiting for transfers between devices, sum_by_halving(): recv = lax.ppermute(buf, AXES, _pair(count, 1 << k))  19.3 us
    dot_general x1, matrix products, per_device(): jnp.dot(rows_t, rows_t.T, precision=lax.Precision.HIGHEST, preferred_elem...  9.49 us
    all_to_all x1, starting transfers between devices, per_device(): lax.all_to_all(sample_t, AXES, split_axis=1, concat_axis=0, tiled=True)  7.43 us
    all_to_all x1, local copies, waits for them, and re-layouts, per_device(): lax.all_to_all(sample_t, AXES, split_axis=1, concat_axis=0, tiled=True)  4.7 us
  transfers between devices with their start and end apart: 11, of which 11 were waited for; matrix products, arithmetic and copies ran while one was open for 0% of the time, Pallas kernels for 0%

profile of v8, /device:TPU:0, one launch (start us, length us, event | category | flops | bytes accessed | tf_op | source)
XLA Modules:
  0.0 217.2 jit_solution(11001181069921978274)
XLA Ops:
  0.6 4.7 %copy.6 = f32[2,32,8,2048]{3,2,0,1:T(8,128)} copy(f32[2,32,8,2048]{3,2,1,0:T(8,128)} %bitcast.10) | data formatting | bytes 8388608 | tf_op jit(solution)/shard_map/all_to_all | solution.py:124
  5.3 7.4 %all-to-all-start = ((f32[16,32,2048]{2,0,1:T(8,128)}), f32[16,32,2048]{2,0,1:T(8,128)}, u32[]{:S(2)}, u32[]{:S(2)}) async-start(f32[16,32,2048]{2,0,1:T(8,128)} %bitcast.9), calls=%async_computation | async-start | bytes 8388608 | tf_op jit(solution)/shard_map/all_to_all | solution.py:124
  12.8 93.9 %all-to-all-done = f32[16,32,2048]{2,0,1:T(8,128)} async-done(((f32[16,32,2048]{2,0,1:T(8,128)}), f32[16,32,2048]{2,0,1:T(8,128)}, u32[]{:S(2)}, u32[]{:S(2)}) %all-to-all-start) | async-done | bytes 4194336 | tf_op jit(solution)/shard_map/all_to_all | solution.py:124
  106.6 9.5 %fusion = f32[512,512]{1,0:T(8,128)S(1)} fusion(f32[512,2048]{1,0:T(8,128)} %bitcast.1.rt_ref), kind=kOutput, calls=%fused_computation.26 | convolution fusion | flops 6442450944 | bytes 5242880 | tf_op jit(solution)/shard_map/dot_general | solution.py:125
  116.3 1.9 collective-permute-done
  118.2 0.1 dynamic-slice_add_fusion
  118.3 1.3 collective-permute-start.1
  119.6 7.1 %collective-permute-done.1 = f32[128,512]{1,0:T(8,128)S(1)} collective-permute-done((f32[128,512]{1,0:T(8,128)S(1)}, f32[128,512]{1,0:T(8,128)S(1)}, u32[]{:S(2)}, u32[]{:S(2)}) %collective-permute-start.1) | collective-permute-done | bytes 262176 | tf_op jit(solution)/shard_map/ppermute | solution.py:110
  126.8 1.3 collective-permute-start.2
  128.1 3.7 %collective-permute-done.2 = f32[64,512]{1,0:T(8,128)S(1)} collective-permute-done((f32[64,512]{1,0:T(8,128)S(1)}, f32[64,512]{1,0:T(8,128)S(1)}, u32[]{:S(2)}, u32[]{:S(2)}) %collective-permute-start.2) | collective-permute-done | bytes 131104 | tf_op jit(solution)/shard_map/ppermute | solution.py:110
  131.9 4.2 %collective-permute-done.3 = f32[32,512]{1,0:T(8,128)S(1)} collective-permute-done((f32[32,512]{1,0:T(8,128)S(1)}, f32[32,512]{1,0:T(8,128)S(1)}, u32[]{:S(2)}, u32[]{:S(2)}) %collective-permute-start.3) | collective-permute-done | bytes 65568 | tf_op jit(solution)/shard_map/ppermute | solution.py:110
  136.2 0.7 collective-permute-start.4
  136.9 4.7 %collective-permute-done.4 = f32[16,512]{1,0:T(8,128)S(1)} collective-permute-done((f32[16,512]{1,0:T(8,128)S(1)}, f32[16,512]{1,0:T(8,128)S(1)}, u32[]{:S(2)}, u32[]{:S(2)}) %collective-permute-start.4) | collective-permute-done | bytes 32800 | tf_op jit(solution)/shard_map/ppermute | solution.py:110
  141.6 0.5 collective-permute-start.5
  142.1 4.3 %collective-permute-done.5 = f32[16,512]{1,0:T(8,128)S(1)} collective-permute-done((f32[16,512]{1,0:T(8,128)S(1)}, f32[16,512]{1,0:T(8,128)S(1)}, u32[]{:S(2)}, u32[]{:S(2)}) %collective-permute-start.5) | collective-permute-done | bytes 32800 | tf_op jit(solution)/shard_map/ppermute | solution.py:113
  146.5 4.2 %collective-permute-done.6 = f32[32,512]{1,0:T(8,128)S(1)} collective-permute-done((f32[32,512]{1,0:T(8,128)S(1)}, f32[32,512]{1,0:T(8,128)S(1)}, u32[]{:S(2)}, u32[]{:S(2)}) %collective-permute-start.6) | collective-permute-done | bytes 65568 | tf_op jit(solution)/shard_map/ppermute | solution.py:113
  150.8 1.3 collective-permute-start.7
  152.1 3.7 %collective-permute-done.7 = f32[64,512]{1,0:T(8,128)S(1)} collective-permute-done((f32[64,512]{1,0:T(8,128)S(1)}, f32[64,512]{1,0:T(8,128)S(1)}, u32[]{:S(2)}, u32[]{:S(2)}) %collective-permute-start.7) | collective-permute-done | bytes 131104 | tf_op jit(solution)/shard_map/ppermute | solution.py:113
  155.9 1.3 collective-permute-start.8
  157.2 5.1 %collective-permute-done.8 = f32[128,512]{1,0:T(8,128)S(1)} collective-permute-done((f32[128,512]{1,0:T(8,128)S(1)}, f32[128,512]{1,0:T(8,128)S(1)}, u32[]{:S(2)}, u32[]{:S(2)}) %collective-permute-start.8) | collective-permute-done | bytes 262176 | tf_op jit(solution)/shard_map/ppermute | solution.py:113
  162.5 1.9 collective-permute-done.9
  164.4 0.1 broadcast_select_fusion.1
  164.5 1.1 pad_maximum_fusion.g_ref
  165.5 51.6 %shard_map.30 = (f32[512,512]{1,0:T(8,128)}, f32[2048,512]{1,0:T(8,128)}) custom-call(f32[512,512]{1,0:T(8,128)} %pad_maximum_fusion.g_ref, f32[512,2048]{1,0:T(8,128)} %bitcast.1.rt_ref), custom_call_target="tpu_custom_call" | custom-call | flops 1342177280 | bytes 11534336 | tf_op jit(solution)/shard_map/pallas_call | solution.py:85
  (21 shorter events, 0.6 us)
Async XLA Ops:
  5.3 101.3 %all-to-all-start = ((f32[16,32,2048]{2,0,1:T(8,128)}), f32[16,32,2048]{2,0,1:T(8,128)}, u32[]{:S(2)}, u32[]{:S(2)}) async-start(f32[16,32,2048]{2,0,1:T(8,128)} %bitcast.9), calls=%async_computation | async-start | bytes 8388608 | tf_op jit(solution)/shard_map/all_to_all | solution.py:124
  116.2 2.0 collective-permute-start
  118.3 8.4 %collective-permute-start.1 = (f32[128,512]{1,0:T(8,128)S(1)}, f32[128,512]{1,0:T(8,128)S(1)}, u32[]{:S(2)}, u32[]{:S(2)}) collective-permute-start(f32[128,512]{1,0:T(8,128)S(1)} %constant_dynamic-slice_fusion.3), channel_id=1, source_target_pairs={{0,2},{1,3},{2,0},{3,1},{4,6},{5,7},{6,4},{7,5},{8,10},{9,11},{10,... | collective-permute-start | bytes 786440 | tf_op jit(solution)/shard_map/ppermute | solution.py:110
  126.8 5.0 %collective-permute-start.2 = (f32[64,512]{1,0:T(8,128)S(1)}, f32[64,512]{1,0:T(8,128)S(1)}, u32[]{:S(2)}, u32[]{:S(2)}) collective-permute-start(f32[64,512]{1,0:T(8,128)S(1)} %constant_dynamic-slice_fusion.2), channel_id=1, source_target_pairs={{0,4},{1,5},{2,6},{3,7},{4,0},{5,1},{6,2},{7,3},{8,12},{9,13},{10,... | collective-permute-start | bytes 393224 | tf_op jit(solution)/shard_map/ppermute | solution.py:110
  131.8 4.3 %collective-permute-start.3 = (f32[32,512]{1,0:T(8,128)S(1)}, f32[32,512]{1,0:T(8,128)S(1)}, u32[]{:S(2)}, u32[]{:S(2)}) collective-permute-start(f32[32,512]{1,0:T(8,128)S(1)} %constant_dynamic-slice_fusion.1), channel_id=1, source_target_pairs={{0,8},{1,9},{2,10},{3,11},{4,12},{5,13},{6,14},{7,15},{8,0},{9,1},... | collective-permute-start | bytes 196616 | tf_op jit(solution)/shard_map/ppermute | solution.py:110
  136.2 5.4 %collective-permute-start.4 = (f32[16,512]{1,0:T(8,128)S(1)}, f32[16,512]{1,0:T(8,128)S(1)}, u32[]{:S(2)}, u32[]{:S(2)}) collective-permute-start(f32[16,512]{1,0:T(8,128)S(1)} %constant_dynamic-slice_fusion), channel_id=1, source_target_pairs={{0,16},{1,17},{2,18},{3,19},{4,20},{5,21},{6,22},{7,23},{8,24},{9,... | collective-permute-start | bytes 98312 | tf_op jit(solution)/shard_map/ppermute | solution.py:110
  141.6 4.8 %collective-permute-start.5 = (f32[16,512]{1,0:T(8,128)S(1)}, f32[16,512]{1,0:T(8,128)S(1)}, u32[]{:S(2)}, u32[]{:S(2)}) collective-permute-start(f32[16,512]{1,0:T(8,128)S(1)} %dynamic-slice_add_fusion.4), channel_id=1, source_target_pairs={{0,16},{1,17},{2,18},{3,19},{4,20},{5,21},{6,22},{7,23},{8,24},{9,... | collective-permute-start | bytes 98312 | tf_op jit(solution)/shard_map/ppermute | solution.py:113
  146.4 4.3 %collective-permute-start.6 = (f32[32,512]{1,0:T(8,128)S(1)}, f32[32,512]{1,0:T(8,128)S(1)}, u32[]{:S(2)}, u32[]{:S(2)}) collective-permute-start(f32[32,512]{1,0:T(8,128)S(1)} %pad_maximum_fusion.4), channel_id=1, source_target_pairs={{0,8},{1,9},{2,10},{3,11},{4,12},{5,13},{6,14},{7,15},{8,0},{9,1},... | collective-permute-start | bytes 196616 | tf_op jit(solution)/shard_map/ppermute | solution.py:113
  150.8 5.0 %collective-permute-start.7 = (f32[64,512]{1,0:T(8,128)S(1)}, f32[64,512]{1,0:T(8,128)S(1)}, u32[]{:S(2)}, u32[]{:S(2)}) collective-permute-start(f32[64,512]{1,0:T(8,128)S(1)} %pad_maximum_fusion.3), channel_id=1, source_target_pairs={{0,4},{1,5},{2,6},{3,7},{4,0},{5,1},{6,2},{7,3},{8,12},{9,13},{10,... | collective-permute-start | bytes 393224 | tf_op jit(solution)/shard_map/ppermute | solution.py:113
  155.9 6.4 %collective-permute-start.8 = (f32[128,512]{1,0:T(8,128)S(1)}, f32[128,512]{1,0:T(8,128)S(1)}, u32[]{:S(2)}, u32[]{:S(2)}) collective-permute-start(f32[128,512]{1,0:T(8,128)S(1)} %pad_maximum_fusion.2), channel_id=1, source_target_pairs={{0,2},{1,3},{2,0},{3,1},{4,6},{5,7},{6,4},{7,5},{8,10},{9,11},{10,... | collective-permute-start | bytes 786440 | tf_op jit(solution)/shard_map/ppermute | solution.py:113
  162.4 2.0 collective-permute-start.9

commit v9 on v8

--- a/solution.py
+++ b/solution.py
@@ -93,24 +93,27 @@
     )(gram, rows_t)
 
 
-def _pair(count, bit):
-    return [(i, i ^ bit) for i in range(count)]
-
-
 def sum_by_halving(local, count):
     steps = count.bit_length() - 1
     assert 1 << steps == count and local.shape[0] % count == 0
+    order = [list(range(steps)), list(range(steps))]
+    if steps >= 3:
+        order[1][1], order[1][2] = 2, 1
     idx = lax.axis_index(AXES)
+    core = idx & 1
     buf = local
-    for k in range(steps):
+    rounds = []
+    for r in range(steps):
+        perm = [(i, i ^ (1 << order[i & 1][r])) for i in range(count)]
+        bit = jnp.where(core == 0, order[0][r], order[1][r])
+        rounds.append((perm, (idx >> bit) & 1))
+    for perm, b in rounds:
         half = buf.shape[0] // 2
-        b = (idx >> k) & 1
         keep = lax.dynamic_slice_in_dim(buf, b * half, half, 0)
         send = lax.dynamic_slice_in_dim(buf, (1 - b) * half, half, 0)
-        buf = keep + lax.ppermute(send, AXES, _pair(count, 1 << k))
-    for k in reversed(range(steps)):
-        b = (idx >> k) & 1
-        recv = lax.ppermute(buf, AXES, _pair(count, 1 << k))
+        buf = keep + lax.ppermute(send, AXES, perm)
+    for perm, b in reversed(rounds):
+        recv = lax.ppermute(buf, AXES, perm)
         lo = jnp.where(b == 0, buf, recv)
         hi = jnp.where(b == 0, recv, buf)
         buf = jnp.concatenate([lo, hi], 0)

time: 217 us -> 215 us (level)
  no operation moved by 1% of the time
where the time goes in v9:
time: 215 us
  waiting for transfers between devices  133 us (62%)
  Pallas kernels  51.6 us (24%)
  starting transfers between devices  14.1 us (7%)
  matrix products  9.49 us (4%)
  local copies, waits for them, and re-layouts  4.81 us (2%)
    all_to_all x1, waiting for transfers between devices, per_device(): lax.all_to_all(sample_t, AXES, split_axis=1, concat_axis=0, tiled=True)  93.9 us
    pallas_call x1, Pallas kernels, factor_and_basis(): pl.pallas_call(functools.partial(_fused_kernel, b=b, scale=scale), out_sh...  51.6 us
    ppermute x5, waiting for transfers between devices, sum_by_halving(): buf = keep + lax.ppermute(send, AXES, perm)  19.6 us
    ppermute x5, waiting for transfers between devices, sum_by_halving(): recv = lax.ppermute(buf, AXES, perm)  19.3 us
    dot_general x1, matrix products, per_device(): jnp.dot(rows_t, rows_t.T, precision=lax.Precision.HIGHEST, preferred_elem...  9.49 us
    all_to_all x1, starting transfers between devices, per_device(): lax.all_to_all(sample_t, AXES, split_axis=1, concat_axis=0, tiled=True)  7.43 us
    all_to_all x1, local copies, waits for them, and re-layouts, per_device(): lax.all_to_all(sample_t, AXES, split_axis=1, concat_axis=0, tiled=True)  4.7 us
  transfers between devices with their start and end apart: 11, of which 11 were waited for; matrix products, arithmetic and copies ran while one was open for 0% of the time, Pallas kernels for 0%

profile of v9, /device:TPU:0, one launch (start us, length us, event | category | flops | bytes accessed | tf_op | source)
XLA Modules:
  0.0 215.2 jit_solution(12350634381418584903)
XLA Ops:
  0.6 4.7 %copy.6 = f32[2,32,8,2048]{3,2,0,1:T(8,128)} copy(f32[2,32,8,2048]{3,2,1,0:T(8,128)} %bitcast.10) | data formatting | bytes 8388608 | tf_op jit(solution)/shard_map/all_to_all | solution.py:127
  5.3 7.4 %all-to-all-start = ((f32[16,32,2048]{2,0,1:T(8,128)}), f32[16,32,2048]{2,0,1:T(8,128)}, u32[]{:S(2)}, u32[]{:S(2)}) async-start(f32[16,32,2048]{2,0,1:T(8,128)} %bitcast.9), calls=%async_computation | async-start | bytes 8388608 | tf_op jit(solution)/shard_map/all_to_all | solution.py:127
  12.8 93.9 %all-to-all-done = f32[16,32,2048]{2,0,1:T(8,128)} async-done(((f32[16,32,2048]{2,0,1:T(8,128)}), f32[16,32,2048]{2,0,1:T(8,128)}, u32[]{:S(2)}, u32[]{:S(2)}) %all-to-all-start) | async-done | bytes 4194336 | tf_op jit(solution)/shard_map/all_to_all | solution.py:127
  106.6 9.5 %fusion = f32[512,512]{1,0:T(8,128)S(1)} fusion(f32[512,2048]{1,0:T(8,128)} %bitcast.1.rt_ref), kind=kOutput, calls=%fused_computation.26 | convolution fusion | flops 6442450944 | bytes 5242880 | tf_op jit(solution)/shard_map/dot_general | solution.py:128
  116.3 1.9 collective-permute-done
  118.2 0.1 dynamic-slice_add_fusion
  118.3 1.3 collective-permute-start.1
  119.6 5.1 %collective-permute-done.1 = f32[128,512]{1,0:T(8,128)S(1)} collective-permute-done((f32[128,512]{1,0:T(8,128)S(1)}, f32[128,512]{1,0:T(8,128)S(1)}, u32[]{:S(2)}, u32[]{:S(2)}) %collective-permute-start.1) | collective-permute-done | bytes 262176 | tf_op jit(solution)/shard_map/ppermute | solution.py:114
  124.8 1.3 collective-permute-start.2
  126.1 3.7 %collective-permute-done.2 = f32[64,512]{1,0:T(8,128)S(1)} collective-permute-done((f32[64,512]{1,0:T(8,128)S(1)}, f32[64,512]{1,0:T(8,128)S(1)}, u32[]{:S(2)}, u32[]{:S(2)}) %collective-permute-start.2) | collective-permute-done | bytes 131104 | tf_op jit(solution)/shard_map/ppermute | solution.py:114
  129.9 4.2 %collective-permute-done.3 = f32[32,512]{1,0:T(8,128)S(1)} collective-permute-done((f32[32,512]{1,0:T(8,128)S(1)}, f32[32,512]{1,0:T(8,128)S(1)}, u32[]{:S(2)}, u32[]{:S(2)}) %collective-permute-start.3) | collective-permute-done | bytes 65568 | tf_op jit(solution)/shard_map/ppermute | solution.py:114
  134.2 0.7 collective-permute-start.4
  134.9 4.7 %collective-permute-done.4 = f32[16,512]{1,0:T(8,128)S(1)} collective-permute-done((f32[16,512]{1,0:T(8,128)S(1)}, f32[16,512]{1,0:T(8,128)S(1)}, u32[]{:S(2)}, u32[]{:S(2)}) %collective-permute-start.4) | collective-permute-done | bytes 32800 | tf_op jit(solution)/shard_map/ppermute | solution.py:114
  139.6 0.5 collective-permute-start.5
  140.1 4.3 %collective-permute-done.5 = f32[16,512]{1,0:T(8,128)S(1)} collective-permute-done((f32[16,512]{1,0:T(8,128)S(1)}, f32[16,512]{1,0:T(8,128)S(1)}, u32[]{:S(2)}, u32[]{:S(2)}) %collective-permute-start.5) | collective-permute-done | bytes 32800 | tf_op jit(solution)/shard_map/ppermute | solution.py:116
  144.5 4.2 %collective-permute-done.6 = f32[32,512]{1,0:T(8,128)S(1)} collective-permute-done((f32[32,512]{1,0:T(8,128)S(1)}, f32[32,512]{1,0:T(8,128)S(1)}, u32[]{:S(2)}, u32[]{:S(2)}) %collective-permute-start.6) | collective-permute-done | bytes 65568 | tf_op jit(solution)/shard_map/ppermute | solution.py:116
  148.8 1.3 collective-permute-start.7
  150.1 3.7 %collective-permute-done.7 = f32[64,512]{1,0:T(8,128)S(1)} collective-permute-done((f32[64,512]{1,0:T(8,128)S(1)}, f32[64,512]{1,0:T(8,128)S(1)}, u32[]{:S(2)}, u32[]{:S(2)}) %collective-permute-start.7) | collective-permute-done | bytes 131104 | tf_op jit(solution)/shard_map/ppermute | solution.py:116
  153.9 1.3 collective-permute-start.8
  155.2 5.1 %collective-permute-done.8 = f32[128,512]{1,0:T(8,128)S(1)} collective-permute-done((f32[128,512]{1,0:T(8,128)S(1)}, f32[128,512]{1,0:T(8,128)S(1)}, u32[]{:S(2)}, u32[]{:S(2)}) %collective-permute-start.8) | collective-permute-done | bytes 262176 | tf_op jit(solution)/shard_map/ppermute | solution.py:116
  160.5 1.9 collective-permute-done.9
  162.4 0.1 broadcast_select_fusion.1
  162.5 1.1 pad_maximum_fusion.g_ref
  163.5 51.6 %shard_map.30 = (f32[512,512]{1,0:T(8,128)}, f32[2048,512]{1,0:T(8,128)}) custom-call(f32[512,512]{1,0:T(8,128)} %pad_maximum_fusion.g_ref, f32[512,2048]{1,0:T(8,128)} %bitcast.1.rt_ref), custom_call_target="tpu_custom_call" | custom-call | flops 1342177280 | bytes 11534336 | tf_op jit(solution)/shard_map/pallas_call | solution.py:85
  (21 shorter events, 0.6 us)
Async XLA Ops:
  5.3 101.3 %all-to-all-start = ((f32[16,32,2048]{2,0,1:T(8,128)}), f32[16,32,2048]{2,0,1:T(8,128)}, u32[]{:S(2)}, u32[]{:S(2)}) async-start(f32[16,32,2048]{2,0,1:T(8,128)} %bitcast.9), calls=%async_computation | async-start | bytes 8388608 | tf_op jit(solution)/shard_map/all_to_all | solution.py:127
  116.2 2.0 collective-permute-start
  118.3 6.4 %collective-permute-start.1 = (f32[128,512]{1,0:T(8,128)S(1)}, f32[128,512]{1,0:T(8,128)S(1)}, u32[]{:S(2)}, u32[]{:S(2)}) collective-permute-start(f32[128,512]{1,0:T(8,128)S(1)} %constant_dynamic-slice_fusion.3), channel_id=1, source_target_pairs={{0,2},{1,5},{2,0},{3,7},{4,6},{5,1},{6,4},{7,3},{8,10},{9,13},{10,... | collective-permute-start | bytes 786440 | tf_op jit(solution)/shard_map/ppermute | solution.py:114
  124.8 5.0 %collective-permute-start.2 = (f32[64,512]{1,0:T(8,128)S(1)}, f32[64,512]{1,0:T(8,128)S(1)}, u32[]{:S(2)}, u32[]{:S(2)}) collective-permute-start(f32[64,512]{1,0:T(8,128)S(1)} %constant_dynamic-slice_fusion.2), channel_id=1, source_target_pairs={{0,4},{1,3},{2,6},{3,1},{4,0},{5,7},{6,2},{7,5},{8,12},{9,11},{10,... | collective-permute-start | bytes 393224 | tf_op jit(solution)/shard_map/ppermute | solution.py:114
  129.9 4.3 %collective-permute-start.3 = (f32[32,512]{1,0:T(8,128)S(1)}, f32[32,512]{1,0:T(8,128)S(1)}, u32[]{:S(2)}, u32[]{:S(2)}) collective-permute-start(f32[32,512]{1,0:T(8,128)S(1)} %constant_dynamic-slice_fusion.1), channel_id=1, source_target_pairs={{0,8},{1,9},{2,10},{3,11},{4,12},{5,13},{6,14},{7,15},{8,0},{9,1},... | collective-permute-start | bytes 196616 | tf_op jit(solution)/shard_map/ppermute | solution.py:114
  134.2 5.3 %collective-permute-start.4 = (f32[16,512]{1,0:T(8,128)S(1)}, f32[16,512]{1,0:T(8,128)S(1)}, u32[]{:S(2)}, u32[]{:S(2)}) collective-permute-start(f32[16,512]{1,0:T(8,128)S(1)} %constant_dynamic-slice_fusion), channel_id=1, source_target_pairs={{0,16},{1,17},{2,18},{3,19},{4,20},{5,21},{6,22},{7,23},{8,24},{9,... | collective-permute-start | bytes 98312 | tf_op jit(solution)/shard_map/ppermute | solution.py:114
  139.6 4.8 %collective-permute-start.5 = (f32[16,512]{1,0:T(8,128)S(1)}, f32[16,512]{1,0:T(8,128)S(1)}, u32[]{:S(2)}, u32[]{:S(2)}) collective-permute-start(f32[16,512]{1,0:T(8,128)S(1)} %dynamic-slice_add_fusion.4), channel_id=1, source_target_pairs={{0,16},{1,17},{2,18},{3,19},{4,20},{5,21},{6,22},{7,23},{8,24},{9,... | collective-permute-start | bytes 98312 | tf_op jit(solution)/shard_map/ppermute | solution.py:116
  144.4 4.3 %collective-permute-start.6 = (f32[32,512]{1,0:T(8,128)S(1)}, f32[32,512]{1,0:T(8,128)S(1)}, u32[]{:S(2)}, u32[]{:S(2)}) collective-permute-start(f32[32,512]{1,0:T(8,128)S(1)} %pad_maximum_fusion.4), channel_id=1, source_target_pairs={{0,8},{1,9},{2,10},{3,11},{4,12},{5,13},{6,14},{7,15},{8,0},{9,1},... | collective-permute-start | bytes 196616 | tf_op jit(solution)/shard_map/ppermute | solution.py:116
  148.8 5.0 %collective-permute-start.7 = (f32[64,512]{1,0:T(8,128)S(1)}, f32[64,512]{1,0:T(8,128)S(1)}, u32[]{:S(2)}, u32[]{:S(2)}) collective-permute-start(f32[64,512]{1,0:T(8,128)S(1)} %pad_maximum_fusion.3), channel_id=1, source_target_pairs={{0,4},{1,3},{2,6},{3,1},{4,0},{5,7},{6,2},{7,5},{8,12},{9,11},{10,... | collective-permute-start | bytes 393224 | tf_op jit(solution)/shard_map/ppermute | solution.py:116
  153.9 6.4 %collective-permute-start.8 = (f32[128,512]{1,0:T(8,128)S(1)}, f32[128,512]{1,0:T(8,128)S(1)}, u32[]{:S(2)}, u32[]{:S(2)}) collective-permute-start(f32[128,512]{1,0:T(8,128)S(1)} %pad_maximum_fusion.2), channel_id=1, source_target_pairs={{0,2},{1,5},{2,0},{3,7},{4,6},{5,1},{6,4},{7,3},{8,10},{9,13},{10,... | collective-permute-start | bytes 786440 | tf_op jit(solution)/shard_map/ppermute | solution.py:116
  160.4 2.0 collective-permute-start.9

commit v10 on v9

--- a/solution.py
+++ b/solution.py
@@ -93,9 +93,9 @@
     )(gram, rows_t)
 
 
-def sum_by_halving(local, count):
+def sum_by_halving(local, count, first=None):
     steps = count.bit_length() - 1
-    assert 1 << steps == count and local.shape[0] % count == 0
+    assert 1 << steps == count
     order = [list(range(steps)), list(range(steps))]
     if steps >= 3:
         order[1][1], order[1][2] = 2, 1
@@ -107,7 +107,12 @@
         perm = [(i, i ^ (1 << order[i & 1][r])) for i in range(count)]
         bit = jnp.where(core == 0, order[0][r], order[1][r])
         rounds.append((perm, (idx >> bit) & 1))
-    for perm, b in rounds:
+    for r, (perm, b) in enumerate(rounds):
+        if r == 0 and first is not None:
+            send = first(1 - b)
+            recv = lax.ppermute(send, AXES, perm)
+            buf = first(b) + recv
+            continue
         half = buf.shape[0] // 2
         keep = lax.dynamic_slice_in_dim(buf, b * half, half, 0)
         send = lax.dynamic_slice_in_dim(buf, (1 - b) * half, half, 0)
@@ -125,10 +130,14 @@
     narrow_count = lax.axis_size("narrow")
     count = wide_count * narrow_count
     rows_t = lax.all_to_all(sample_t, AXES, split_axis=1, concat_axis=0, tiled=True)
-    gram_local = jnp.dot(
-        rows_t, rows_t.T, precision=lax.Precision.HIGHEST, preferred_element_type=jnp.float32
-    )
-    gram_total = sum_by_halving(gram_local, count)
+    half = rows_t.shape[0] // 2
+
+    def gram_half(h):
+        part = lax.dynamic_slice_in_dim(rows_t, h * half, half, 0)
+        return jnp.dot(part, rows_t.T, precision=lax.Precision.HIGHEST,
+                       preferred_element_type=jnp.float32)
+
+    gram_total = sum_by_halving(None, count, first=gram_half)
     total_rows = rows_t.shape[1] * count
     scale_root = math.sqrt(total_rows)
     factor_out, product = factor_and_basis(gram_total, rows_t, scale_root)

time: 215 us -> 219 us (1.019)
  matrix products: 9.49 us -> 13.1 us
    dot_general x1 -> x2, matrix products: 9.49 us -> 13.1 us  [gram_half(): jnp.dot(part, rows_t.T, precision=lax.Precision.HIGHEST, preferred_elemen...]
    ppermute x5 -> x4, waiting for transfers between devices: 19.6 us -> 17.2 us  [sum_by_halving(): buf = keep + lax.ppermute(send, AXES, perm)]
where the time goes in v10:
time: 219 us
  waiting for transfers between devices  133 us (61%)
  Pallas kernels  51.6 us (24%)
  starting transfers between devices  14.1 us (6%)
  matrix products  13.1 us (6%)
  local copies, waits for them, and re-layouts  4.77 us (2%)
    all_to_all x1, waiting for transfers between devices, per_device(): lax.all_to_all(sample_t, AXES, split_axis=1, concat_axis=0, tiled=True)  93.9 us
    pallas_call x1, Pallas kernels, factor_and_basis(): pl.pallas_call(functools.partial(_fused_kernel, b=b, scale=scale), out_sh...  51.6 us
    ppermute x5, waiting for transfers between devices, sum_by_halving(): recv = lax.ppermute(buf, AXES, perm)  19.9 us
    ppermute x4, waiting for transfers between devices, sum_by_halving(): buf = keep + lax.ppermute(send, AXES, perm)  17.2 us
    dot_general x2, matrix products, gram_half(): jnp.dot(part, rows_t.T, precision=lax.Precision.HIGHEST, preferred_elemen...  13.1 us
    all_to_all x1, starting transfers between devices, per_device(): lax.all_to_all(sample_t, AXES, split_axis=1, concat_axis=0, tiled=True)  7.43 us
    all_to_all x1, local copies, waits for them, and re-layouts, per_device(): lax.all_to_all(sample_t, AXES, split_axis=1, concat_axis=0, tiled=True)  4.7 us
  transfers between devices with their start and end apart: 11, of which 11 were waited for; matrix products, arithmetic and copies ran while one was open for 0% of the time, Pallas kernels for 0%

profile of v10, /device:TPU:0, one launch (start us, length us, event | category | flops | bytes accessed | tf_op | source)
XLA Modules:
  0.0 218.6 jit_solution(6567451169792916828)
XLA Ops:
  0.6 4.7 %copy.6 = f32[2,32,8,2048]{3,2,0,1:T(8,128)} copy(f32[2,32,8,2048]{3,2,1,0:T(8,128)} %bitcast.10) | data formatting | bytes 8388608 | tf_op jit(solution)/shard_map/all_to_all | solution.py:132
  5.3 7.4 %all-to-all-start = ((f32[16,32,2048]{2,0,1:T(8,128)}), f32[16,32,2048]{2,0,1:T(8,128)}, u32[]{:S(2)}, u32[]{:S(2)}) async-start(f32[16,32,2048]{2,0,1:T(8,128)} %bitcast.9), calls=%async_computation | async-start | bytes 8388608 | tf_op jit(solution)/shard_map/all_to_all | solution.py:132
  12.8 93.9 %all-to-all-done = f32[16,32,2048]{2,0,1:T(8,128)} async-done(((f32[16,32,2048]{2,0,1:T(8,128)}), f32[16,32,2048]{2,0,1:T(8,128)}, u32[]{:S(2)}, u32[]{:S(2)}) %all-to-all-start) | async-done | bytes 4194336 | tf_op jit(solution)/shard_map/all_to_all | solution.py:132
  106.6 6.2 %fusion = f32[256,512]{1,0:T(8,128)S(1)} fusion(f32[512,2048]{1,0:T(8,128)} %bitcast.1.rt_ref, s32[]{:T(128)S(6)} %select_n.108), kind=kOutput, calls=%fused_computation.1 | convolution fusion | flops 3221225472 | bytes 6815748 | tf_op jit(solution)/shard_map/dot_general | solution.py:137
  112.9 0.2 collective-permute-start
  113.0 1.8 collective-permute-done
  114.9 6.8 %fusion.4 = f32[256,512]{1,0:T(8,128)S(1)} fusion(f32[256,512]{1,0:T(8,128)S(1)} %collective-permute-done, f32[512,2048]{1,0:T(8,128)} %bitcast.1.rt_ref, s32[]{:T(128)S(6)} %select_n.107), kind=kOutput, calls=%fused_computation.5 | convolution fusion | flops 3221356544 | bytes 7340036 | tf_op jit(solution)/shard_map/dot_general | solution.py:137
  121.7 1.3 collective-permute-start.1
  123.1 5.1 %collective-permute-done.1 = f32[128,512]{1,0:T(8,128)S(1)} collective-permute-done((f32[128,512]{1,0:T(8,128)S(1)}, f32[128,512]{1,0:T(8,128)S(1)}, u32[]{:S(2)}, u32[]{:S(2)}) %collective-permute-start.1) | collective-permute-done | bytes 262176 | tf_op jit(solution)/shard_map/ppermute | solution.py:119
  128.2 1.3 collective-permute-start.2
  129.5 3.7 %collective-permute-done.2 = f32[64,512]{1,0:T(8,128)S(1)} collective-permute-done((f32[64,512]{1,0:T(8,128)S(1)}, f32[64,512]{1,0:T(8,128)S(1)}, u32[]{:S(2)}, u32[]{:S(2)}) %collective-permute-start.2) | collective-permute-done | bytes 131104 | tf_op jit(solution)/shard_map/ppermute | solution.py:119
  133.4 4.2 %collective-permute-done.3 = f32[32,512]{1,0:T(8,128)S(1)} collective-permute-done((f32[32,512]{1,0:T(8,128)S(1)}, f32[32,512]{1,0:T(8,128)S(1)}, u32[]{:S(2)}, u32[]{:S(2)}) %collective-permute-start.3) | collective-permute-done | bytes 65568 | tf_op jit(solution)/shard_map/ppermute | solution.py:119
  137.7 1.2 collective-permute-start.4
  138.9 4.1 %collective-permute-done.4 = f32[16,512]{1,0:T(8,128)S(1)} collective-permute-done((f32[16,512]{1,0:T(8,128)S(1)}, f32[16,512]{1,0:T(8,128)S(1)}, u32[]{:S(2)}, u32[]{:S(2)}) %collective-permute-start.4) | collective-permute-done | bytes 32800 | tf_op jit(solution)/shard_map/ppermute | solution.py:119
  143.0 0.8 collective-permute-start.5
  143.8 4.0 %collective-permute-done.5 = f32[16,512]{1,0:T(8,128)S(1)} collective-permute-done((f32[16,512]{1,0:T(8,128)S(1)}, f32[16,512]{1,0:T(8,128)S(1)}, u32[]{:S(2)}, u32[]{:S(2)}) %collective-permute-start.5) | collective-permute-done | bytes 32800 | tf_op jit(solution)/shard_map/ppermute | solution.py:121
  147.9 4.2 %collective-permute-done.6 = f32[32,512]{1,0:T(8,128)S(1)} collective-permute-done((f32[32,512]{1,0:T(8,128)S(1)}, f32[32,512]{1,0:T(8,128)S(1)}, u32[]{:S(2)}, u32[]{:S(2)}) %collective-permute-start.6) | collective-permute-done | bytes 65568 | tf_op jit(solution)/shard_map/ppermute | solution.py:121
  152.2 0.9 collective-permute-start.7
  153.1 4.2 %collective-permute-done.7 = f32[64,512]{1,0:T(8,128)S(1)} collective-permute-done((f32[64,512]{1,0:T(8,128)S(1)}, f32[64,512]{1,0:T(8,128)S(1)}, u32[]{:S(2)}, u32[]{:S(2)}) %collective-permute-start.7) | collective-permute-done | bytes 131104 | tf_op jit(solution)/shard_map/ppermute | solution.py:121
  157.3 0.9 collective-permute-start.8
  158.2 5.5 %collective-permute-done.8 = f32[128,512]{1,0:T(8,128)S(1)} collective-permute-done((f32[128,512]{1,0:T(8,128)S(1)}, f32[128,512]{1,0:T(8,128)S(1)}, u32[]{:S(2)}, u32[]{:S(2)}) %collective-permute-start.8) | collective-permute-done | bytes 262176 | tf_op jit(solution)/shard_map/ppermute | solution.py:121
  163.9 1.9 collective-permute-done.9
  165.9 1.1 pad_maximum_fusion.g_ref
  167.0 51.6 %shard_map.30 = (f32[512,512]{1,0:T(8,128)}, f32[2048,512]{1,0:T(8,128)}) custom-call(f32[512,512]{1,0:T(8,128)} %pad_maximum_fusion.g_ref, f32[512,2048]{1,0:T(8,128)} %bitcast.1.rt_ref), custom_call_target="tpu_custom_call" | custom-call | flops 1342177280 | bytes 11534336 | tf_op jit(solution)/shard_map/pallas_call | solution.py:85
  (20 shorter events, 0.6 us)
Async XLA Ops:
  5.3 101.3 %all-to-all-start = ((f32[16,32,2048]{2,0,1:T(8,128)}), f32[16,32,2048]{2,0,1:T(8,128)}, u32[]{:S(2)}, u32[]{:S(2)}) async-start(f32[16,32,2048]{2,0,1:T(8,128)} %bitcast.9), calls=%async_computation | async-start | bytes 8388608 | tf_op jit(solution)/shard_map/all_to_all | solution.py:132
  112.9 2.0 collective-permute-start
  121.7 6.4 %collective-permute-start.1 = (f32[128,512]{1,0:T(8,128)S(1)}, f32[128,512]{1,0:T(8,128)S(1)}, u32[]{:S(2)}, u32[]{:S(2)}) collective-permute-start(f32[128,512]{1,0:T(8,128)S(1)} %constant_dynamic-slice_fusion.3), channel_id=1, source_target_pairs={{0,2},{1,5},{2,0},{3,7},{4,6},{5,1},{6,4},{7,3},{8,10},{9,13},{10,... | collective-permute-start | bytes 786440 | tf_op jit(solution)/shard_map/ppermute | solution.py:119
  128.2 5.0 %collective-permute-start.2 = (f32[64,512]{1,0:T(8,128)S(1)}, f32[64,512]{1,0:T(8,128)S(1)}, u32[]{:S(2)}, u32[]{:S(2)}) collective-permute-start(f32[64,512]{1,0:T(8,128)S(1)} %constant_dynamic-slice_fusion.2), channel_id=1, source_target_pairs={{0,4},{1,3},{2,6},{3,1},{4,0},{5,7},{6,2},{7,5},{8,12},{9,11},{10,... | collective-permute-start | bytes 393224 | tf_op jit(solution)/shard_map/ppermute | solution.py:119
  133.3 4.3 %collective-permute-start.3 = (f32[32,512]{1,0:T(8,128)S(1)}, f32[32,512]{1,0:T(8,128)S(1)}, u32[]{:S(2)}, u32[]{:S(2)}) collective-permute-start(f32[32,512]{1,0:T(8,128)S(1)} %constant_dynamic-slice_fusion.1), channel_id=1, source_target_pairs={{0,8},{1,9},{2,10},{3,11},{4,12},{5,13},{6,14},{7,15},{8,0},{9,1},... | collective-permute-start | bytes 196616 | tf_op jit(solution)/shard_map/ppermute | solution.py:119
  137.7 5.3 %collective-permute-start.4 = (f32[16,512]{1,0:T(8,128)S(1)}, f32[16,512]{1,0:T(8,128)S(1)}, u32[]{:S(2)}, u32[]{:S(2)}) collective-permute-start(f32[16,512]{1,0:T(8,128)S(1)} %constant_dynamic-slice_fusion), channel_id=1, source_target_pairs={{0,16},{1,17},{2,18},{3,19},{4,20},{5,21},{6,22},{7,23},{8,24},{9,... | collective-permute-start | bytes 98312 | tf_op jit(solution)/shard_map/ppermute | solution.py:119
  143.0 4.8 %collective-permute-start.5 = (f32[16,512]{1,0:T(8,128)S(1)}, f32[16,512]{1,0:T(8,128)S(1)}, u32[]{:S(2)}, u32[]{:S(2)}) collective-permute-start(f32[16,512]{1,0:T(8,128)S(1)} %dynamic-slice_add_fusion.3), channel_id=1, source_target_pairs={{0,16},{1,17},{2,18},{3,19},{4,20},{5,21},{6,22},{7,23},{8,24},{9,... | collective-permute-start | bytes 98312 | tf_op jit(solution)/shard_map/ppermute | solution.py:121
  147.9 4.3 %collective-permute-start.6 = (f32[32,512]{1,0:T(8,128)S(1)}, f32[32,512]{1,0:T(8,128)S(1)}, u32[]{:S(2)}, u32[]{:S(2)}) collective-permute-start(f32[32,512]{1,0:T(8,128)S(1)} %pad_maximum_fusion.4), channel_id=1, source_target_pairs={{0,8},{1,9},{2,10},{3,11},{4,12},{5,13},{6,14},{7,15},{8,0},{9,1},... | collective-permute-start | bytes 196616 | tf_op jit(solution)/shard_map/ppermute | solution.py:121
  152.2 5.0 %collective-permute-start.7 = (f32[64,512]{1,0:T(8,128)S(1)}, f32[64,512]{1,0:T(8,128)S(1)}, u32[]{:S(2)}, u32[]{:S(2)}) collective-permute-start(f32[64,512]{1,0:T(8,128)S(1)} %pad_maximum_fusion.3), channel_id=1, source_target_pairs={{0,4},{1,3},{2,6},{3,1},{4,0},{5,7},{6,2},{7,5},{8,12},{9,11},{10,... | collective-permute-start | bytes 393224 | tf_op jit(solution)/shard_map/ppermute | solution.py:121
  157.3 6.4 %collective-permute-start.8 = (f32[128,512]{1,0:T(8,128)S(1)}, f32[128,512]{1,0:T(8,128)S(1)}, u32[]{:S(2)}, u32[]{:S(2)}) collective-permute-start(f32[128,512]{1,0:T(8,128)S(1)} %pad_maximum_fusion.2), channel_id=1, source_target_pairs={{0,2},{1,5},{2,0},{3,7},{4,6},{5,1},{6,4},{7,3},{8,10},{9,13},{10,... | collective-permute-start | bytes 786440 | tf_op jit(solution)/shard_map/ppermute | solution.py:121
  163.8 2.0 collective-permute-start.9

commit v11 on v9

--- a/solution.py
+++ b/solution.py
@@ -125,9 +125,18 @@
     narrow_count = lax.axis_size("narrow")
     count = wide_count * narrow_count
     rows_t = lax.all_to_all(sample_t, AXES, split_axis=1, concat_axis=0, tiled=True)
-    gram_local = jnp.dot(
-        rows_t, rows_t.T, precision=lax.Precision.HIGHEST, preferred_element_type=jnp.float32
-    )
+    half = rows_t.shape[0] // 2
+    top, bottom = rows_t[:half], rows_t[half:]
+
+    def gram_of(x, y):
+        return jnp.dot(x, y.T, precision=lax.Precision.HIGHEST,
+                       preferred_element_type=jnp.float32)
+
+    lower_left = gram_of(bottom, top)
+    gram_local = jnp.concatenate([
+        jnp.concatenate([gram_of(top, top), lower_left.T], 1),
+        jnp.concatenate([lower_left, gram_of(bottom, bottom)], 1),
+    ], 0)
     gram_total = sum_by_halving(gram_local, count)
     total_rows = rows_t.shape[1] * count
     scale_root = math.sqrt(total_rows)

time: 215 us -> 214 us (level)
  matrix products: 9.49 us -> 5.6 us
  local copies, waits for them, and re-layouts: 4.81 us -> 7.44 us
    dot_general x1 -> x3, matrix products: 9.49 us -> 5.6 us  [gram_of(): jnp.dot(x, y.T, precision=lax.Precision.HIGHEST, preferred_element_type=j...]
    slice x0 -> x1, local copies, waits for them, and re-layouts: none -> 2.49 us  [per_device(): top, bottom = (rows_t[:half], rows_t[half:])]
where the time goes in v11:
time: 214 us
  waiting for transfers between devices  133 us (62%)
  Pallas kernels  51.5 us (24%)
  starting transfers between devices  14.1 us (7%)
  local copies, waits for them, and re-layouts  7.44 us (3%)
  matrix products  5.6 us (3%)
    all_to_all x1, waiting for transfers between devices, per_device(): lax.all_to_all(sample_t, AXES, split_axis=1, concat_axis=0, tiled=True)  93.9 us
    pallas_call x1, Pallas kernels, factor_and_basis(): pl.pallas_call(functools.partial(_fused_kernel, b=b, scale=scale), out_sh...  51.5 us
    ppermute x5, waiting for transfers between devices, sum_by_halving(): buf = keep + lax.ppermute(send, AXES, perm)  19.6 us
    ppermute x5, waiting for transfers between devices, sum_by_halving(): recv = lax.ppermute(buf, AXES, perm)  19.3 us
    all_to_all x1, starting transfers between devices, per_device(): lax.all_to_all(sample_t, AXES, split_axis=1, concat_axis=0, tiled=True)  7.43 us
    dot_general x3, matrix products, gram_of(): jnp.dot(x, y.T, precision=lax.Precision.HIGHEST, preferred_element_type=j...  5.6 us
    all_to_all x1, local copies, waits for them, and re-layouts, per_device(): lax.all_to_all(sample_t, AXES, split_axis=1, concat_axis=0, tiled=True)  4.7 us
  transfers between devices with their start and end apart: 11, of which 11 were waited for; matrix products, arithmetic and copies ran while one was open for 0% of the time, Pallas kernels for 0%

profile of v11, /device:TPU:0, one launch (start us, length us, event | category | flops | bytes accessed | tf_op | source)
XLA Modules:
  0.0 214.0 jit_solution(3187507491676499165)
XLA Ops:
  0.6 4.7 %copy.11 = f32[2,32,8,2048]{3,2,0,1:T(8,128)} copy(f32[2,32,8,2048]{3,2,1,0:T(8,128)} %bitcast.21) | data formatting | bytes 8388608 | tf_op jit(solution)/shard_map/all_to_all | solution.py:127
  5.3 7.4 %all-to-all-start = ((f32[16,32,2048]{2,0,1:T(8,128)}), f32[16,32,2048]{2,0,1:T(8,128)}, u32[]{:S(2)}, u32[]{:S(2)}) async-start(f32[16,32,2048]{2,0,1:T(8,128)} %bitcast.20), calls=%async_computation | async-start | bytes 8388608 | tf_op jit(solution)/shard_map/all_to_all | solution.py:127
  12.8 93.9 %all-to-all-done = f32[16,32,2048]{2,0,1:T(8,128)} async-done(((f32[16,32,2048]{2,0,1:T(8,128)}), f32[16,32,2048]{2,0,1:T(8,128)}, u32[]{:S(2)}, u32[]{:S(2)}) %all-to-all-start) | async-done | bytes 4194336 | tf_op jit(solution)/shard_map/all_to_all | solution.py:127
  106.6 2.5 %fusion = (f32[16,16,2048]{2,1,0:T(8,128)S(1)}, f32[16,16,2048]{2,1,0:T(8,128)S(1)}) fusion(f32[32,16,2048]{2,1,0:T(8,128)} %bitcast), kind=kLoop, calls=%fused_computation.27 | loop fusion | bytes 8388608 | tf_op jit(solution)/shard_map/slice | solution.py:129
  109.1 1.9 fusion.1
  111.0 1.9 fusion.2
  112.9 1.9 fusion.3
  115.2 1.9 collective-permute-done
  117.2 1.3 collective-permute-start.1
  118.5 5.1 %collective-permute-done.1 = f32[128,512]{1,0:T(8,128)S(1)} collective-permute-done((f32[128,512]{1,0:T(8,128)S(1)}, f32[128,512]{1,0:T(8,128)S(1)}, u32[]{:S(2)}, u32[]{:S(2)}) %collective-permute-start.1) | collective-permute-done | bytes 262176 | tf_op jit(solution)/shard_map/ppermute | solution.py:114
  123.7 1.3 collective-permute-start.2
  125.0 3.7 %collective-permute-done.2 = f32[64,512]{1,0:T(8,128)S(1)} collective-permute-done((f32[64,512]{1,0:T(8,128)S(1)}, f32[64,512]{1,0:T(8,128)S(1)}, u32[]{:S(2)}, u32[]{:S(2)}) %collective-permute-start.2) | collective-permute-done | bytes 131104 | tf_op jit(solution)/shard_map/ppermute | solution.py:114
  128.9 4.2 %collective-permute-done.3 = f32[32,512]{1,0:T(8,128)S(1)} collective-permute-done((f32[32,512]{1,0:T(8,128)S(1)}, f32[32,512]{1,0:T(8,128)S(1)}, u32[]{:S(2)}, u32[]{:S(2)}) %collective-permute-start.3) | collective-permute-done | bytes 65568 | tf_op jit(solution)/shard_map/ppermute | solution.py:114
  133.1 0.7 collective-permute-start.4
  133.8 4.7 %collective-permute-done.4 = f32[16,512]{1,0:T(8,128)S(1)} collective-permute-done((f32[16,512]{1,0:T(8,128)S(1)}, f32[16,512]{1,0:T(8,128)S(1)}, u32[]{:S(2)}, u32[]{:S(2)}) %collective-permute-start.4) | collective-permute-done | bytes 32800 | tf_op jit(solution)/shard_map/ppermute | solution.py:114
  139.0 4.3 %collective-permute-done.5 = f32[16,512]{1,0:T(8,128)S(1)} collective-permute-done((f32[16,512]{1,0:T(8,128)S(1)}, f32[16,512]{1,0:T(8,128)S(1)}, u32[]{:S(2)}, u32[]{:S(2)}) %collective-permute-start.5) | collective-permute-done | bytes 32800 | tf_op jit(solution)/shard_map/ppermute | solution.py:116
  143.4 4.2 %collective-permute-done.6 = f32[32,512]{1,0:T(8,128)S(1)} collective-permute-done((f32[32,512]{1,0:T(8,128)S(1)}, f32[32,512]{1,0:T(8,128)S(1)}, u32[]{:S(2)}, u32[]{:S(2)}) %collective-permute-start.6) | collective-permute-done | bytes 65568 | tf_op jit(solution)/shard_map/ppermute | solution.py:116
  147.7 1.3 collective-permute-start.7
  149.0 3.7 %collective-permute-done.7 = f32[64,512]{1,0:T(8,128)S(1)} collective-permute-done((f32[64,512]{1,0:T(8,128)S(1)}, f32[64,512]{1,0:T(8,128)S(1)}, u32[]{:S(2)}, u32[]{:S(2)}) %collective-permute-start.7) | collective-permute-done | bytes 131104 | tf_op jit(solution)/shard_map/ppermute | solution.py:116
  152.8 1.3 collective-permute-start.8
  154.1 5.1 %collective-permute-done.8 = f32[128,512]{1,0:T(8,128)S(1)} collective-permute-done((f32[128,512]{1,0:T(8,128)S(1)}, f32[128,512]{1,0:T(8,128)S(1)}, u32[]{:S(2)}, u32[]{:S(2)}) %collective-permute-start.8) | collective-permute-done | bytes 262176 | tf_op jit(solution)/shard_map/ppermute | solution.py:116
  159.4 1.9 collective-permute-done.9
  161.4 1.0 pad_maximum_fusion.g_ref
  162.4 51.5 %shard_map.30 = (f32[512,512]{1,0:T(8,128)}, f32[2048,512]{1,0:T(8,128)}) custom-call(f32[512,512]{1,0:T(8,128)} %pad_maximum_fusion.g_ref, f32[512,2048]{1,0:T(8,128)} %bitcast.4.rt_ref), custom_call_target="tpu_custom_call" | custom-call | flops 1342177280 | bytes 11534336 | tf_op jit(solution)/shard_map/pallas_call | solution.py:85
  (26 shorter events, 1.6 us)
Async XLA Ops:
  5.3 101.3 %all-to-all-start = ((f32[16,32,2048]{2,0,1:T(8,128)}), f32[16,32,2048]{2,0,1:T(8,128)}, u32[]{:S(2)}, u32[]{:S(2)}) async-start(f32[16,32,2048]{2,0,1:T(8,128)} %bitcast.20), calls=%async_computation | async-start | bytes 8388608 | tf_op jit(solution)/shard_map/all_to_all | solution.py:127
  115.1 2.0 collective-permute-start
  117.2 6.4 %collective-permute-start.1 = (f32[128,512]{1,0:T(8,128)S(1)}, f32[128,512]{1,0:T(8,128)S(1)}, u32[]{:S(2)}, u32[]{:S(2)}) collective-permute-start(f32[128,512]{1,0:T(8,128)S(1)} %constant_dynamic-slice_fusion.3), channel_id=1, source_target_pairs={{0,2},{1,5},{2,0},{3,7},{4,6},{5,1},{6,4},{7,3},{8,10},{9,13},{10,... | collective-permute-start | bytes 786440 | tf_op jit(solution)/shard_map/ppermute | solution.py:114
  123.7 5.0 %collective-permute-start.2 = (f32[64,512]{1,0:T(8,128)S(1)}, f32[64,512]{1,0:T(8,128)S(1)}, u32[]{:S(2)}, u32[]{:S(2)}) collective-permute-start(f32[64,512]{1,0:T(8,128)S(1)} %constant_dynamic-slice_fusion.2), channel_id=1, source_target_pairs={{0,4},{1,3},{2,6},{3,1},{4,0},{5,7},{6,2},{7,5},{8,12},{9,11},{10,... | collective-permute-start | bytes 393224 | tf_op jit(solution)/shard_map/ppermute | solution.py:114
  128.8 4.3 %collective-permute-start.3 = (f32[32,512]{1,0:T(8,128)S(1)}, f32[32,512]{1,0:T(8,128)S(1)}, u32[]{:S(2)}, u32[]{:S(2)}) collective-permute-start(f32[32,512]{1,0:T(8,128)S(1)} %constant_dynamic-slice_fusion.1), channel_id=1, source_target_pairs={{0,8},{1,9},{2,10},{3,11},{4,12},{5,13},{6,14},{7,15},{8,0},{9,1},... | collective-permute-start | bytes 196616 | tf_op jit(solution)/shard_map/ppermute | solution.py:114
  133.1 5.3 %collective-permute-start.4 = (f32[16,512]{1,0:T(8,128)S(1)}, f32[16,512]{1,0:T(8,128)S(1)}, u32[]{:S(2)}, u32[]{:S(2)}) collective-permute-start(f32[16,512]{1,0:T(8,128)S(1)} %constant_dynamic-slice_fusion), channel_id=1, source_target_pairs={{0,16},{1,17},{2,18},{3,19},{4,20},{5,21},{6,22},{7,23},{8,24},{9,... | collective-permute-start | bytes 98312 | tf_op jit(solution)/shard_map/ppermute | solution.py:114
  138.5 4.8 %collective-permute-start.5 = (f32[16,512]{1,0:T(8,128)S(1)}, f32[16,512]{1,0:T(8,128)S(1)}, u32[]{:S(2)}, u32[]{:S(2)}) collective-permute-start(f32[16,512]{1,0:T(8,128)S(1)} %dynamic-slice_add_fusion.4), channel_id=1, source_target_pairs={{0,16},{1,17},{2,18},{3,19},{4,20},{5,21},{6,22},{7,23},{8,24},{9,... | collective-permute-start | bytes 98312 | tf_op jit(solution)/shard_map/ppermute | solution.py:116
  143.3 4.3 %collective-permute-start.6 = (f32[32,512]{1,0:T(8,128)S(1)}, f32[32,512]{1,0:T(8,128)S(1)}, u32[]{:S(2)}, u32[]{:S(2)}) collective-permute-start(f32[32,512]{1,0:T(8,128)S(1)} %pad_maximum_fusion.4), channel_id=1, source_target_pairs={{0,8},{1,9},{2,10},{3,11},{4,12},{5,13},{6,14},{7,15},{8,0},{9,1},... | collective-permute-start | bytes 196616 | tf_op jit(solution)/shard_map/ppermute | solution.py:116
  147.7 5.0 %collective-permute-start.7 = (f32[64,512]{1,0:T(8,128)S(1)}, f32[64,512]{1,0:T(8,128)S(1)}, u32[]{:S(2)}, u32[]{:S(2)}) collective-permute-start(f32[64,512]{1,0:T(8,128)S(1)} %pad_maximum_fusion.3), channel_id=1, source_target_pairs={{0,4},{1,3},{2,6},{3,1},{4,0},{5,7},{6,2},{7,5},{8,12},{9,11},{10,... | collective-permute-start | bytes 393224 | tf_op jit(solution)/shard_map/ppermute | solution.py:116
  152.8 6.4 %collective-permute-start.8 = (f32[128,512]{1,0:T(8,128)S(1)}, f32[128,512]{1,0:T(8,128)S(1)}, u32[]{:S(2)}, u32[]{:S(2)}) collective-permute-start(f32[128,512]{1,0:T(8,128)S(1)} %pad_maximum_fusion.2), channel_id=1, source_target_pairs={{0,2},{1,5},{2,0},{3,7},{4,6},{5,1},{6,4},{7,3},{8,10},{9,13},{10,... | collective-permute-start | bytes 786440 | tf_op jit(solution)/shard_map/ppermute | solution.py:116
  159.3 2.0 collective-permute-start.9

commit v12 on v11

--- a/solution.py
+++ b/solution.py
@@ -99,6 +99,8 @@
     order = [list(range(steps)), list(range(steps))]
     if steps >= 3:
         order[1][1], order[1][2] = 2, 1
+    if steps >= 5:
+        order[1][3], order[1][4] = 4, 3
     idx = lax.axis_index(AXES)
     core = idx & 1
     buf = local

time: 214 us -> 214 us (level)
  no operation moved by 1% of the time
where the time goes in v12:
time: 214 us
  waiting for transfers between devices  132 us (62%)
  Pallas kernels  51.6 us (24%)
  starting transfers between devices  14.2 us (7%)
  local copies, waits for them, and re-layouts  7.44 us (3%)
  matrix products  5.6 us (3%)
    all_to_all x1, waiting for transfers between devices, per_device(): lax.all_to_all(sample_t, AXES, split_axis=1, concat_axis=0, tiled=True)  93.9 us
    pallas_call x1, Pallas kernels, factor_and_basis(): pl.pallas_call(functools.partial(_fused_kernel, b=b, scale=scale), out_sh...  51.6 us
    ppermute x5, waiting for transfers between devices, sum_by_halving(): recv = lax.ppermute(buf, AXES, perm)  19.2 us
    ppermute x5, waiting for transfers between devices, sum_by_halving(): buf = keep + lax.ppermute(send, AXES, perm)  19.2 us
    all_to_all x1, starting transfers between devices, per_device(): lax.all_to_all(sample_t, AXES, split_axis=1, concat_axis=0, tiled=True)  7.43 us
    dot_general x3, matrix products, gram_of(): jnp.dot(x, y.T, precision=lax.Precision.HIGHEST, preferred_element_type=j...  5.6 us
    all_to_all x1, local copies, waits for them, and re-layouts, per_device(): lax.all_to_all(sample_t, AXES, split_axis=1, concat_axis=0, tiled=True)  4.7 us
  transfers between devices with their start and end apart: 11, of which 11 were waited for; matrix products, arithmetic and copies ran while one was open for 0% of the time, Pallas kernels for 0%

profile of v12, /device:TPU:0, one launch (start us, length us, event | category | flops | bytes accessed | tf_op | source)
XLA Modules:
  0.0 213.5 jit_solution(7416641354237633954)
XLA Ops:
  0.6 4.7 %copy.11 = f32[2,32,8,2048]{3,2,0,1:T(8,128)} copy(f32[2,32,8,2048]{3,2,1,0:T(8,128)} %bitcast.21) | data formatting | bytes 8388608 | tf_op jit(solution)/shard_map/all_to_all | solution.py:129
  5.3 7.4 %all-to-all-start = ((f32[16,32,2048]{2,0,1:T(8,128)}), f32[16,32,2048]{2,0,1:T(8,128)}, u32[]{:S(2)}, u32[]{:S(2)}) async-start(f32[16,32,2048]{2,0,1:T(8,128)} %bitcast.20), calls=%async_computation | async-start | bytes 8388608 | tf_op jit(solution)/shard_map/all_to_all | solution.py:129
  12.8 93.9 %all-to-all-done = f32[16,32,2048]{2,0,1:T(8,128)} async-done(((f32[16,32,2048]{2,0,1:T(8,128)}), f32[16,32,2048]{2,0,1:T(8,128)}, u32[]{:S(2)}, u32[]{:S(2)}) %all-to-all-start) | async-done | bytes 4194336 | tf_op jit(solution)/shard_map/all_to_all | solution.py:129
  106.6 2.5 %fusion = (f32[16,16,2048]{2,1,0:T(8,128)S(1)}, f32[16,16,2048]{2,1,0:T(8,128)S(1)}) fusion(f32[32,16,2048]{2,1,0:T(8,128)} %bitcast), kind=kLoop, calls=%fused_computation.27 | loop fusion | bytes 8388608 | tf_op jit(solution)/shard_map/slice | solution.py:131
  109.1 1.9 fusion.1
  111.0 1.9 fusion.2
  112.9 1.9 fusion.3
  115.2 1.9 collective-permute-done
  117.2 1.3 collective-permute-start.1
  118.5 5.1 %collective-permute-done.1 = f32[128,512]{1,0:T(8,128)S(1)} collective-permute-done((f32[128,512]{1,0:T(8,128)S(1)}, f32[128,512]{1,0:T(8,128)S(1)}, u32[]{:S(2)}, u32[]{:S(2)}) %collective-permute-start.1) | collective-permute-done | bytes 262176 | tf_op jit(solution)/shard_map/ppermute | solution.py:116
  123.7 1.3 collective-permute-start.2
  125.0 3.7 %collective-permute-done.2 = f32[64,512]{1,0:T(8,128)S(1)} collective-permute-done((f32[64,512]{1,0:T(8,128)S(1)}, f32[64,512]{1,0:T(8,128)S(1)}, u32[]{:S(2)}, u32[]{:S(2)}) %collective-permute-start.2) | collective-permute-done | bytes 131104 | tf_op jit(solution)/shard_map/ppermute | solution.py:116
  128.9 4.2 %collective-permute-done.3 = f32[32,512]{1,0:T(8,128)S(1)} collective-permute-done((f32[32,512]{1,0:T(8,128)S(1)}, f32[32,512]{1,0:T(8,128)S(1)}, u32[]{:S(2)}, u32[]{:S(2)}) %collective-permute-start.3) | collective-permute-done | bytes 65568 | tf_op jit(solution)/shard_map/ppermute | solution.py:116
  133.1 0.7 collective-permute-start.4
  133.8 4.2 %collective-permute-done.4 = f32[16,512]{1,0:T(8,128)S(1)} collective-permute-done((f32[16,512]{1,0:T(8,128)S(1)}, f32[16,512]{1,0:T(8,128)S(1)}, u32[]{:S(2)}, u32[]{:S(2)}) %collective-permute-start.4) | collective-permute-done | bytes 32800 | tf_op jit(solution)/shard_map/ppermute | solution.py:116
  138.6 4.2 %collective-permute-done.5 = f32[16,512]{1,0:T(8,128)S(1)} collective-permute-done((f32[16,512]{1,0:T(8,128)S(1)}, f32[16,512]{1,0:T(8,128)S(1)}, u32[]{:S(2)}, u32[]{:S(2)}) %collective-permute-start.5) | collective-permute-done | bytes 32800 | tf_op jit(solution)/shard_map/ppermute | solution.py:118
  142.9 4.2 %collective-permute-done.6 = f32[32,512]{1,0:T(8,128)S(1)} collective-permute-done((f32[32,512]{1,0:T(8,128)S(1)}, f32[32,512]{1,0:T(8,128)S(1)}, u32[]{:S(2)}, u32[]{:S(2)}) %collective-permute-start.6) | collective-permute-done | bytes 65568 | tf_op jit(solution)/shard_map/ppermute | solution.py:118
  147.2 1.3 collective-permute-start.7
  148.5 3.7 %collective-permute-done.7 = f32[64,512]{1,0:T(8,128)S(1)} collective-permute-done((f32[64,512]{1,0:T(8,128)S(1)}, f32[64,512]{1,0:T(8,128)S(1)}, u32[]{:S(2)}, u32[]{:S(2)}) %collective-permute-start.7) | collective-permute-done | bytes 131104 | tf_op jit(solution)/shard_map/ppermute | solution.py:118
  152.3 1.3 collective-permute-start.8
  153.6 5.1 %collective-permute-done.8 = f32[128,512]{1,0:T(8,128)S(1)} collective-permute-done((f32[128,512]{1,0:T(8,128)S(1)}, f32[128,512]{1,0:T(8,128)S(1)}, u32[]{:S(2)}, u32[]{:S(2)}) %collective-permute-start.8) | collective-permute-done | bytes 262176 | tf_op jit(solution)/shard_map/ppermute | solution.py:118
  158.9 1.9 collective-permute-done.9
  160.9 1.0 pad_maximum_fusion.g_ref
  162.0 51.6 %shard_map.30 = (f32[512,512]{1,0:T(8,128)}, f32[2048,512]{1,0:T(8,128)}) custom-call(f32[512,512]{1,0:T(8,128)} %pad_maximum_fusion.g_ref, f32[512,2048]{1,0:T(8,128)} %bitcast.4.rt_ref), custom_call_target="tpu_custom_call" | custom-call | flops 1342177280 | bytes 11534336 | tf_op jit(solution)/shard_map/pallas_call | solution.py:85
  (26 shorter events, 1.7 us)
Async XLA Ops:
  5.3 101.3 %all-to-all-start = ((f32[16,32,2048]{2,0,1:T(8,128)}), f32[16,32,2048]{2,0,1:T(8,128)}, u32[]{:S(2)}, u32[]{:S(2)}) async-start(f32[16,32,2048]{2,0,1:T(8,128)} %bitcast.20), calls=%async_computation | async-start | bytes 8388608 | tf_op jit(solution)/shard_map/all_to_all | solution.py:129
  115.1 2.0 collective-permute-start
  117.2 6.4 %collective-permute-start.1 = (f32[128,512]{1,0:T(8,128)S(1)}, f32[128,512]{1,0:T(8,128)S(1)}, u32[]{:S(2)}, u32[]{:S(2)}) collective-permute-start(f32[128,512]{1,0:T(8,128)S(1)} %constant_dynamic-slice_fusion.3), channel_id=1, source_target_pairs={{0,2},{1,5},{2,0},{3,7},{4,6},{5,1},{6,4},{7,3},{8,10},{9,13},{10,... | collective-permute-start | bytes 786440 | tf_op jit(solution)/shard_map/ppermute | solution.py:116
  123.7 5.0 %collective-permute-start.2 = (f32[64,512]{1,0:T(8,128)S(1)}, f32[64,512]{1,0:T(8,128)S(1)}, u32[]{:S(2)}, u32[]{:S(2)}) collective-permute-start(f32[64,512]{1,0:T(8,128)S(1)} %constant_dynamic-slice_fusion.2), channel_id=1, source_target_pairs={{0,4},{1,3},{2,6},{3,1},{4,0},{5,7},{6,2},{7,5},{8,12},{9,11},{10,... | collective-permute-start | bytes 393224 | tf_op jit(solution)/shard_map/ppermute | solution.py:116
  128.8 4.3 %collective-permute-start.3 = (f32[32,512]{1,0:T(8,128)S(1)}, f32[32,512]{1,0:T(8,128)S(1)}, u32[]{:S(2)}, u32[]{:S(2)}) collective-permute-start(f32[32,512]{1,0:T(8,128)S(1)} %constant_dynamic-slice_fusion.1), channel_id=1, source_target_pairs={{0,8},{1,17},{2,10},{3,19},{4,12},{5,21},{6,14},{7,23},{8,0},{9,25... | collective-permute-start | bytes 196616 | tf_op jit(solution)/shard_map/ppermute | solution.py:116
  133.1 4.9 %collective-permute-start.4 = (f32[16,512]{1,0:T(8,128)S(1)}, f32[16,512]{1,0:T(8,128)S(1)}, u32[]{:S(2)}, u32[]{:S(2)}) collective-permute-start(f32[16,512]{1,0:T(8,128)S(1)} %constant_dynamic-slice_fusion), channel_id=1, source_target_pairs={{0,16},{1,9},{2,18},{3,11},{4,20},{5,13},{6,22},{7,15},{8,24},{9,1... | collective-permute-start | bytes 98312 | tf_op jit(solution)/shard_map/ppermute | solution.py:116
  138.0 4.8 %collective-permute-start.5 = (f32[16,512]{1,0:T(8,128)S(1)}, f32[16,512]{1,0:T(8,128)S(1)}, u32[]{:S(2)}, u32[]{:S(2)}) collective-permute-start(f32[16,512]{1,0:T(8,128)S(1)} %dynamic-slice_add_fusion.4), channel_id=1, source_target_pairs={{0,16},{1,9},{2,18},{3,11},{4,20},{5,13},{6,22},{7,15},{8,24},{9,1... | collective-permute-start | bytes 98312 | tf_op jit(solution)/shard_map/ppermute | solution.py:118
  142.9 4.3 %collective-permute-start.6 = (f32[32,512]{1,0:T(8,128)S(1)}, f32[32,512]{1,0:T(8,128)S(1)}, u32[]{:S(2)}, u32[]{:S(2)}) collective-permute-start(f32[32,512]{1,0:T(8,128)S(1)} %pad_maximum_fusion.4), channel_id=1, source_target_pairs={{0,8},{1,17},{2,10},{3,19},{4,12},{5,21},{6,14},{7,23},{8,0},{9,25... | collective-permute-start | bytes 196616 | tf_op jit(solution)/shard_map/ppermute | solution.py:118
  147.2 5.0 %collective-permute-start.7 = (f32[64,512]{1,0:T(8,128)S(1)}, f32[64,512]{1,0:T(8,128)S(1)}, u32[]{:S(2)}, u32[]{:S(2)}) collective-permute-start(f32[64,512]{1,0:T(8,128)S(1)} %pad_maximum_fusion.3), channel_id=1, source_target_pairs={{0,4},{1,3},{2,6},{3,1},{4,0},{5,7},{6,2},{7,5},{8,12},{9,11},{10,... | collective-permute-start | bytes 393224 | tf_op jit(solution)/shard_map/ppermute | solution.py:118
  152.3 6.4 %collective-permute-start.8 = (f32[128,512]{1,0:T(8,128)S(1)}, f32[128,512]{1,0:T(8,128)S(1)}, u32[]{:S(2)}, u32[]{:S(2)}) collective-permute-start(f32[128,512]{1,0:T(8,128)S(1)} %pad_maximum_fusion.2), channel_id=1, source_target_pairs={{0,2},{1,5},{2,0},{3,7},{4,6},{5,1},{6,4},{7,3},{8,10},{9,13},{10,... | collective-permute-start | bytes 786440 | tf_op jit(solution)/shard_map/ppermute | solution.py:118
  158.8 2.0 collective-permute-start.9
